TPU v7x, 256 devices: a whole 4x4x8 slice. The times are simulated.
256 devices in a mesh: seq: 32 (over y, z), grp: 8 (over x, core).
Axes of the slice: x: 4, y: 4, z: 8, core: 2. Of those that a mesh axis runs over, the one named last changes fastest.
Arguments:
- query: bfloat16 [8, 4096, 2048], P('grp', 'seq'), may hold values from -6 to 6
- key_in: bfloat16 [8, 4096, 2048], P('grp', 'seq'), may hold values from -6 to 6
- value: bfloat16 [8, 4096, 2048], P('grp', 'seq'), may hold values from -6 to 6
- cotangent: bfloat16 [8, 4096, 2048], P('grp', 'seq'), may hold values from -6 to 6
- routes: int32 [8, 4096, 6], P('grp', 'seq'), may hold values from 0 to 63, as said below
- gates: float32 [8, 4096, 6], P('grp', 'seq'), may hold values from 0.01 to 0.1
- hidden: bfloat16 [8, 4096, 6, 704], P('grp', 'seq'), may hold values from -6 to 6
Outputs:
- attention_out: bfloat16 [8, 4096, 2048], P('grp', 'seq')
- grad_query: bfloat16 [8, 4096, 2048], P('grp', 'seq')
- grad_key: bfloat16 [8, 4096, 2048], P('grp', 'seq')
- grad_value: bfloat16 [8, 4096, 2048], P('grp', 'seq')
- expert_grad: bfloat16 [64, 704, 2048], P('seq', 'grp')
Inputs may be any that keep to these rules, and one draw needn't show every extreme that they name: `routes`: the 6 experts of a token differ. Among the 128 tokens of one device (aligned blocks of the positions of a sequence) no expert is named more than 32 times, and in every sequence some expert is named exactly 32 times by the tokens of each device. Expert ids are small integers and may be packed several to a word whenever they are sent.
All inputs are finite; a program needn't handle non-finite values.
Results may differ from a plain program's by a relative error of at most 0.04.
Values may be sent and summed in bfloat16 or wider, within the bound.
No kernel may reach another device: no remote copies, remote signals or barrier semaphores. Data moves between devices by JAX's collectives and lax.ppermute only.
A program may use at most 192 MiB of HBM per device.

v0:
```python
import jax
import jax.numpy as jnp
from jax import lax
from jax.sharding import PartitionSpec as P

HEADS = 16
TOPK = 6
EXP_DEV = 2


PRECISE = lax.Precision.HIGHEST


def carried_in(array, axis, join, neutral, backward):
    count = lax.axis_size(axis)
    place = lax.axis_index(axis)
    ahead = count - 1 - place if backward else place
    gathered = lax.all_gather(array.astype(jnp.bfloat16), axis)
    state = jnp.zeros_like(array) + jnp.asarray(neutral, array.dtype)

    def one(lap, state):
        source = count - 1 - lap if backward else lap
        return join(state, lax.dynamic_index_in_dim(gathered, source, 0, False).astype(array.dtype))

    return lax.fori_loop(0, ahead, one, state)


def add_states(first_term, second_term):
    return first_term + second_term


def per_device(query, key_in, value, cotangent, routes, gates, hidden):
    tokens = query.shape[1]
    width = query.shape[2]
    head_dim = width // HEADS
    hidden_units = hidden.shape[3]
    seq_count = lax.axis_size("seq")
    seq_index = lax.axis_index("seq")
    query_raw = query[0].reshape(tokens, HEADS, head_dim)
    key_raw = key_in[0].reshape(tokens, HEADS, head_dim)
    value_raw = value[0].reshape(tokens, HEADS, head_dim)
    grad_raw = cotangent[0].reshape(tokens, HEADS, head_dim)
    query_full = query_raw.astype(jnp.float32)
    key_full = key_raw.astype(jnp.float32)
    value_full = value_raw.astype(jnp.float32)
    grad_out = grad_raw.astype(jnp.float32)
    position = seq_index * tokens + jnp.arange(tokens, dtype=jnp.int32)
    scaling = 1.0 / jnp.sqrt(head_dim * (position + 1).astype(jnp.float32))
    row_scale = scaling[:, None, None]
    causal = jnp.tril(jnp.ones((tokens, tokens), jnp.float32))
    state_sum = jnp.einsum("thd,the->hde", key_raw, value_raw, preferred_element_type=jnp.float32)
    grad_sum = jnp.einsum("thd,the->hde", query_full * row_scale, grad_out, precision=PRECISE)
    empty = jnp.zeros_like(state_sum)
    prefix_state = carried_in(state_sum, "seq", add_states, empty, False)
    after_state = carried_in(grad_sum, "seq", add_states, empty, True)
    scores = (
        jnp.einsum("thd,uhd->htu", query_raw, key_raw, preferred_element_type=jnp.float32) * causal
    )
    outputs = jnp.einsum("htu,uhe->the", scores, value_full, precision=PRECISE)
    outputs = (
        outputs + jnp.einsum("thd,hde->the", query_full, prefix_state, precision=PRECISE)
    ) * row_scale
    grad_scores = (
        jnp.einsum("the,uhe->htu", grad_raw, value_raw, preferred_element_type=jnp.float32) * causal
    )
    grad_q = jnp.einsum("htu,uhd->thd", grad_scores, key_full, precision=PRECISE)
    grad_q = (
        grad_q + jnp.einsum("the,hde->thd", grad_out, prefix_state, precision=PRECISE)
    ) * row_scale
    col_scale = scaling[None, :, None]
    weighted = scores * col_scale
    grad_weighted = grad_scores * col_scale
    grad_k = jnp.einsum("htu,thd->uhd", grad_weighted, query_full, precision=PRECISE)
    grad_k = grad_k + jnp.einsum("uhe,hde->uhd", value_full, after_state, precision=PRECISE)
    grad_v = jnp.einsum("htu,the->uhe", weighted, grad_out, precision=PRECISE)
    grad_v = grad_v + jnp.einsum("uhd,hde->uhe", key_full, after_state, precision=PRECISE)

    def to_shard(array):
        return array.reshape(1, tokens, width).astype(jnp.bfloat16)

    experts_total = EXP_DEV * seq_count
    capacity = tokens * TOPK * 8 // (experts_total * 3)
    assigned = tokens * TOPK
    flat_ids = routes[0].reshape(assigned)
    expert_range = jnp.arange(experts_total, dtype=jnp.int32)
    matches = (flat_ids[:, None] == expert_range[None, :]).astype(jnp.int32)
    ranking = jnp.sum((jnp.cumsum(matches, axis=0) - matches) * matches, axis=1)
    slot_index = flat_ids * capacity + ranking
    scaled = (
        gates[0].reshape(assigned, 1)
        * hidden[0].reshape(assigned, hidden_units).astype(jnp.float32)
    ).astype(jnp.bfloat16)
    hidden_slots = (
        jnp.zeros((experts_total * capacity, hidden_units), jnp.bfloat16).at[slot_index].set(scaled)
    )
    hidden_slots = hidden_slots.reshape(seq_count, EXP_DEV, capacity, hidden_units)
    token_index = jnp.arange(assigned, dtype=jnp.int32) // TOPK
    all_routes = lax.all_gather(routes, "seq", axis=1, tiled=True)[0].reshape(seq_count, assigned)
    arrived_hidden = lax.all_to_all(hidden_slots, "seq", split_axis=0, concat_axis=0, tiled=True)
    all_cotangent = lax.all_gather(cotangent, "seq", axis=1, tiled=True)[0]
    own_experts = seq_index * EXP_DEV + jnp.arange(EXP_DEV, dtype=jnp.int32)
    source_match = (all_routes[:, None, :] == own_experts[None, :, None]).astype(jnp.int32)
    source_rank = jnp.cumsum(source_match, axis=2) - source_match
    slot_range = jnp.arange(capacity, dtype=jnp.int32)
    placed = (source_match[..., None] == 1) & (source_rank[..., None] == slot_range)
    token_of_slot = jnp.sum(jnp.where(placed, token_index[None, None, :, None], 0), axis=2)
    wanted = (
        jnp.arange(seq_count, dtype=jnp.int32)[:, None, None] * tokens + token_of_slot
    ).reshape(-1)
    cot_rows = jnp.take(all_cotangent, wanted, axis=0).reshape(seq_count, EXP_DEV, capacity, width)
    group_term = jnp.einsum(
        "sxcf,sxcd->xfd", arrived_hidden, cot_rows, preferred_element_type=jnp.float32
    )
    rounded = lax.optimization_barrier(group_term.astype(jnp.bfloat16)).astype(jnp.float32)
    expert_grad = lax.psum_scatter(
        rounded.astype(jnp.bfloat16), "grp", scatter_dimension=1, tiled=True
    )
    return (to_shard(outputs), to_shard(grad_q), to_shard(grad_k), to_shard(grad_v), expert_grad)


def solution(mesh):
    in_specs = (
        P("grp", "seq", None),
        P("grp", "seq", None),
        P("grp", "seq", None),
        P("grp", "seq", None),
        P("grp", "seq", None),
        P("grp", "seq", None),
        P("grp", "seq", None, None),
    )
    out_specs = (
        P("grp", "seq", None),
        P("grp", "seq", None),
        P("grp", "seq", None),
        P("grp", "seq", None),
        P("seq", "grp", None),
    )
    return jax.shard_map(
        per_device, mesh=mesh, in_specs=in_specs, out_specs=out_specs, check_vma=False
    )
```

profile of v0, /device:TPU:32, one launch (start us, length us, event | category | flops | bytes accessed | tf_op | source)
XLA Modules:
  0.0 539.0 jit_solution(5347873770166369445)
XLA Ops:
  9.3 1.3 copy.106
  10.7 2.0 convolution_convert_fusion.1
  15.0 1.8 reduce-window.14
  17.5 3.1 copy.128
  20.6 2.7 reshape.242
  24.7 9.7 %scatter_custom_fusion = bf16[2048,704]{1,0:T(8,128)(2,1)} fusion(s32[768]{0:T(1024)S(1)} %fusion.41, bf16[]{:T(256)} %constant.88.clone.1, f32[768,704]{1,0:T(8,128)S(1)} %reshape.242, f32[768]{0:T(1024)S(1)} %mul.127), kind=kCustom, calls=%fused_computation.13 | custom fusion | flops 1081344 | bytes 5246978 | tf_op jit(solution)/shard_map/scatter | solution.py:94
  34.4 11.4 %all-to-all-start = ((bf16[32,2,32,704]{3,2,1,0:T(8,128)(2,1)}), bf16[32,2,32,704]{3,2,1,0:T(8,128)(2,1)}, u32[]{:S(2)}, u32[]{:S(2)}) async-start(bf16[32,2,32,704]{3,2,1,0:T(8,128)(2,1)} %bitcast.127), calls=%async_computation | async-start | bytes 6291456 | tf_op jit(solution)/shard_map/all_to_all | solution.py:99
  45.9 125.3 %all_gather.22 = s32[1,4096,6]{1,0,2:T(1,128)S(1)} all-gather(s32[1,128,6]{1,0,2:T(1,128)S(1)} %copy-done.9), channel_id=1, replica_groups=mesh['seq'=32,'grp'=8] {'seq'}, dimensions={1}, use_global_device_ids=true | all-gather | bytes 101376 | tf_op jit(solution)/shard_map/all_gather | solution.py:98
  171.8 1.7 eq.94
  174.8 3.5 reduce-window.16
  179.2 1.6 select_reduce_fusion
  181.1 21.2 %all-gather.6.cloned.1.call-done = bf16[1,4096,2048]{2,1,0:T(8,128)(2,1)} async-done(((bf16[1,128,2048]{2,1,0:T(8,128)(2,1)}), bf16[1,4096,2048]{2,1,0:T(8,128)(2,1)}) %all-gather.6.cloned.1.call-update) | async-done | bytes 16777232 | tf_op jit(solution)/shard_map/all_gather | solution.py:100
  202.2 24.3 %gather_fusion = bf16[2048,2048]{1,0:T(8,128)(2,1)} fusion(bf16[4096,2048]{1,0:T(8,128)(2,1)} %bitcast.112, s32[2048]{0:T(1024)S(1)} %broadcast_clamp_fusion), kind=kCustom, calls=%fused_computation | custom fusion | bytes 16785408 | tf_op jit(solution)/shard_map/jit(_take)/gather | solution.py:110
  226.5 9.7 %bitcast_convert_fusion = bf16[2,704,2048]{2,1,0:T(8,128)(2,1)S(1)} fusion(bf16[32,2,32,704]{3,2,1,0:T(8,128)(2,1)} %all-to-all-done, bf16[32,2,32,2048]{3,2,1,0:T(8,128)(2,1)} %bitcast.128, pred[32,2,32]{2,1,0:T(4,128)(4,1)S(1)} %get-tuple-element.122), kind=kOutput, calls=%fused_computation.4 | convolution fusion | flops 5912657920 | bytes 17041408 | tf_op jit(solution)/shard_map/sxcf,sxcd->xfd/dot_general | solution.py:111
  236.2 12.1 %copy.143 = bf16[2,704,2048]{2,0,1:T(2,128)(2,1)S(1)} copy(bf16[2,704,2048]{2,1,0:T(8,128)(2,1)S(1)} %bitcast_convert_fusion) | data formatting | bytes 11534336
  248.4 6.2 %copy.150 = bf16[88,8,2,2048]{3,1,2,0:T(8,128)(2,1)} copy(bf16[88,8,2,2048]{3,2,1,0:T(2,128)(2,1)S(1)} %bitcast.114) | data formatting | bytes 11534336
  256.3 2.2 convolution_bitcast_fusion.5
  258.5 2.2 convolution_bitcast_fusion.7
  260.6 1.8 convolution_bitcast_fusion.3
  262.5 1.7 convolution_bitcast_fusion.1
  264.2 78.8 %all-gather.10.cloned.1.call-done = bf16[512,128,128]{2,1,0:T(8,128)(2,1)} async-done(((bf16[16,128,128]{2,1,0:T(8,128)(2,1)}), bf16[512,128,128]{2,1,0:T(8,128)(2,1)}) %all-gather.10.cloned.1.call-update) | async-done | bytes 16777232 | tf_op jit(solution)/shard_map/all_gather | solution.py:18
  343.0 39.5 %while.23 = (s32[]{:T(128)}, f32[16,128,128]{2,1,0:T(8,128)S(1)}, s32[]{:T(128)}, bf16[32,16,128,128]{3,2,1,0:T(8,128)(2,1)}, s32[]{:T(128)}, /*index=5*/s32[]{:T(128)}, s32[]{:T(128)}, s32[]{:T(128)}) while((s32[]{:T(128)}, f32[16,128,128]{2,1,0:T(8,128)S(1)}, s32[]{:T(128)}, bf16[32,16,128,128]{3,2,1,0:T(8,128)(2,1)}, s32[]{:T(128)}, ...), condition=%wide.region_3.4_spmd, body=%wide.region_2.3_spmd.sunk | while | flops 524294 | bytes 2621575 | solution.py:25
  356.2 1.3 convert_add_fusion.5
  382.5 3.2 fusion.15
  385.8 2.0 copy.137
  387.8 2.2 fusion.16
  391.1 92.7 %all-gather.8.cloned.1.call-done = bf16[512,128,128]{2,1,0:T(8,128)(2,1)} async-done(((bf16[16,128,128]{2,1,0:T(8,128)(2,1)}), bf16[512,128,128]{2,1,0:T(8,128)(2,1)}) %all-gather.8.cloned.1.call-update) | async-done | bytes 16777232 | tf_op jit(solution)/shard_map/all_gather | solution.py:18
  483.9 1.5 while.22
  485.4 1.9 fusion.18
  488.3 2.2 fusion.17
  491.6 37.2 %reduce-scatter.4.cloned.1.call-done = bf16[88,4096]{1,0:T(8,128)(2,1)} async-done(((bf16[704,4096]{1,0:T(8,128)(2,1)}), bf16[88,4096]{1,0:T(8,128)(2,1)}) %reduce-scatter.4.cloned.1.call-update) | async-done | bytes 720912
  528.7 2.4 reshape.263
  (107 shorter events, 54.1 us)
Async XLA Ops:
  7.2 5.6 %copy-start.7 = (bf16[1,128,2048]{2,1,0:T(8,128)(2,1)S(1)}, bf16[1,128,2048]{2,1,0:T(8,128)(2,1)}, u32[]{:S(2)}) copy-start(bf16[1,128,2048]{2,1,0:T(8,128)(2,1)} %param.13) | copy-start | bytes 1572868
  7.2 5.7 %copy-start.8 = (bf16[1,128,2048]{2,1,0:T(8,128)(2,1)S(1)}, bf16[1,128,2048]{2,1,0:T(8,128)(2,1)}, u32[]{:S(2)}) copy-start(bf16[1,128,2048]{2,1,0:T(8,128)(2,1)} %param.12) | copy-start | bytes 1572868
  7.2 195.0 %all-gather.6.cloned.1.call-start = ((), (), s32[]{:S(2)}) async-start(), calls=%async_computation.2 | async-start | bytes 17301504 | tf_op jit(solution)/shard_map/all_gather | solution.py:100
  7.9 335.0 %all-gather.10.cloned.1.call-start = ((), (), s32[]{:S(2)}) async-start(), calls=%async_computation.4 | async-start | bytes 17301504 | tf_op jit(solution)/shard_map/all_gather | solution.py:18
  9.3 5.3 copy-start.9
  10.6 6.6 %copy-start = (bf16[1,128,2048]{1,2,0:T(8,128)(2,1)}, bf16[1,128,2048]{1,2,0:T(8,128)(2,1)S(1)}, u32[]{:S(2)}) copy-start(bf16[1,128,2048]{1,2,0:T(8,128)(2,1)S(1)} %copy.106) | copy-start | bytes 1572868
  12.7 471.1 %all-gather.8.cloned.1.call-start = ((), (), s32[]{:S(2)}) async-start(), calls=%async_computation.3 | async-start | bytes 17301504 | tf_op jit(solution)/shard_map/all_gather | solution.py:18
  13.0 4.4 copy-start.2
  13.5 3.9 copy-start.4
  16.8 0.7 copy-start.6
  17.5 5.8 %copy-start.10 = (f32[1,128,6]{1,0,2:T(1,128)S(1)}, f32[1,128,6]{1,0,2:T(1,128)}, u32[]{:S(2)}) copy-start(f32[1,128,6]{1,0,2:T(1,128)} %param.16) | copy-start | bytes 9220
  34.4 192.1 %all-to-all-start = ((bf16[32,2,32,704]{3,2,1,0:T(8,128)(2,1)}), bf16[32,2,32,704]{3,2,1,0:T(8,128)(2,1)}, u32[]{:S(2)}, u32[]{:S(2)}) async-start(bf16[32,2,32,704]{3,2,1,0:T(8,128)(2,1)} %bitcast.127), calls=%async_computation | async-start | bytes 6291456 | tf_op jit(solution)/shard_map/all_to_all | solution.py:99
  45.8 482.9 %reduce-scatter.4.cloned.1.call-start = ((), (), s32[]{:S(2)}) async-start(), calls=%async_computation.5 | async-start | bytes 6488064
  254.6 1.0 copy-start.1
  254.6 1.2 copy-start.3
  254.6 1.7 copy-start.5
Sparse Core Ops, SparseCore 0:
  10.6 191.5 all-gather.5
  205.4 137.5 all-gather.9
  346.1 137.6 all-gather.7
  486.2 42.4 reduce-scatter.3
where the time goes:
time: 548 us; the launch traced here: 539 us
  waiting for transfers between devices  231 us (42%)
  blocking collectives  125 us (23%)
  local copies, waits for them, and re-layouts  66.7 us (12%)
  other arithmetic  58.1 us (11%)
  matrix products  31.3 us (6%)
  between operations  14.4 us (3%)
  starting transfers between devices  11.6 us (2%)
    all_gather x2, waiting for transfers between devices, carried_in(): gathered = lax.all_gather(array.astype(jnp.bfloat16), axis)  171 us
    all_gather x1, blocking collectives, per_device(): lax.all_gather(routes, 'seq', axis=1, tiled=True)[0]  125 us
    add x31, other arithmetic, add_states(): return first_term + second_term  39.9 us
    unnamed x5, waiting for transfers between devices  37.9 us
    unnamed x35, local copies, waits for them, and re-layouts  29.5 us
    gather x1, local copies, waits for them, and re-layouts, per_device(): jnp.take(all_cotangent, wanted, axis=0)  24.3 us
    all_gather x1, waiting for transfers between devices, per_device(): all_cotangent = lax.all_gather(cotangent, 'seq', axis=1, tiled=True)[0]  21.2 us
    all_to_all x1, starting transfers between devices, per_device(): lax.all_to_all(hidden_slots, 'seq', split_axis=0, concat_axis=0, tiled=True)  11.4 us
  transfers between devices with their start and end apart: 5, of which 4 were waited for; matrix products, arithmetic and copies ran while one was open for 28% of the time, Pallas kernels for 0%

commit v1 on v0

v1 whole, which is shorter than its diff:
```python
import jax
import jax.numpy as jnp
from jax import lax
from jax.sharding import PartitionSpec as P

HEADS = 16
TOPK = 6
EXP_DEV = 2
CAP = 32


PRECISE = lax.Precision.HIGHEST


def exclusive_scan(local_sum, axis, backward):
    count = lax.axis_size(axis)
    window = local_sum
    total = jnp.zeros_like(local_sum)
    shift = 1
    while shift < count:
        if backward:
            pairs = [(src, src - shift) for src in range(shift, count)]
        else:
            pairs = [(src, src + shift) for src in range(count - shift)]
        arrived = lax.ppermute(window.astype(jnp.bfloat16), axis, pairs)
        total = total + arrived.astype(jnp.float32)
        window = local_sum + total
        shift *= 2
    return total


def per_device(query, key_in, value, cotangent, routes, gates, hidden):
    tokens = query.shape[1]
    width = query.shape[2]
    head_dim = width // HEADS
    hidden_units = hidden.shape[3]
    seq_count = lax.axis_size("seq")
    seq_index = lax.axis_index("seq")

    experts_total = EXP_DEV * seq_count
    assigned = tokens * TOPK
    slots = experts_total * CAP
    flat_ids = routes[0].reshape(assigned)
    expert_range = jnp.arange(experts_total, dtype=jnp.int32)
    matches = (flat_ids[:, None] == expert_range[None, :]).astype(jnp.int32)
    ranking = jnp.sum((jnp.cumsum(matches, axis=0) - matches) * matches, axis=1)
    slot_index = flat_ids * CAP + ranking
    slot_range = jnp.arange(slots, dtype=jnp.int32)
    pick = slot_index[None, :] == slot_range[:, None]
    scaled = (
        gates[0].reshape(assigned, 1)
        * hidden[0].reshape(assigned, hidden_units).astype(jnp.float32)
    ).astype(jnp.bfloat16)
    hidden_slots = jnp.dot(
        pick.astype(jnp.bfloat16), scaled, preferred_element_type=jnp.float32
    ).astype(jnp.bfloat16)
    pick_token = jnp.any(pick.reshape(slots, tokens, TOPK), axis=2)
    cot_slots = jnp.dot(
        pick_token.astype(jnp.bfloat16), cotangent[0], preferred_element_type=jnp.float32
    ).astype(jnp.bfloat16)
    hidden_slots = hidden_slots.reshape(seq_count, EXP_DEV, CAP, hidden_units)
    cot_slots = cot_slots.reshape(seq_count, EXP_DEV, CAP, width)
    arrived_hidden = lax.all_to_all(hidden_slots, "seq", split_axis=0, concat_axis=0, tiled=True)
    arrived_cot = lax.all_to_all(cot_slots, "seq", split_axis=0, concat_axis=0, tiled=True)

    query_raw = query[0].reshape(tokens, HEADS, head_dim)
    key_raw = key_in[0].reshape(tokens, HEADS, head_dim)
    value_raw = value[0].reshape(tokens, HEADS, head_dim)
    grad_raw = cotangent[0].reshape(tokens, HEADS, head_dim)
    query_full = query_raw.astype(jnp.float32)
    key_full = key_raw.astype(jnp.float32)
    value_full = value_raw.astype(jnp.float32)
    grad_out = grad_raw.astype(jnp.float32)
    position = seq_index * tokens + jnp.arange(tokens, dtype=jnp.int32)
    scaling = 1.0 / jnp.sqrt(head_dim * (position + 1).astype(jnp.float32))
    row_scale = scaling[:, None, None]
    causal = jnp.tril(jnp.ones((tokens, tokens), jnp.float32))
    state_sum = jnp.einsum("thd,the->hde", key_raw, value_raw, preferred_element_type=jnp.float32)
    grad_sum = jnp.einsum("thd,the->hde", query_full * row_scale, grad_out, precision=PRECISE)
    prefix_state = exclusive_scan(state_sum, "seq", False)
    after_state = exclusive_scan(grad_sum, "seq", True)
    scores = (
        jnp.einsum("thd,uhd->htu", query_raw, key_raw, preferred_element_type=jnp.float32) * causal
    )
    outputs = jnp.einsum("htu,uhe->the", scores, value_full, precision=PRECISE)
    outputs = (
        outputs + jnp.einsum("thd,hde->the", query_full, prefix_state, precision=PRECISE)
    ) * row_scale
    grad_scores = (
        jnp.einsum("the,uhe->htu", grad_raw, value_raw, preferred_element_type=jnp.float32) * causal
    )
    grad_q = jnp.einsum("htu,uhd->thd", grad_scores, key_full, precision=PRECISE)
    grad_q = (
        grad_q + jnp.einsum("the,hde->thd", grad_out, prefix_state, precision=PRECISE)
    ) * row_scale
    col_scale = scaling[None, :, None]
    weighted = scores * col_scale
    grad_weighted = grad_scores * col_scale
    grad_k = jnp.einsum("htu,thd->uhd", grad_weighted, query_full, precision=PRECISE)
    grad_k = grad_k + jnp.einsum("uhe,hde->uhd", value_full, after_state, precision=PRECISE)
    grad_v = jnp.einsum("htu,the->uhe", weighted, grad_out, precision=PRECISE)
    grad_v = grad_v + jnp.einsum("uhd,hde->uhe", key_full, after_state, precision=PRECISE)

    def to_shard(array):
        return array.reshape(1, tokens, width).astype(jnp.bfloat16)

    group_term = jnp.einsum(
        "sxcf,sxcd->xfd", arrived_hidden, arrived_cot, preferred_element_type=jnp.float32
    )
    rounded = lax.optimization_barrier(group_term.astype(jnp.bfloat16)).astype(jnp.float32)
    expert_grad = lax.psum_scatter(
        rounded.astype(jnp.bfloat16), "grp", scatter_dimension=1, tiled=True
    )
    return (to_shard(outputs), to_shard(grad_q), to_shard(grad_k), to_shard(grad_v), expert_grad)


def solution(mesh):
    in_specs = (
        P("grp", "seq", None),
        P("grp", "seq", None),
        P("grp", "seq", None),
        P("grp", "seq", None),
        P("grp", "seq", None),
        P("grp", "seq", None),
        P("grp", "seq", None, None),
    )
    out_specs = (
        P("grp", "seq", None),
        P("grp", "seq", None),
        P("grp", "seq", None),
        P("grp", "seq", None),
        P("seq", "grp", None),
    )
    return jax.shard_map(
        per_device, mesh=mesh, in_specs=in_specs, out_specs=out_specs, check_vma=False
    )
```

time: 548 us -> 515 us (0.940); the launches traced: 539 us -> 512 us
  waiting for transfers between devices: 231 us -> 112 us
  starting transfers between devices: 11.6 us -> 99.6 us
  blocking collectives: 125 us -> 195 us
  other arithmetic: 58.1 us -> 5.99 us
  local copies, waits for them, and re-layouts: 66.7 us -> 42.4 us
  matrix products: 31.3 us -> 42.1 us
    all_to_all x0 -> x1, blocking collectives: none -> 195 us  [per_device(): lax.all_to_all(cot_slots, 'seq', split_axis=0, concat_axis=0, tiled=True)]
    all_gather x3 -> x0, waiting for transfers between devices: 193 us -> none  [the longest x2 171 us: carried_in(): gathered = lax.all_gather(array.astype(jnp.bfloat16), axis)]
    all_gather x1 -> x0, blocking collectives: 125 us -> none  [per_device(): lax.all_gather(routes, 'seq', axis=1, tiled=True)[0]]
    ppermute x0 -> x10, starting transfers between devices: none -> 88.2 us  [exclusive_scan(): arrived = lax.ppermute(window.astype(jnp.bfloat16), axis, pairs)]
    all_to_all x1, waiting for transfers between devices: 0.01 us -> 63 us  [per_device(): lax.all_to_all(hidden_slots, 'seq', split_axis=0, concat_axis=0, tiled=True)]
    ppermute x0 -> x10, waiting for transfers between devices: none -> 49 us  [exclusive_scan(): arrived = lax.ppermute(window.astype(jnp.bfloat16), axis, pairs)]
    add x32 -> x2, other arithmetic: 40 us -> 0.02 us  [per_device(): slot_index = flat_ids * CAP + ranking]
    unnamed x5 -> x2, waiting for transfers between devices: 37.9 us -> 0.02 us
  transfers between devices with their start and end apart: 5 -> 12, of which waited for: 4 -> 8; matrix products, arithmetic and copies ran while one was open for 28% -> 9% of each run, Pallas kernels for 0% -> 0%
where the time goes in v1:
time: 515 us; the launch traced here: 512 us
  blocking collectives  195 us (38%)
  waiting for transfers between devices  112 us (22%)
  starting transfers between devices  99.6 us (19%)
  local copies, waits for them, and re-layouts  42.4 us (8%)
  matrix products  42.1 us (8%)
  between operations  14.5 us (3%)
  other arithmetic  5.99 us (1%)
    all_to_all x1, blocking collectives, per_device(): lax.all_to_all(cot_slots, 'seq', split_axis=0, concat_axis=0, tiled=True)  195 us
    ppermute x10, starting transfers between devices, exclusive_scan(): arrived = lax.ppermute(window.astype(jnp.bfloat16), axis, pairs)  88.2 us
    all_to_all x1, waiting for transfers between devices, per_device(): lax.all_to_all(hidden_slots, 'seq', split_axis=0, concat_axis=0, tiled=True)  63 us
    ppermute x10, waiting for transfers between devices, exclusive_scan(): arrived = lax.ppermute(window.astype(jnp.bfloat16), axis, pairs)  49 us
    unnamed x53, local copies, waits for them, and re-layouts  33.2 us
    all_to_all x1, starting transfers between devices, per_device(): lax.all_to_all(hidden_slots, 'seq', split_axis=0, concat_axis=0, tiled=True)  11.4 us
  transfers between devices with their start and end apart: 12, of which 8 were waited for; matrix products, arithmetic and copies ran while one was open for 9% of the time, Pallas kernels for 0%

profile of v1, /device:TPU:32, one launch (start us, length us, event | category | flops | bytes accessed | tf_op | source)
XLA Modules:
  0.0 511.7 jit_solution(2646884813191889871)
XLA Ops:
  9.2 1.8 reduce-window.6
  11.4 2.0 copy.117
  15.1 4.3 fusion.2
  19.4 2.9 copy.118
  22.3 11.4 %all-to-all-start = ((bf16[32,2,32,704]{3,2,1,0:T(8,128)(2,1)}), bf16[32,2,32,704]{3,2,1,0:T(8,128)(2,1)S(1)}, u32[]{:S(2)}, u32[]{:S(2)}) async-start(bf16[32,2,32,704]{3,2,1,0:T(8,128)(2,1)} %bitcast.14), calls=%async_computation | async-start | bytes 6291456 | tf_op jit(solution)/shard_map/all_to_all | solution.py:63
  35.0 6.6 %convolution_convert_fusion = bf16[2048,2048]{1,0:T(8,128)(2,1)} fusion(pred[2048,128]{1,0:T(8,128)(4,1)S(1)} %fusion.1, bf16[1,128,2048]{2,1,0:T(8,128)(2,1)} %param.10), kind=kOutput, calls=%fused_computation.1 | convolution fusion | flops 1077936128 | bytes 9175040 | tf_op jit(solution)/shard_map/dot_general | solution.py:58
  41.6 63.0 %all-to-all-done = bf16[32,2,32,704]{3,2,1,0:T(8,128)(2,1)S(1)} async-done(((bf16[32,2,32,704]{3,2,1,0:T(8,128)(2,1)}), bf16[32,2,32,704]{3,2,1,0:T(8,128)(2,1)S(1)}, u32[]{:S(2)}, u32[]{:S(2)}) %all-to-all-start) | async-done | bytes 2883616 | tf_op jit(solution)/shard_map/all_to_all | solution.py:63
  104.6 195.2 %all_to_all.10 = bf16[32,2,32,2048]{3,2,1,0:T(8,128)(2,1)S(1)} all-to-all(bf16[32,2,32,2048]{3,2,1,0:T(8,128)(2,1)} %bitcast.95), channel_id=1, replica_groups=mesh['seq'=32,'grp'=8] {'seq'}, dimensions={0} | all-to-all | bytes 16777216 | tf_op jit(solution)/shard_map/all_to_all | solution.py:64
  299.8 6.7 %bitcast_convert_fusion = bf16[2,704,2048]{2,1,0:T(8,128)(2,1)S(1)} fusion(bf16[32,2,32,704]{3,2,1,0:T(8,128)(2,1)S(1)} %all-to-all-done, bf16[32,2,32,2048]{3,2,1,0:T(8,128)(2,1)S(1)} %all_to_all.10), kind=kOutput, calls=%fused_computation | convolution fusion | flops 5908463616 | bytes 17039360 | tf_op jit(solution)/shard_map/sxcf,sxcd->xfd/dot_general | solution.py:107
  306.4 12.0 %copy.129 = bf16[2,704,2048]{2,0,1:T(2,128)(2,1)S(1)} copy(bf16[2,704,2048]{2,1,0:T(8,128)(2,1)S(1)} %bitcast_convert_fusion) | data formatting | bytes 11534336
  318.4 6.2 %copy.135 = bf16[88,8,2,2048]{3,1,2,0:T(8,128)(2,1)} copy(bf16[88,8,2,2048]{3,2,1,0:T(2,128)(2,1)S(1)} %bitcast.97) | data formatting | bytes 11534336
  327.5 1.9 collective-permute-start
  333.5 4.0 collective-permute-start.5
  339.3 1.8 convolution_bitcast_fusion.1
  341.2 3.3 collective-permute-start.1
  348.4 15.9 %collective-permute-done.1 = bf16[16,128,128]{2,1,0:T(8,128)(2,1)S(1)} collective-permute-done((bf16[16,128,128]{2,1,0:T(8,128)(2,1)S(1)}, bf16[16,128,128]{2,1,0:T(8,128)(2,1)S(1)}, u32[]{:S(2)}, u32[]{:S(2)}) %collective-permute-start.1) | collective-permute-done | bytes 524320 | tf_op jit(solution)/shard_map/ppermute | solution.py:25
  364.5 7.3 %collective-permute-start.2 = (bf16[16,128,128]{2,1,0:T(8,128)(2,1)S(1)}, bf16[16,128,128]{2,1,0:T(8,128)(2,1)S(1)}, u32[]{:S(2)}, u32[]{:S(2)}) collective-permute-start(bf16[16,128,128]{2,1,0:T(8,128)(2,1)S(1)} %add_convert_fusion.5), channel_id=1, source_target_pairs={{0,32},{8,40},{16,48},{24,56},{32,64},{40,72},{48,80},{56,88},{64,... | collective-permute-start | bytes 1572872 | tf_op jit(solution)/shard_map/ppermute | solution.py:25
  376.7 16.0 %collective-permute-done.2 = bf16[16,128,128]{2,1,0:T(8,128)(2,1)S(1)} collective-permute-done((bf16[16,128,128]{2,1,0:T(8,128)(2,1)S(1)}, bf16[16,128,128]{2,1,0:T(8,128)(2,1)S(1)}, u32[]{:S(2)}, u32[]{:S(2)}) %collective-permute-start.2) | collective-permute-done | bytes 524320 | tf_op jit(solution)/shard_map/ppermute | solution.py:25
  392.9 31.5 %collective-permute-start.3 = (bf16[16,128,128]{2,1,0:T(8,128)(2,1)S(1)}, bf16[16,128,128]{2,1,0:T(8,128)(2,1)S(1)}, u32[]{:S(2)}, u32[]{:S(2)}) collective-permute-start(bf16[16,128,128]{2,1,0:T(8,128)(2,1)S(1)} %add_convert_fusion.4), channel_id=1, source_target_pairs={{0,64},{8,72},{16,80},{24,88},{32,96},{40,104},{48,112},{56,120},{... | collective-permute-start | bytes 1572872 | tf_op jit(solution)/shard_map/ppermute | solution.py:25
  427.3 3.7 collective-permute-done.3
  431.4 34.9 %collective-permute-start.4 = (bf16[16,128,128]{2,1,0:T(8,128)(2,1)S(1)}, bf16[16,128,128]{2,1,0:T(8,128)(2,1)S(1)}, u32[]{:S(2)}, u32[]{:S(2)}) collective-permute-start(bf16[16,128,128]{2,1,0:T(8,128)(2,1)S(1)} %add_convert_fusion.3), channel_id=1, source_target_pairs={{0,128},{8,136},{16,144},{24,152},{32,160},{40,168},{48,176},{56,1... | collective-permute-start | bytes 1572872 | tf_op jit(solution)/shard_map/ppermute | solution.py:25
  466.4 2.3 convolution_bitcast_fusion.5
  471.3 5.4 %collective-permute-done.4 = bf16[16,128,128]{2,1,0:T(8,128)(2,1)S(1)} collective-permute-done((bf16[16,128,128]{2,1,0:T(8,128)(2,1)S(1)}, bf16[16,128,128]{2,1,0:T(8,128)(2,1)S(1)}, u32[]{:S(2)}, u32[]{:S(2)}) %collective-permute-start.4) | collective-permute-done | bytes 524320 | tf_op jit(solution)/shard_map/ppermute | solution.py:25
  476.7 2.0 fusion.12
  478.7 2.0 copy.121
  480.8 3.5 fusion.13
  484.3 2.0 copy.122
  486.3 5.5 %collective-permute-done.9 = bf16[16,128,128]{2,1,0:T(8,128)(2,1)} collective-permute-done((bf16[16,128,128]{2,1,0:T(8,128)(2,1)}, bf16[16,128,128]{2,1,0:T(8,128)(2,1)}, u32[]{:S(2)}, u32[]{:S(2)}) %collective-permute-start.9) | collective-permute-done | bytes 524320 | tf_op jit(solution)/shard_map/ppermute | solution.py:25
  491.8 3.9 fusion.10
  495.6 2.0 copy.123
  497.7 2.6 fusion.11
  501.3 2.4 reshape.143
  (90 shorter events, 31.4 us)
Async XLA Ops:
  22.3 82.4 %all-to-all-start = ((bf16[32,2,32,704]{3,2,1,0:T(8,128)(2,1)}), bf16[32,2,32,704]{3,2,1,0:T(8,128)(2,1)S(1)}, u32[]{:S(2)}, u32[]{:S(2)}) async-start(bf16[32,2,32,704]{3,2,1,0:T(8,128)(2,1)} %bitcast.14), calls=%async_computation | async-start | bytes 6291456 | tf_op jit(solution)/shard_map/all_to_all | solution.py:63
  33.6 467.7 %reduce-scatter.4.cloned.1.call-start = ((), (), s32[]{:S(2)}) async-start(), calls=%async_computation.3 | async-start | bytes 6488064
  324.6 1.0 copy-start.18
  324.6 1.7 copy-start.19
  325.8 1.7 copy-start.10
  326.3 4.5 copy-start.15
  326.4 18.1 %copy-start = (bf16[16,8,16,128]{3,2,1,0:T(8,128)(2,1)}, bf16[16,8,16,128]{3,2,1,0:T(8,128)(2,1)S(1)}, u32[]{:S(2)}) copy-start(bf16[16,8,16,128]{3,2,1,0:T(8,128)(2,1)S(1)} %copy.134) | copy-start | bytes 1572868
  327.5 13.6 %collective-permute-start = (bf16[16,128,128]{2,1,0:T(8,128)(2,1)}, bf16[16,128,128]{2,1,0:T(8,128)(2,1)S(1)}, u32[]{:S(2)}, u32[]{:S(2)}) collective-permute-start(bf16[16,128,128]{2,1,0:T(8,128)(2,1)} %get-tuple-element.25), channel_id=1, source_target_pairs={{0,8},{8,16},{16,24},{24,32},{32,40},{40,48},{48,56},{56,64},{64,7... | collective-permute-start | bytes 1572872 | tf_op jit(solution)/shard_map/ppermute | solution.py:25
  330.8 10.3 %copy-start.3 = (bf16[1,128,2048]{1,2,0:T(8,128)(2,1)}, bf16[1,128,2048]{1,2,0:T(8,128)(2,1)S(1)}, u32[]{:S(2)}) copy-start(bf16[1,128,2048]{1,2,0:T(8,128)(2,1)S(1)} %copy.131) | copy-start | bytes 1572868
  332.3 1.2 copy-start.5
  333.5 13.4 %collective-permute-start.5 = (bf16[16,128,128]{2,1,0:T(8,128)(2,1)S(1)}, bf16[16,128,128]{2,1,0:T(8,128)(2,1)S(1)}, u32[]{:S(2)}, u32[]{:S(2)}) collective-permute-start(bf16[16,128,128]{2,1,0:T(8,128)(2,1)S(1)} %get-tuple-element.27), channel_id=1, source_target_pairs={{8,0},{16,8},{24,16},{32,24},{40,32},{48,40},{56,48},{64,56},{72,6... | collective-permute-start | bytes 1572872 | tf_op jit(solution)/shard_map/ppermute | solution.py:25
  341.2 30.5 %copy-start.6 = (bf16[1,128,2048]{1,2,0:T(8,128)(2,1)S(1)}, bf16[1,128,2048]{1,2,0:T(8,128)(2,1)}, u32[]{:S(2)}) copy-start(bf16[1,128,2048]{1,2,0:T(8,128)(2,1)} %copy-done.5) | copy-start | bytes 1572868
  341.2 23.0 %collective-permute-start.1 = (bf16[16,128,128]{2,1,0:T(8,128)(2,1)S(1)}, bf16[16,128,128]{2,1,0:T(8,128)(2,1)S(1)}, u32[]{:S(2)}, u32[]{:S(2)}) collective-permute-start(bf16[16,128,128]{2,1,0:T(8,128)(2,1)S(1)} %fusion.15), channel_id=1, source_target_pairs={{0,16},{8,24},{16,32},{24,40},{32,48},{40,56},{48,64},{56,72},{64,... | collective-permute-start | bytes 1572872 | tf_op jit(solution)/shard_map/ppermute | solution.py:25
  347.1 28.1 %collective-permute-start.6 = (bf16[16,128,128]{2,1,0:T(8,128)(2,1)S(1)}, bf16[16,128,128]{2,1,0:T(8,128)(2,1)S(1)}, u32[]{:S(2)}, u32[]{:S(2)}) collective-permute-start(bf16[16,128,128]{2,1,0:T(8,128)(2,1)S(1)} %fusion.16), channel_id=1, source_target_pairs={{16,0},{24,8},{32,16},{40,24},{48,32},{56,40},{64,48},{72,56},{80,... | collective-permute-start | bytes 1572872 | tf_op jit(solution)/shard_map/ppermute | solution.py:25
  364.5 28.2 %collective-permute-start.2 = (bf16[16,128,128]{2,1,0:T(8,128)(2,1)S(1)}, bf16[16,128,128]{2,1,0:T(8,128)(2,1)S(1)}, u32[]{:S(2)}, u32[]{:S(2)}) collective-permute-start(bf16[16,128,128]{2,1,0:T(8,128)(2,1)S(1)} %add_convert_fusion.5), channel_id=1, source_target_pairs={{0,32},{8,40},{16,48},{24,56},{32,64},{40,72},{48,80},{56,88},{64,... | collective-permute-start | bytes 1572872 | tf_op jit(solution)/shard_map/ppermute | solution.py:25
  373.5 50.9 %copy-start.1 = (bf16[16,8,16,128]{3,2,1,0:T(8,128)(2,1)S(1)}, bf16[16,8,16,128]{3,2,1,0:T(8,128)(2,1)}, u32[]{:S(2)}) copy-start(bf16[16,8,16,128]{3,2,1,0:T(8,128)(2,1)} %copy-done) | copy-start | bytes 1572868
  375.4 50.2 %collective-permute-start.7 = (bf16[16,128,128]{2,1,0:T(8,128)(2,1)S(1)}, bf16[16,128,128]{2,1,0:T(8,128)(2,1)S(1)}, u32[]{:S(2)}, u32[]{:S(2)}) collective-permute-start(bf16[16,128,128]{2,1,0:T(8,128)(2,1)S(1)} %add_convert_fusion.2), channel_id=1, source_target_pairs={{32,0},{40,8},{48,16},{56,24},{64,32},{72,40},{80,48},{88,56},{96,... | collective-permute-start | bytes 1572872 | tf_op jit(solution)/shard_map/ppermute | solution.py:25
  392.6 84.1 %copy-start.9 = (bf16[16,128,128]{2,1,0:T(8,128)(2,1)}, bf16[16,128,128]{2,1,0:T(8,128)(2,1)S(1)}, u32[]{:S(2)}) copy-start(bf16[16,128,128]{2,1,0:T(8,128)(2,1)S(1)} %collective-permute-done.2) | copy-start | bytes 1572868
  392.9 38.1 %collective-permute-start.3 = (bf16[16,128,128]{2,1,0:T(8,128)(2,1)S(1)}, bf16[16,128,128]{2,1,0:T(8,128)(2,1)S(1)}, u32[]{:S(2)}, u32[]{:S(2)}) collective-permute-start(bf16[16,128,128]{2,1,0:T(8,128)(2,1)S(1)} %add_convert_fusion.4), channel_id=1, source_target_pairs={{0,64},{8,72},{16,80},{24,88},{32,96},{40,104},{48,112},{56,120},{... | collective-permute-start | bytes 1572872 | tf_op jit(solution)/shard_map/ppermute | solution.py:25
  425.6 40.8 %copy-start.16 = (bf16[128,16,128]{0,2,1:T(8,128)(2,1)S(1)}, bf16[128,16,128]{0,2,1:T(8,128)(2,1)}, u32[]{:S(2)}) copy-start(bf16[128,16,128]{0,2,1:T(8,128)(2,1)} %copy-done.15) | copy-start | bytes 1572868
  425.6 43.0 %copy-start.7 = (bf16[16,128,128]{2,1,0:T(8,128)(2,1)}, bf16[16,128,128]{2,1,0:T(8,128)(2,1)S(1)}, u32[]{:S(2)}) copy-start(bf16[16,128,128]{2,1,0:T(8,128)(2,1)S(1)} %collective-permute-done.7) | copy-start | bytes 1572868
  425.9 42.7 %collective-permute-start.8 = (bf16[16,128,128]{2,1,0:T(8,128)(2,1)S(1)}, bf16[16,128,128]{2,1,0:T(8,128)(2,1)S(1)}, u32[]{:S(2)}, u32[]{:S(2)}) collective-permute-start(bf16[16,128,128]{2,1,0:T(8,128)(2,1)S(1)} %add_convert_fusion.1), channel_id=1, source_target_pairs={{64,0},{72,8},{80,16},{88,24},{96,32},{104,40},{112,48},{120,56},{... | collective-permute-start | bytes 1572872 | tf_op jit(solution)/shard_map/ppermute | solution.py:25
  431.0 45.7 %copy-start.14 = (bf16[16,128,128]{2,1,0:T(8,128)(2,1)}, bf16[16,128,128]{2,1,0:T(8,128)(2,1)S(1)}, u32[]{:S(2)}) copy-start(bf16[16,128,128]{2,1,0:T(8,128)(2,1)S(1)} %collective-permute-done.3) | copy-start | bytes 1572868
  431.4 45.3 %collective-permute-start.4 = (bf16[16,128,128]{2,1,0:T(8,128)(2,1)S(1)}, bf16[16,128,128]{2,1,0:T(8,128)(2,1)S(1)}, u32[]{:S(2)}, u32[]{:S(2)}) collective-permute-start(bf16[16,128,128]{2,1,0:T(8,128)(2,1)S(1)} %add_convert_fusion.3), channel_id=1, source_target_pairs={{0,128},{8,136},{16,144},{24,152},{32,160},{40,168},{48,176},{56,1... | collective-permute-start | bytes 1572872 | tf_op jit(solution)/shard_map/ppermute | solution.py:25
  468.6 1.2 copy-start.12
  469.9 10.9 %copy-start.4 = (bf16[1,128,2048]{1,2,0:T(8,128)(2,1)S(1)}, bf16[1,128,2048]{1,2,0:T(8,128)(2,1)}, u32[]{:S(2)}) copy-start(bf16[1,128,2048]{1,2,0:T(8,128)(2,1)} %copy-done.3) | copy-start | bytes 1572868
  469.9 21.9 %collective-permute-start.9 = (bf16[16,128,128]{2,1,0:T(8,128)(2,1)}, bf16[16,128,128]{2,1,0:T(8,128)(2,1)}, u32[]{:S(2)}, u32[]{:S(2)}) collective-permute-start(bf16[16,128,128]{2,1,0:T(8,128)(2,1)} %add_convert_fusion), channel_id=1, source_target_pairs={{128,0},{136,8},{144,16},{152,24},{160,32},{168,40},{176,48},{184,... | collective-permute-start | bytes 1572872 | tf_op jit(solution)/shard_map/ppermute | solution.py:25
  476.7 2.0 copy-start.17
  480.8 11.0 %copy-start.2 = (bf16[16,8,16,128]{3,2,1,0:T(8,128)(2,1)S(1)}, bf16[16,8,16,128]{3,2,1,0:T(8,128)(2,1)}, u32[]{:S(2)}) copy-start(bf16[16,8,16,128]{3,2,1,0:T(8,128)(2,1)} %copy-done) | copy-start | bytes 1572868
  486.3 11.4 %copy-start.8 = (bf16[16,128,128]{2,1,0:T(8,128)(2,1)S(1)}, bf16[16,128,128]{2,1,0:T(8,128)(2,1)}, u32[]{:S(2)}) copy-start(bf16[16,128,128]{2,1,0:T(8,128)(2,1)} %copy-done.7) | copy-start | bytes 1572868
  486.3 11.4 %copy-start.11 = (bf16[16,8,16,128]{3,2,1,0:T(8,128)(2,1)S(1)}, bf16[16,8,16,128]{3,2,1,0:T(8,128)(2,1)}, u32[]{:S(2)}) copy-start(bf16[16,8,16,128]{3,2,1,0:T(8,128)(2,1)} %copy-done.10) | copy-start | bytes 1572868
  486.3 11.4 %copy-start.13 = (bf16[16,128,128]{2,1,0:T(8,128)(2,1)S(1)}, bf16[16,128,128]{2,1,0:T(8,128)(2,1)}, u32[]{:S(2)}) copy-start(bf16[16,128,128]{2,1,0:T(8,128)(2,1)} %copy-done.12) | copy-start | bytes 1572868
Sparse Core Ops, SparseCore 0:
  324.8 40.1 reduce-scatter.3

commit v2 on v1

--- a/solution.py
+++ b/solution.py
@@ -51,17 +51,30 @@
         gates[0].reshape(assigned, 1)
         * hidden[0].reshape(assigned, hidden_units).astype(jnp.float32)
     ).astype(jnp.bfloat16)
+    lanes = -(-(hidden_units + 1) // 128) * 128
+    token_tag = (jnp.arange(assigned, dtype=jnp.int32) // TOPK + 1).astype(jnp.bfloat16)
+    tagged = jnp.concatenate(
+        [
+            scaled,
+            token_tag[:, None],
+            jnp.zeros((assigned, lanes - hidden_units - 1), jnp.bfloat16),
+        ],
+        axis=1,
+    )
     hidden_slots = jnp.dot(
-        pick.astype(jnp.bfloat16), scaled, preferred_element_type=jnp.float32
+        pick.astype(jnp.bfloat16), tagged, preferred_element_type=jnp.float32
     ).astype(jnp.bfloat16)
-    pick_token = jnp.any(pick.reshape(slots, tokens, TOPK), axis=2)
-    cot_slots = jnp.dot(
-        pick_token.astype(jnp.bfloat16), cotangent[0], preferred_element_type=jnp.float32
-    ).astype(jnp.bfloat16)
-    hidden_slots = hidden_slots.reshape(seq_count, EXP_DEV, CAP, hidden_units)
-    cot_slots = cot_slots.reshape(seq_count, EXP_DEV, CAP, width)
-    arrived_hidden = lax.all_to_all(hidden_slots, "seq", split_axis=0, concat_axis=0, tiled=True)
-    arrived_cot = lax.all_to_all(cot_slots, "seq", split_axis=0, concat_axis=0, tiled=True)
+    hidden_slots = hidden_slots.reshape(seq_count, EXP_DEV, CAP, lanes)
+    arrived = lax.all_to_all(hidden_slots, "seq", split_axis=0, concat_axis=0, tiled=True)
+    all_cotangent = lax.all_gather(cotangent, "seq", axis=1, tiled=True)[0]
+    arrived_hidden = arrived[..., :hidden_units]
+    slot_token = jnp.maximum(arrived[..., hidden_units].astype(jnp.int32) - 1, 0)
+    wanted = (
+        jnp.arange(seq_count, dtype=jnp.int32)[:, None, None] * tokens + slot_token
+    ).reshape(-1)
+    arrived_cot = jnp.take(all_cotangent, wanted, axis=0).reshape(
+        seq_count, EXP_DEV, CAP, width
+    )
 
     query_raw = query[0].reshape(tokens, HEADS, head_dim)
     key_raw = key_in[0].reshape(tokens, HEADS, head_dim)

time: 515 us -> 434 us (0.84)
  the two profiles are of different devices: /device:TPU:32 before, /device:TPU:88 now
where the time goes in v2:
time: 434 us; the launch traced here: 428 us
  waiting for transfers between devices  219 us (50%)
  starting transfers between devices  74.7 us (17%)
  local copies, waits for them, and re-layouts  67.3 us (16%)
  matrix products  44.7 us (10%)
  between operations  15 us (3%)
  other arithmetic  6.91 us (2%)
    all_to_all x1, waiting for transfers between devices, per_device(): lax.all_to_all(hidden_slots, 'seq', split_axis=0, concat_axis=0, tiled=True)  90.3 us
    all_gather x1, waiting for transfers between devices, per_device(): all_cotangent = lax.all_gather(cotangent, 'seq', axis=1, tiled=True)[0]  70.1 us
    ppermute x10, starting transfers between devices, exclusive_scan(): arrived = lax.ppermute(window.astype(jnp.bfloat16), axis, pairs)  64 us
    ppermute x10, waiting for transfers between devices, exclusive_scan(): arrived = lax.ppermute(window.astype(jnp.bfloat16), axis, pairs)  58.2 us
    unnamed x56, local copies, waits for them, and re-layouts  35 us
    gather x1, local copies, waits for them, and re-layouts, per_device(): jnp.take(all_cotangent, wanted, axis=0)  24.5 us
    dot_general x1, matrix products, per_device(): jnp.einsum('sxcf,sxcd->xfd', arrived_hidden, arrived_cot, preferred_eleme...  15.3 us
    all_to_all x1, starting transfers between devices, per_device(): lax.all_to_all(hidden_slots, 'seq', split_axis=0, concat_axis=0, tiled=True)  10.6 us
  transfers between devices with their start and end apart: 13, of which 8 were waited for; matrix products, arithmetic and copies ran while one was open for 13% of the time, Pallas kernels for 0%

profile of v2, /device:TPU:88, one launch (start us, length us, event | category | flops | bytes accessed | tf_op | source)
XLA Modules:
  0.0 427.9 jit_solution(12064112105560147103)
XLA Ops:
  12.0 2.0 copy.88
  17.9 4.7 %fusion.4 = bf16[2048,768]{1,0:T(8,128)(2,1)} fusion(s32[768]{0:T(1024)S(1)} %multiply_add_fusion, bf16[768,1]{1,0:T(8,128)(2,1)S(1)} %fusion.35, bf16[768,704]{1,0:T(8,128)(2,1)S(1)} %multiply_convert_fusion, bf16[768]{0:T(1024)(128)(2,1)S(1)} %pad.2.clone), kind=kOutput, calls=%fused_computation.8 | convolution fusion | flops 2422603776 | bytes 4233216 | tf_op jit(solution)/shard_map/dot_general | solution.py:64
  22.6 10.6 %all-to-all-start = ((bf16[32,2,32,768]{3,2,1,0:T(8,128)(2,1)}), bf16[32,2,32,768]{3,2,1,0:T(8,128)(2,1)S(1)}, u32[]{:S(2)}, u32[]{:S(2)}) async-start(bf16[32,2,32,768]{3,2,1,0:T(8,128)(2,1)} %bitcast.119), calls=%async_computation | async-start | bytes 6291456 | tf_op jit(solution)/shard_map/all_to_all | solution.py:68
  33.5 90.3 %all-to-all-done = bf16[32,2,32,768]{3,2,1,0:T(8,128)(2,1)S(1)} async-done(((bf16[32,2,32,768]{3,2,1,0:T(8,128)(2,1)}), bf16[32,2,32,768]{3,2,1,0:T(8,128)(2,1)S(1)}, u32[]{:S(2)}, u32[]{:S(2)}) %all-to-all-start) | async-done | bytes 3145760 | tf_op jit(solution)/shard_map/all_to_all | solution.py:68
  126.9 70.1 %all-gather.2.cloned.1.call-done = bf16[1,4096,2048]{2,1,0:T(8,128)(2,1)} async-done(((bf16[1,128,2048]{2,1,0:T(8,128)(2,1)}), bf16[1,4096,2048]{2,1,0:T(8,128)(2,1)}) %all-gather.2.cloned.1.call-update) | async-done | bytes 16777232 | tf_op jit(solution)/shard_map/all_gather | solution.py:69
  197.0 24.5 %gather_fusion = bf16[2048,2048]{1,0:T(8,128)(2,1)} fusion(bf16[4096,2048]{1,0:T(8,128)(2,1)} %bitcast.99, s32[2048]{0:T(1024)S(1)} %broadcast_clamp_fusion), kind=kCustom, calls=%fused_computation | custom fusion | bytes 16785408 | tf_op jit(solution)/shard_map/jit(_take)/gather | solution.py:75
  221.5 15.3 %bitcast_convert_fusion = bf16[2,704,2048]{2,1,0:T(8,128)(2,1)S(1)} fusion(bf16[32,2,32,2048]{3,2,1,0:T(8,128)(2,1)} %bitcast.114, pred[32,2,32]{0,2,1:T(8,128)(4,1)S(1)} %copy.91, bf16[32,2,32,704]{3,2,1,0:T(8,128)(2,1)} %bitcast.118), kind=kOutput, calls=%fused_computation.1 | convolution fusion | flops 5912657920 | bytes 17041408 | tf_op jit(solution)/shard_map/sxcf,sxcd->xfd/dot_general | solution.py:120
  236.9 12.2 %copy.104 = bf16[2,704,2048]{2,0,1:T(2,128)(2,1)S(1)} copy(bf16[2,704,2048]{2,1,0:T(8,128)(2,1)S(1)} %bitcast_convert_fusion) | data formatting | bytes 11534336
  249.1 6.2 %copy.112 = bf16[88,8,2,2048]{3,1,2,0:T(8,128)(2,1)} copy(bf16[88,8,2,2048]{3,2,1,0:T(2,128)(2,1)S(1)} %bitcast.101) | data formatting | bytes 11534336
  258.1 3.0 collective-permute-start
  265.2 2.9 collective-permute-start.5
  271.6 2.5 collective-permute-done
  274.3 5.3 %collective-permute-start.1 = (bf16[16,128,128]{2,1,0:T(8,128)(2,1)S(1)}, bf16[16,128,128]{2,1,0:T(8,128)(2,1)S(1)}, u32[]{:S(2)}, u32[]{:S(2)}) collective-permute-start(bf16[16,128,128]{2,1,0:T(8,128)(2,1)S(1)} %fusion.21), channel_id=1, source_target_pairs={{0,16},{8,24},{16,32},{24,40},{32,48},{40,56},{48,64},{56,72},{64,... | collective-permute-start | bytes 1572872 | tf_op jit(solution)/shard_map/ppermute | solution.py:25
  281.3 2.7 collective-permute-start.6
  284.0 17.1 %collective-permute-done.1 = bf16[16,128,128]{2,1,0:T(8,128)(2,1)S(1)} collective-permute-done((bf16[16,128,128]{2,1,0:T(8,128)(2,1)S(1)}, bf16[16,128,128]{2,1,0:T(8,128)(2,1)S(1)}, u32[]{:S(2)}, u32[]{:S(2)}) %collective-permute-start.1) | collective-permute-done | bytes 524320 | tf_op jit(solution)/shard_map/ppermute | solution.py:25
  301.3 1.9 collective-permute-start.2
  305.2 8.7 %collective-permute-start.7 = (bf16[16,128,128]{2,1,0:T(8,128)(2,1)S(1)}, bf16[16,128,128]{2,1,0:T(8,128)(2,1)S(1)}, u32[]{:S(2)}, u32[]{:S(2)}) collective-permute-start(bf16[16,128,128]{2,1,0:T(8,128)(2,1)S(1)} %add_convert_fusion.2), channel_id=1, source_target_pairs={{32,0},{40,8},{48,16},{56,24},{64,32},{72,40},{80,48},{88,56},{96,... | collective-permute-start | bytes 1572872 | tf_op jit(solution)/shard_map/ppermute | solution.py:25
  313.9 6.3 %collective-permute-done.2 = bf16[16,128,128]{2,1,0:T(8,128)(2,1)S(1)} collective-permute-done((bf16[16,128,128]{2,1,0:T(8,128)(2,1)S(1)}, bf16[16,128,128]{2,1,0:T(8,128)(2,1)S(1)}, u32[]{:S(2)}, u32[]{:S(2)}) %collective-permute-start.2) | collective-permute-done | bytes 524320 | tf_op jit(solution)/shard_map/ppermute | solution.py:25
  323.0 22.3 %collective-permute-done.7 = bf16[16,128,128]{2,1,0:T(8,128)(2,1)S(1)} collective-permute-done((bf16[16,128,128]{2,1,0:T(8,128)(2,1)S(1)}, bf16[16,128,128]{2,1,0:T(8,128)(2,1)S(1)}, u32[]{:S(2)}, u32[]{:S(2)}) %collective-permute-start.7) | collective-permute-done | bytes 524320 | tf_op jit(solution)/shard_map/ppermute | solution.py:25
  345.6 7.1 %collective-permute-start.8 = (bf16[16,128,128]{2,1,0:T(8,128)(2,1)S(1)}, bf16[16,128,128]{2,1,0:T(8,128)(2,1)S(1)}, u32[]{:S(2)}, u32[]{:S(2)}) collective-permute-start(bf16[16,128,128]{2,1,0:T(8,128)(2,1)S(1)} %add_convert_fusion.1), channel_id=1, source_target_pairs={{64,0},{72,8},{80,16},{88,24},{96,32},{104,40},{112,48},{120,56},{... | collective-permute-start | bytes 1572872 | tf_op jit(solution)/shard_map/ppermute | solution.py:25
  352.8 3.3 collective-permute-done.3
  357.8 2.3 convolution_bitcast_fusion.5
  361.3 29.8 %collective-permute-start.9 = (bf16[16,128,128]{2,1,0:T(8,128)(2,1)}, bf16[16,128,128]{2,1,0:T(8,128)(2,1)}, u32[]{:S(2)}, u32[]{:S(2)}) collective-permute-start(bf16[16,128,128]{2,1,0:T(8,128)(2,1)} %add_convert_fusion), channel_id=1, source_target_pairs={{128,0},{136,8},{144,16},{152,24},{160,32},{168,40},{176,48},{184,... | collective-permute-start | bytes 1572872 | tf_op jit(solution)/shard_map/ppermute | solution.py:25
  391.1 6.7 %collective-permute-done.4 = bf16[16,128,128]{2,1,0:T(8,128)(2,1)S(1)} collective-permute-done((bf16[16,128,128]{2,1,0:T(8,128)(2,1)S(1)}, bf16[16,128,128]{2,1,0:T(8,128)(2,1)S(1)}, u32[]{:S(2)}, u32[]{:S(2)}) %collective-permute-start.4) | collective-permute-done | bytes 524320 | tf_op jit(solution)/shard_map/ppermute | solution.py:25
  397.8 2.0 fusion.15
  399.8 2.0 copy.95
  401.9 3.5 fusion.16
  405.4 2.0 copy.96
  407.4 4.0 fusion.13
  411.4 2.0 copy.97
  413.5 2.6 fusion.14
  417.1 2.4 reshape.242
  (105 shorter events, 34.4 us)
Async XLA Ops:
  7.2 189.9 %all-gather.2.cloned.1.call-start = ((), (), s32[]{:S(2)}) async-start(), calls=%async_computation.2 | async-start | bytes 17301504 | tf_op jit(solution)/shard_map/all_gather | solution.py:69
  22.6 101.1 %all-to-all-start = ((bf16[32,2,32,768]{3,2,1,0:T(8,128)(2,1)}), bf16[32,2,32,768]{3,2,1,0:T(8,128)(2,1)S(1)}, u32[]{:S(2)}, u32[]{:S(2)}) async-start(bf16[32,2,32,768]{3,2,1,0:T(8,128)(2,1)} %bitcast.119), calls=%async_computation | async-start | bytes 6291456 | tf_op jit(solution)/shard_map/all_to_all | solution.py:68
  33.3 383.8 %reduce-scatter.4.cloned.1.call-start = ((), (), s32[]{:S(2)}) async-start(), calls=%async_computation.3 | async-start | bytes 6488064
  123.8 97.8 %copy-start.17 = (bf16[32,2,32,768]{3,2,1,0:T(8,128)(2,1)}, bf16[32,2,32,768]{3,2,1,0:T(8,128)(2,1)S(1)}, u32[]{:S(2)}) copy-start(bf16[32,2,32,768]{3,2,1,0:T(8,128)(2,1)S(1)} %all-to-all-done) | copy-start | bytes 9437188
  255.2 1.7 copy-start.20
  256.4 1.7 copy-start.10
  256.9 5.6 %copy-start.15 = (bf16[128,16,128]{0,2,1:T(8,128)(2,1)}, bf16[128,16,128]{0,2,1:T(8,128)(2,1)S(1)}, u32[]{:S(2)}) copy-start(bf16[128,16,128]{0,2,1:T(8,128)(2,1)S(1)} %copy.71) | copy-start | bytes 1572868
  257.0 22.6 %copy-start = (bf16[16,8,16,128]{3,2,1,0:T(8,128)(2,1)}, bf16[16,8,16,128]{3,2,1,0:T(8,128)(2,1)S(1)}, u32[]{:S(2)}) copy-start(bf16[16,8,16,128]{3,2,1,0:T(8,128)(2,1)S(1)} %copy.111) | copy-start | bytes 1572868
  258.1 16.0 %collective-permute-start = (bf16[16,128,128]{2,1,0:T(8,128)(2,1)}, bf16[16,128,128]{2,1,0:T(8,128)(2,1)S(1)}, u32[]{:S(2)}, u32[]{:S(2)}) collective-permute-start(bf16[16,128,128]{2,1,0:T(8,128)(2,1)} %get-tuple-element.20), channel_id=1, source_target_pairs={{0,8},{8,16},{16,24},{24,32},{32,40},{40,48},{48,56},{56,64},{64,7... | collective-permute-start | bytes 1572872 | tf_op jit(solution)/shard_map/ppermute | solution.py:25
  262.4 9.2 %copy-start.3 = (bf16[1,128,2048]{1,2,0:T(8,128)(2,1)}, bf16[1,128,2048]{1,2,0:T(8,128)(2,1)S(1)}, u32[]{:S(2)}) copy-start(bf16[1,128,2048]{1,2,0:T(8,128)(2,1)S(1)} %copy.108) | copy-start | bytes 1572868
  264.0 1.2 copy-start.5
  265.2 16.0 %collective-permute-start.5 = (bf16[16,128,128]{2,1,0:T(8,128)(2,1)S(1)}, bf16[16,128,128]{2,1,0:T(8,128)(2,1)S(1)}, u32[]{:S(2)}, u32[]{:S(2)}) collective-permute-start(bf16[16,128,128]{2,1,0:T(8,128)(2,1)S(1)} %get-tuple-element.22), channel_id=1, source_target_pairs={{8,0},{16,8},{24,16},{32,24},{40,32},{48,40},{56,48},{64,56},{72,6... | collective-permute-start | bytes 1572872 | tf_op jit(solution)/shard_map/ppermute | solution.py:25
  274.2 29.0 %copy-start.6 = (bf16[1,128,2048]{1,2,0:T(8,128)(2,1)S(1)}, bf16[1,128,2048]{1,2,0:T(8,128)(2,1)}, u32[]{:S(2)}) copy-start(bf16[1,128,2048]{1,2,0:T(8,128)(2,1)} %copy-done.5) | copy-start | bytes 1572868
  274.3 26.8 %collective-permute-start.1 = (bf16[16,128,128]{2,1,0:T(8,128)(2,1)S(1)}, bf16[16,128,128]{2,1,0:T(8,128)(2,1)S(1)}, u32[]{:S(2)}, u32[]{:S(2)}) collective-permute-start(bf16[16,128,128]{2,1,0:T(8,128)(2,1)S(1)} %fusion.21), channel_id=1, source_target_pairs={{0,16},{8,24},{16,32},{24,40},{32,48},{40,56},{48,64},{56,72},{64,... | collective-permute-start | bytes 1572872 | tf_op jit(solution)/shard_map/ppermute | solution.py:25
  281.3 23.7 %collective-permute-start.6 = (bf16[16,128,128]{2,1,0:T(8,128)(2,1)S(1)}, bf16[16,128,128]{2,1,0:T(8,128)(2,1)S(1)}, u32[]{:S(2)}, u32[]{:S(2)}) collective-permute-start(bf16[16,128,128]{2,1,0:T(8,128)(2,1)S(1)} %fusion.22), channel_id=1, source_target_pairs={{16,0},{24,8},{32,16},{40,24},{48,32},{56,40},{64,48},{72,56},{80,... | collective-permute-start | bytes 1572872 | tf_op jit(solution)/shard_map/ppermute | solution.py:25
  301.3 19.0 %collective-permute-start.2 = (bf16[16,128,128]{2,1,0:T(8,128)(2,1)S(1)}, bf16[16,128,128]{2,1,0:T(8,128)(2,1)S(1)}, u32[]{:S(2)}, u32[]{:S(2)}) collective-permute-start(bf16[16,128,128]{2,1,0:T(8,128)(2,1)S(1)} %add_convert_fusion.5), channel_id=1, source_target_pairs={{0,32},{8,40},{16,48},{24,56},{32,64},{40,72},{48,80},{56,88},{64,... | collective-permute-start | bytes 1572872 | tf_op jit(solution)/shard_map/ppermute | solution.py:25
  305.0 16.9 %copy-start.1 = (bf16[16,8,16,128]{3,2,1,0:T(8,128)(2,1)S(1)}, bf16[16,8,16,128]{3,2,1,0:T(8,128)(2,1)}, u32[]{:S(2)}) copy-start(bf16[16,8,16,128]{3,2,1,0:T(8,128)(2,1)} %copy-done) | copy-start | bytes 1572868
  305.2 40.1 %collective-permute-start.7 = (bf16[16,128,128]{2,1,0:T(8,128)(2,1)S(1)}, bf16[16,128,128]{2,1,0:T(8,128)(2,1)S(1)}, u32[]{:S(2)}, u32[]{:S(2)}) collective-permute-start(bf16[16,128,128]{2,1,0:T(8,128)(2,1)S(1)} %add_convert_fusion.2), channel_id=1, source_target_pairs={{32,0},{40,8},{48,16},{56,24},{64,32},{72,40},{80,48},{88,56},{96,... | collective-permute-start | bytes 1572872 | tf_op jit(solution)/shard_map/ppermute | solution.py:25
  320.3 77.6 %copy-start.9 = (bf16[16,128,128]{2,1,0:T(8,128)(2,1)}, bf16[16,128,128]{2,1,0:T(8,128)(2,1)S(1)}, u32[]{:S(2)}) copy-start(bf16[16,128,128]{2,1,0:T(8,128)(2,1)S(1)} %collective-permute-done.2) | copy-start | bytes 1572868
  320.5 35.5 %collective-permute-start.3 = (bf16[16,128,128]{2,1,0:T(8,128)(2,1)S(1)}, bf16[16,128,128]{2,1,0:T(8,128)(2,1)S(1)}, u32[]{:S(2)}, u32[]{:S(2)}) collective-permute-start(bf16[16,128,128]{2,1,0:T(8,128)(2,1)S(1)} %add_convert_fusion.4), channel_id=1, source_target_pairs={{0,64},{8,72},{16,80},{24,88},{32,96},{40,104},{48,112},{56,120},{... | collective-permute-start | bytes 1572872 | tf_op jit(solution)/shard_map/ppermute | solution.py:25
  323.0 34.7 %copy-start.16 = (bf16[128,16,128]{0,2,1:T(8,128)(2,1)S(1)}, bf16[128,16,128]{0,2,1:T(8,128)(2,1)}, u32[]{:S(2)}) copy-start(bf16[128,16,128]{0,2,1:T(8,128)(2,1)} %copy-done.15) | copy-start | bytes 1572868
  345.3 14.7 %copy-start.7 = (bf16[16,128,128]{2,1,0:T(8,128)(2,1)}, bf16[16,128,128]{2,1,0:T(8,128)(2,1)S(1)}, u32[]{:S(2)}) copy-start(bf16[16,128,128]{2,1,0:T(8,128)(2,1)S(1)} %collective-permute-done.7) | copy-start | bytes 1572868
  345.6 14.4 %collective-permute-start.8 = (bf16[16,128,128]{2,1,0:T(8,128)(2,1)S(1)}, bf16[16,128,128]{2,1,0:T(8,128)(2,1)S(1)}, u32[]{:S(2)}, u32[]{:S(2)}) collective-permute-start(bf16[16,128,128]{2,1,0:T(8,128)(2,1)S(1)} %add_convert_fusion.1), channel_id=1, source_target_pairs={{64,0},{72,8},{80,16},{88,24},{96,32},{104,40},{112,48},{120,56},{... | collective-permute-start | bytes 1572872 | tf_op jit(solution)/shard_map/ppermute | solution.py:25
  356.1 41.8 %copy-start.14 = (bf16[16,128,128]{2,1,0:T(8,128)(2,1)}, bf16[16,128,128]{2,1,0:T(8,128)(2,1)S(1)}, u32[]{:S(2)}) copy-start(bf16[16,128,128]{2,1,0:T(8,128)(2,1)S(1)} %collective-permute-done.3) | copy-start | bytes 1572868
  356.4 41.4 %collective-permute-start.4 = (bf16[16,128,128]{2,1,0:T(8,128)(2,1)S(1)}, bf16[16,128,128]{2,1,0:T(8,128)(2,1)S(1)}, u32[]{:S(2)}, u32[]{:S(2)}) collective-permute-start(bf16[16,128,128]{2,1,0:T(8,128)(2,1)S(1)} %add_convert_fusion.3), channel_id=1, source_target_pairs={{0,128},{8,136},{16,144},{24,152},{32,160},{40,168},{48,176},{56,1... | collective-permute-start | bytes 1572872 | tf_op jit(solution)/shard_map/ppermute | solution.py:25
  361.3 40.6 %copy-start.4 = (bf16[1,128,2048]{1,2,0:T(8,128)(2,1)S(1)}, bf16[1,128,2048]{1,2,0:T(8,128)(2,1)}, u32[]{:S(2)}) copy-start(bf16[1,128,2048]{1,2,0:T(8,128)(2,1)} %copy-done.3) | copy-start | bytes 1572868
  361.3 46.2 %collective-permute-start.9 = (bf16[16,128,128]{2,1,0:T(8,128)(2,1)}, bf16[16,128,128]{2,1,0:T(8,128)(2,1)}, u32[]{:S(2)}, u32[]{:S(2)}) collective-permute-start(bf16[16,128,128]{2,1,0:T(8,128)(2,1)} %add_convert_fusion), channel_id=1, source_target_pairs={{128,0},{136,8},{144,16},{152,24},{160,32},{168,40},{176,48},{184,... | collective-permute-start | bytes 1572872 | tf_op jit(solution)/shard_map/ppermute | solution.py:25
  397.8 2.0 copy-start.18
  401.9 5.5 %copy-start.2 = (bf16[16,8,16,128]{3,2,1,0:T(8,128)(2,1)S(1)}, bf16[16,8,16,128]{3,2,1,0:T(8,128)(2,1)}, u32[]{:S(2)}) copy-start(bf16[16,8,16,128]{3,2,1,0:T(8,128)(2,1)} %copy-done) | copy-start | bytes 1572868
  407.4 6.0 %copy-start.8 = (bf16[16,128,128]{2,1,0:T(8,128)(2,1)S(1)}, bf16[16,128,128]{2,1,0:T(8,128)(2,1)}, u32[]{:S(2)}) copy-start(bf16[16,128,128]{2,1,0:T(8,128)(2,1)} %copy-done.7) | copy-start | bytes 1572868
  407.4 6.0 %copy-start.11 = (bf16[16,8,16,128]{3,2,1,0:T(8,128)(2,1)S(1)}, bf16[16,8,16,128]{3,2,1,0:T(8,128)(2,1)}, u32[]{:S(2)}) copy-start(bf16[16,8,16,128]{3,2,1,0:T(8,128)(2,1)} %copy-done.10) | copy-start | bytes 1572868
  407.4 6.0 %copy-start.13 = (bf16[16,128,128]{2,1,0:T(8,128)(2,1)S(1)}, bf16[16,128,128]{2,1,0:T(8,128)(2,1)}, u32[]{:S(2)}) copy-start(bf16[16,128,128]{2,1,0:T(8,128)(2,1)} %copy-done.12) | copy-start | bytes 1572868
  (2 other events, 2.3 us)
Sparse Core Ops, SparseCore 0:
  10.6 186.3 all-gather.1
  255.4 43.3 reduce-scatter.3

commit v3 on v2

--- a/solution.py
+++ b/solution.py
@@ -12,20 +12,24 @@
 PRECISE = lax.Precision.HIGHEST
 
 
-def exclusive_scan(local_sum, axis, backward):
+def exclusive_scan(local_sum, axis, backward, radix=4):
     count = lax.axis_size(axis)
     window = local_sum
     total = jnp.zeros_like(local_sum)
-    shift = 1
-    while shift < count:
-        if backward:
-            pairs = [(src, src - shift) for src in range(shift, count)]
-        else:
-            pairs = [(src, src + shift) for src in range(count - shift)]
-        arrived = lax.ppermute(window.astype(jnp.bfloat16), axis, pairs)
-        total = total + arrived.astype(jnp.float32)
+    stride = 1
+    while stride < count:
+        sent = window.astype(jnp.bfloat16)
+        for step in range(1, radix):
+            shift = step * stride
+            if shift >= count:
+                break
+            if backward:
+                pairs = [(src, src - shift) for src in range(shift, count)]
+            else:
+                pairs = [(src, src + shift) for src in range(count - shift)]
+            total = total + lax.ppermute(sent, axis, pairs).astype(jnp.float32)
         window = local_sum + total
-        shift *= 2
+        stride *= radix
     return total
 
 
@@ -72,9 +76,6 @@
     wanted = (
         jnp.arange(seq_count, dtype=jnp.int32)[:, None, None] * tokens + slot_token
     ).reshape(-1)
-    arrived_cot = jnp.take(all_cotangent, wanted, axis=0).reshape(
-        seq_count, EXP_DEV, CAP, width
-    )
 
     query_raw = query[0].reshape(tokens, HEADS, head_dim)
     key_raw = key_in[0].reshape(tokens, HEADS, head_dim)
@@ -117,6 +118,12 @@
     def to_shard(array):
         return array.reshape(1, tokens, width).astype(jnp.bfloat16)
 
+    outputs, grad_q, grad_k, grad_v, arrived_hidden, wanted = lax.optimization_barrier(
+        (outputs, grad_q, grad_k, grad_v, arrived_hidden, wanted)
+    )
+    arrived_cot = jnp.take(all_cotangent, wanted, axis=0).reshape(
+        seq_count, EXP_DEV, CAP, width
+    )
     group_term = jnp.einsum(
         "sxcf,sxcd->xfd", arrived_hidden, arrived_cot, preferred_element_type=jnp.float32
     )

time: 434 us -> 509 us (1.17)
  the two profiles are of different devices: /device:TPU:88 before, /device:TPU:32 now
where the time goes in v3:
time: 509 us; the launch traced here: 500 us
  waiting for transfers between devices  234 us (46%)
  starting transfers between devices  137 us (27%)
  local copies, waits for them, and re-layouts  58.9 us (12%)
  other arithmetic  28.8 us (6%)
  matrix products  26.9 us (5%)
  between operations  15 us (3%)
    ppermute x14, waiting for transfers between devices, exclusive_scan(): total = total + lax.ppermute(sent, axis, pairs).astype(jnp.float32)  196 us
    ppermute x14, starting transfers between devices, exclusive_scan(): total = total + lax.ppermute(sent, axis, pairs).astype(jnp.float32)  125 us
    unnamed x3, waiting for transfers between devices  37.4 us
    unnamed x24, local copies, waits for them, and re-layouts  28.2 us
    gather x1, local copies, waits for them, and re-layouts, per_device(): jnp.take(all_cotangent, wanted, axis=0)  24.5 us
    select_n x1, other arithmetic, per_device(): jnp.take(all_cotangent, wanted, axis=0)  15.6 us
    all_to_all x1, starting transfers between devices, per_device(): lax.all_to_all(hidden_slots, 'seq', split_axis=0, concat_axis=0, tiled=True)  11.5 us
  transfers between devices with their start and end apart: 17, of which 7 were waited for; matrix products, arithmetic and copies ran while one was open for 8% of the time, Pallas kernels for 0%

profile of v3, /device:TPU:32, one launch (start us, length us, event | category | flops | bytes accessed | tf_op | source)
XLA Modules:
  0.0 500.3 jit_solution(2556502081858474577)
XLA Ops:
  9.9 1.8 reduce-window.6
  12.0 2.0 copy.108
  14.1 1.6 reshape.188
  16.0 1.9 multiply_convert_fusion
  17.9 4.7 fusion.5
  22.6 11.5 %all-to-all-start = ((bf16[32,2,32,768]{3,2,1,0:T(8,128)(2,1)}), bf16[32,2,32,768]{3,2,1,0:T(8,128)(2,1)}, u32[]{:S(2)}, u32[]{:S(2)}) async-start(bf16[32,2,32,768]{3,2,1,0:T(8,128)(2,1)} %bitcast.10), calls=%async_computation | async-start | bytes 6291456 | tf_op jit(solution)/shard_map/all_to_all | solution.py:72
  34.9 2.2 fusion.52
  39.8 2.2 collective-permute-start.7
  43.4 9.0 %collective-permute-start.2 = (bf16[16,128,128]{2,1,0:T(8,128)(2,1)}, bf16[16,128,128]{2,1,0:T(8,128)(2,1)}, u32[]{:S(2)}, u32[]{:S(2)}) collective-permute-start(bf16[16,128,128]{2,1,0:T(8,128)(2,1)} %get-tuple-element.31), channel_id=1, source_target_pairs={{0,24},{8,32},{16,40},{24,48},{32,56},{40,64},{48,72},{56,80},{64,... | collective-permute-start | bytes 1572872 | tf_op jit(solution)/shard_map/ppermute | solution.py:30
  52.4 4.8 collective-permute-start.1
  60.6 110.2 %collective-permute-done.9 = bf16[16,128,128]{2,1,0:T(8,128)(2,1)} collective-permute-done((bf16[16,128,128]{2,1,0:T(8,128)(2,1)}, bf16[16,128,128]{2,1,0:T(8,128)(2,1)}, u32[]{:S(2)}, u32[]{:S(2)}) %collective-permute-start.9) | collective-permute-done | bytes 524320 | tf_op jit(solution)/shard_map/ppermute | solution.py:30
  170.8 3.8 collective-permute-start
  174.6 26.9 %collective-permute-done.8 = bf16[16,128,128]{2,1,0:T(8,128)(2,1)} collective-permute-done((bf16[16,128,128]{2,1,0:T(8,128)(2,1)}, bf16[16,128,128]{2,1,0:T(8,128)(2,1)}, u32[]{:S(2)}, u32[]{:S(2)}) %collective-permute-start.8) | collective-permute-done | bytes 524320 | tf_op jit(solution)/shard_map/ppermute | solution.py:30
  201.5 1.7 add_convert_fusion.1
  207.8 17.9 %collective-permute-done = bf16[16,128,128]{2,1,0:T(8,128)(2,1)S(1)} collective-permute-done((bf16[16,128,128]{2,1,0:T(8,128)(2,1)}, bf16[16,128,128]{2,1,0:T(8,128)(2,1)S(1)}, u32[]{:S(2)}, u32[]{:S(2)}) %collective-permute-start) | collective-permute-done | bytes 524320 | tf_op jit(solution)/shard_map/ppermute | solution.py:30
  227.2 12.1 %collective-permute-start.5 = (bf16[16,128,128]{2,1,0:T(8,128)(2,1)S(1)}, bf16[16,128,128]{2,1,0:T(8,128)(2,1)S(1)}, u32[]{:S(2)}, u32[]{:S(2)}) collective-permute-start(bf16[16,128,128]{2,1,0:T(8,128)(2,1)S(1)} %add_convert_fusion.3), channel_id=1, source_target_pairs={{0,96},{8,104},{16,112},{24,120},{32,128},{40,136},{48,144},{56,15... | collective-permute-start | bytes 1572872 | tf_op jit(solution)/shard_map/ppermute | solution.py:30
  239.3 8.6 %collective-permute-start.4 = (bf16[16,128,128]{2,1,0:T(8,128)(2,1)S(1)}, bf16[16,128,128]{2,1,0:T(8,128)(2,1)S(1)}, u32[]{:S(2)}, u32[]{:S(2)}) collective-permute-start(bf16[16,128,128]{2,1,0:T(8,128)(2,1)S(1)} %add_convert_fusion.3), channel_id=1, source_target_pairs={{0,64},{8,72},{16,80},{24,88},{32,96},{40,104},{48,112},{56,120},{... | collective-permute-start | bytes 1572872 | tf_op jit(solution)/shard_map/ppermute | solution.py:30
  247.9 14.6 %collective-permute-done.12 = bf16[16,128,128]{2,1,0:T(8,128)(2,1)S(1)} collective-permute-done((bf16[16,128,128]{2,1,0:T(8,128)(2,1)S(1)}, bf16[16,128,128]{2,1,0:T(8,128)(2,1)S(1)}, u32[]{:S(2)}, u32[]{:S(2)}) %collective-permute-start.12) | collective-permute-done | bytes 524320 | tf_op jit(solution)/shard_map/ppermute | solution.py:30
  262.6 11.9 %collective-permute-start.3 = (bf16[16,128,128]{2,1,0:T(8,128)(2,1)S(1)}, bf16[16,128,128]{2,1,0:T(8,128)(2,1)S(1)}, u32[]{:S(2)}, u32[]{:S(2)}) collective-permute-start(bf16[16,128,128]{2,1,0:T(8,128)(2,1)S(1)} %add_convert_fusion.3), channel_id=1, source_target_pairs={{0,32},{8,40},{16,48},{24,56},{32,64},{40,72},{48,80},{56,88},{64,... | collective-permute-start | bytes 1572872 | tf_op jit(solution)/shard_map/ppermute | solution.py:30
  274.5 1.9 add_convert_fusion
  278.4 17.9 %collective-permute-done.3 = bf16[16,128,128]{2,1,0:T(8,128)(2,1)S(1)} collective-permute-done((bf16[16,128,128]{2,1,0:T(8,128)(2,1)S(1)}, bf16[16,128,128]{2,1,0:T(8,128)(2,1)S(1)}, u32[]{:S(2)}, u32[]{:S(2)}) %collective-permute-start.3) | collective-permute-done | bytes 524320 | tf_op jit(solution)/shard_map/ppermute | solution.py:30
  296.2 1.7 add_convert_fusion.2
  298.0 65.0 %collective-permute-start.6 = (bf16[16,128,128]{2,1,0:T(8,128)(2,1)S(1)}, bf16[16,128,128]{2,1,0:T(8,128)(2,1)S(1)}, u32[]{:S(2)}, u32[]{:S(2)}) collective-permute-start(bf16[16,128,128]{2,1,0:T(8,128)(2,1)S(1)} %get-tuple-element.29), channel_id=1, source_target_pairs={{0,128},{8,136},{16,144},{24,152},{32,160},{40,168},{48,176},{56,1... | collective-permute-start | bytes 1572872 | tf_op jit(solution)/shard_map/ppermute | solution.py:30
  365.1 8.9 %collective-permute-done.6 = bf16[16,128,128]{2,1,0:T(8,128)(2,1)S(1)} collective-permute-done((bf16[16,128,128]{2,1,0:T(8,128)(2,1)S(1)}, bf16[16,128,128]{2,1,0:T(8,128)(2,1)S(1)}, u32[]{:S(2)}, u32[]{:S(2)}) %collective-permute-start.6) | collective-permute-done | bytes 524320 | tf_op jit(solution)/shard_map/ppermute | solution.py:30
  376.2 2.4 maximum_reduce_fusion
  378.9 24.5 %gather_fusion = bf16[2048,2048]{1,0:T(8,128)(2,1)} fusion(bf16[4096,2048]{1,0:T(8,128)(2,1)} %bitcast.78, s32[2048]{0:T(1024)S(1)} %fusion.49), kind=kCustom, calls=%fused_computation | custom fusion | bytes 16785408 | tf_op jit(solution)/shard_map/jit(_take)/gather | solution.py:124
  403.4 15.6 %copy_select_fusion = bf16[32,2,32,2048]{3,0,2,1:T(8,128)(2,1)S(1)} fusion(bf16[32,2,32,2048]{3,2,1,0:T(8,128)(2,1)} %bitcast.79, pred[32,2,32]{0,2,1:T(8,128)(4,1)S(1)} %copy.113), kind=kLoop, calls=%fused_computation.4 | loop fusion | flops 4194304 | bytes 16779264 | tf_op jit(solution)/shard_map/jit(_take)/select_n | solution.py:124
  419.1 10.1 %bitcast_convert_fusion = bf16[2,704,2048]{2,1,0:T(8,128)(2,1)S(1)} fusion(bf16[32,2,32,704]{3,2,1,0:T(8,128)(2,1)} %bitcast.77, bf16[32,2,32,2048]{3,0,2,1:T(8,128)(2,1)S(1)} %copy_select_fusion), kind=kOutput, calls=%fused_computation.1 | convolution fusion | flops 5908463616 | bytes 17039360 | tf_op jit(solution)/shard_map/sxcf,sxcd->xfd/dot_general | solution.py:127
  429.1 12.2 %copy.134 = bf16[2,704,2048]{2,0,1:T(2,128)(2,1)S(1)} copy(bf16[2,704,2048]{2,1,0:T(8,128)(2,1)S(1)} %bitcast_convert_fusion) | data formatting | bytes 11534336
  441.4 6.2 %copy.140 = bf16[88,8,2,2048]{3,1,2,0:T(8,128)(2,1)} copy(bf16[88,8,2,2048]{3,2,1,0:T(2,128)(2,1)S(1)} %bitcast.81) | data formatting | bytes 11534336
  452.8 36.7 %reduce-scatter.4.cloned.1.call-done = bf16[88,4096]{1,0:T(8,128)(2,1)} async-done(((bf16[704,4096]{1,0:T(8,128)(2,1)}), bf16[88,4096]{1,0:T(8,128)(2,1)}) %reduce-scatter.4.cloned.1.call-update) | async-done | bytes 720912
  489.4 2.4 reshape.200
  (80 shorter events, 30.1 us)
Async XLA Ops:
  7.2 371.8 %all-gather.2.cloned.1.call-start = ((), (), s32[]{:S(2)}) async-start(), calls=%async_computation.2 | async-start | bytes 17301504 | tf_op jit(solution)/shard_map/all_gather | solution.py:73
  22.6 11.6 %copy-start.2 = (bf16[1,128,2048]{2,1,0:T(8,128)(2,1)S(1)}, bf16[1,128,2048]{2,1,0:T(8,128)(2,1)}, u32[]{:S(2)}) copy-start(bf16[1,128,2048]{2,1,0:T(8,128)(2,1)} %param.7) | copy-start | bytes 1572868
  22.6 12.2 %copy-start.1 = (bf16[1,128,2048]{2,1,0:T(8,128)(2,1)S(1)}, bf16[1,128,2048]{2,1,0:T(8,128)(2,1)}, u32[]{:S(2)}) copy-start(bf16[1,128,2048]{2,1,0:T(8,128)(2,1)} %param.10) | copy-start | bytes 1572868
  22.6 353.6 %all-to-all-start = ((bf16[32,2,32,768]{3,2,1,0:T(8,128)(2,1)}), bf16[32,2,32,768]{3,2,1,0:T(8,128)(2,1)}, u32[]{:S(2)}, u32[]{:S(2)}) async-start(bf16[32,2,32,768]{3,2,1,0:T(8,128)(2,1)} %bitcast.10), calls=%async_computation | async-start | bytes 6291456 | tf_op jit(solution)/shard_map/all_to_all | solution.py:72
  34.1 7.8 %copy-start.3 = (bf16[1,128,2048]{2,1,0:T(8,128)(2,1)S(1)}, bf16[1,128,2048]{2,1,0:T(8,128)(2,1)}, u32[]{:S(2)}) copy-start(bf16[1,128,2048]{2,1,0:T(8,128)(2,1)} %param.8) | copy-start | bytes 1572868
  34.2 455.3 %reduce-scatter.4.cloned.1.call-start = ((), (), s32[]{:S(2)}) async-start(), calls=%async_computation.3 | async-start | bytes 6488064
  34.5 7.6 %copy-start.4 = (bf16[1,128,2048]{2,1,0:T(8,128)(2,1)S(1)}, bf16[1,128,2048]{2,1,0:T(8,128)(2,1)}, u32[]{:S(2)}) copy-start(bf16[1,128,2048]{2,1,0:T(8,128)(2,1)} %param.9) | copy-start | bytes 1572868
  37.2 133.6 %collective-permute-start.9 = (bf16[16,128,128]{2,1,0:T(8,128)(2,1)}, bf16[16,128,128]{2,1,0:T(8,128)(2,1)}, u32[]{:S(2)}, u32[]{:S(2)}) collective-permute-start(bf16[16,128,128]{2,1,0:T(8,128)(2,1)} %get-tuple-element.33), channel_id=1, source_target_pairs={{24,0},{32,8},{40,16},{48,24},{56,32},{64,40},{72,48},{80,56},{88,... | collective-permute-start | bytes 1572872 | tf_op jit(solution)/shard_map/ppermute | solution.py:30
  38.5 163.0 %collective-permute-start.8 = (bf16[16,128,128]{2,1,0:T(8,128)(2,1)}, bf16[16,128,128]{2,1,0:T(8,128)(2,1)}, u32[]{:S(2)}, u32[]{:S(2)}) collective-permute-start(bf16[16,128,128]{2,1,0:T(8,128)(2,1)} %get-tuple-element.33), channel_id=1, source_target_pairs={{16,0},{24,8},{32,16},{40,24},{48,32},{56,40},{64,48},{72,56},{80,... | collective-permute-start | bytes 1572872 | tf_op jit(solution)/shard_map/ppermute | solution.py:30
  39.8 161.7 %collective-permute-start.7 = (bf16[16,128,128]{2,1,0:T(8,128)(2,1)}, bf16[16,128,128]{2,1,0:T(8,128)(2,1)}, u32[]{:S(2)}, u32[]{:S(2)}) collective-permute-start(bf16[16,128,128]{2,1,0:T(8,128)(2,1)} %get-tuple-element.33), channel_id=1, source_target_pairs={{8,0},{16,8},{24,16},{32,24},{40,32},{48,40},{56,48},{64,56},{72,6... | collective-permute-start | bytes 1572872 | tf_op jit(solution)/shard_map/ppermute | solution.py:30
  43.4 162.4 %collective-permute-start.2 = (bf16[16,128,128]{2,1,0:T(8,128)(2,1)}, bf16[16,128,128]{2,1,0:T(8,128)(2,1)}, u32[]{:S(2)}, u32[]{:S(2)}) collective-permute-start(bf16[16,128,128]{2,1,0:T(8,128)(2,1)} %get-tuple-element.31), channel_id=1, source_target_pairs={{0,24},{8,32},{16,40},{24,48},{32,56},{40,64},{48,72},{56,80},{64,... | collective-permute-start | bytes 1572872 | tf_op jit(solution)/shard_map/ppermute | solution.py:30
  52.4 155.4 %collective-permute-start.1 = (bf16[16,128,128]{2,1,0:T(8,128)(2,1)}, bf16[16,128,128]{2,1,0:T(8,128)(2,1)}, u32[]{:S(2)}, u32[]{:S(2)}) collective-permute-start(bf16[16,128,128]{2,1,0:T(8,128)(2,1)} %get-tuple-element.31), channel_id=1, source_target_pairs={{0,16},{8,24},{16,32},{24,40},{32,48},{40,56},{48,64},{56,72},{64,... | collective-permute-start | bytes 1572872 | tf_op jit(solution)/shard_map/ppermute | solution.py:30
  57.9 143.6 %copy-start = (f32[16,128,128]{2,1,0:T(8,128)S(1)}, f32[16,128,128]{2,1,0:T(8,128)}, u32[]{:S(2)}) copy-start(f32[16,128,128]{2,1,0:T(8,128)} %get-tuple-element.34) | copy-start | bytes 3145732
  170.8 54.9 %collective-permute-start = (bf16[16,128,128]{2,1,0:T(8,128)(2,1)}, bf16[16,128,128]{2,1,0:T(8,128)(2,1)S(1)}, u32[]{:S(2)}, u32[]{:S(2)}) collective-permute-start(bf16[16,128,128]{2,1,0:T(8,128)(2,1)} %get-tuple-element.31), channel_id=1, source_target_pairs={{0,8},{8,16},{16,24},{24,32},{32,40},{40,48},{48,56},{56,64},{64,7... | collective-permute-start | bytes 1572872 | tf_op jit(solution)/shard_map/ppermute | solution.py:30
  203.2 59.4 %collective-permute-start.12 = (bf16[16,128,128]{2,1,0:T(8,128)(2,1)S(1)}, bf16[16,128,128]{2,1,0:T(8,128)(2,1)S(1)}, u32[]{:S(2)}, u32[]{:S(2)}) collective-permute-start(bf16[16,128,128]{2,1,0:T(8,128)(2,1)S(1)} %add_convert_fusion.1), channel_id=1, source_target_pairs={{96,0},{104,8},{112,16},{120,24},{128,32},{136,40},{144,48},{152,5... | collective-permute-start | bytes 1572872 | tf_op jit(solution)/shard_map/ppermute | solution.py:30
  204.5 70.0 %collective-permute-start.11 = (bf16[16,128,128]{2,1,0:T(8,128)(2,1)S(1)}, bf16[16,128,128]{2,1,0:T(8,128)(2,1)S(1)}, u32[]{:S(2)}, u32[]{:S(2)}) collective-permute-start(bf16[16,128,128]{2,1,0:T(8,128)(2,1)S(1)} %add_convert_fusion.1), channel_id=1, source_target_pairs={{64,0},{72,8},{80,16},{88,24},{96,32},{104,40},{112,48},{120,56},{... | collective-permute-start | bytes 1572872 | tf_op jit(solution)/shard_map/ppermute | solution.py:30
  205.8 68.7 %collective-permute-start.10 = (bf16[16,128,128]{2,1,0:T(8,128)(2,1)S(1)}, bf16[16,128,128]{2,1,0:T(8,128)(2,1)S(1)}, u32[]{:S(2)}, u32[]{:S(2)}) collective-permute-start(bf16[16,128,128]{2,1,0:T(8,128)(2,1)S(1)} %add_convert_fusion.1), channel_id=1, source_target_pairs={{32,0},{40,8},{48,16},{56,24},{64,32},{72,40},{80,48},{88,56},{96,... | collective-permute-start | bytes 1572872 | tf_op jit(solution)/shard_map/ppermute | solution.py:30
  227.2 51.2 %collective-permute-start.5 = (bf16[16,128,128]{2,1,0:T(8,128)(2,1)S(1)}, bf16[16,128,128]{2,1,0:T(8,128)(2,1)S(1)}, u32[]{:S(2)}, u32[]{:S(2)}) collective-permute-start(bf16[16,128,128]{2,1,0:T(8,128)(2,1)S(1)} %add_convert_fusion.3), channel_id=1, source_target_pairs={{0,96},{8,104},{16,112},{24,120},{32,128},{40,136},{48,144},{56,15... | collective-permute-start | bytes 1572872 | tf_op jit(solution)/shard_map/ppermute | solution.py:30
  239.3 39.1 %collective-permute-start.4 = (bf16[16,128,128]{2,1,0:T(8,128)(2,1)S(1)}, bf16[16,128,128]{2,1,0:T(8,128)(2,1)S(1)}, u32[]{:S(2)}, u32[]{:S(2)}) collective-permute-start(bf16[16,128,128]{2,1,0:T(8,128)(2,1)S(1)} %add_convert_fusion.3), channel_id=1, source_target_pairs={{0,64},{8,72},{16,80},{24,88},{32,96},{40,104},{48,112},{56,120},{... | collective-permute-start | bytes 1572872 | tf_op jit(solution)/shard_map/ppermute | solution.py:30
  262.6 33.7 %collective-permute-start.3 = (bf16[16,128,128]{2,1,0:T(8,128)(2,1)S(1)}, bf16[16,128,128]{2,1,0:T(8,128)(2,1)S(1)}, u32[]{:S(2)}, u32[]{:S(2)}) collective-permute-start(bf16[16,128,128]{2,1,0:T(8,128)(2,1)S(1)} %add_convert_fusion.3), channel_id=1, source_target_pairs={{0,32},{8,40},{16,48},{24,56},{32,64},{40,72},{48,80},{56,88},{64,... | collective-permute-start | bytes 1572872 | tf_op jit(solution)/shard_map/ppermute | solution.py:30
  276.4 86.7 %collective-permute-start.13 = (bf16[16,128,128]{2,1,0:T(8,128)(2,1)S(1)}, bf16[16,128,128]{2,1,0:T(8,128)(2,1)S(1)}, u32[]{:S(2)}, u32[]{:S(2)}) collective-permute-start(bf16[16,128,128]{2,1,0:T(8,128)(2,1)S(1)} %get-tuple-element.27), channel_id=1, source_target_pairs={{128,0},{136,8},{144,16},{152,24},{160,32},{168,40},{176,48},{184,... | collective-permute-start | bytes 1572872 | tf_op jit(solution)/shard_map/ppermute | solution.py:30
  298.0 76.0 %collective-permute-start.6 = (bf16[16,128,128]{2,1,0:T(8,128)(2,1)S(1)}, bf16[16,128,128]{2,1,0:T(8,128)(2,1)S(1)}, u32[]{:S(2)}, u32[]{:S(2)}) collective-permute-start(bf16[16,128,128]{2,1,0:T(8,128)(2,1)S(1)} %get-tuple-element.29), channel_id=1, source_target_pairs={{0,128},{8,136},{16,144},{24,152},{32,160},{40,168},{48,176},{56,1... | collective-permute-start | bytes 1572872 | tf_op jit(solution)/shard_map/ppermute | solution.py:30
Sparse Core Ops, SparseCore 0:
  10.6 300.2 all-gather.1
  447.7 41.7 reduce-scatter.3

commit v4 on v2

--- a/solution.py
+++ b/solution.py
@@ -10,23 +10,6 @@
 
 
 PRECISE = lax.Precision.HIGHEST
-
-
-def exclusive_scan(local_sum, axis, backward):
-    count = lax.axis_size(axis)
-    window = local_sum
-    total = jnp.zeros_like(local_sum)
-    shift = 1
-    while shift < count:
-        if backward:
-            pairs = [(src, src - shift) for src in range(shift, count)]
-        else:
-            pairs = [(src, src + shift) for src in range(count - shift)]
-        arrived = lax.ppermute(window.astype(jnp.bfloat16), axis, pairs)
-        total = total + arrived.astype(jnp.float32)
-        window = local_sum + total
-        shift *= 2
-    return total
 
 
 def per_device(query, key_in, value, cotangent, routes, gates, hidden):
@@ -69,12 +52,7 @@
     all_cotangent = lax.all_gather(cotangent, "seq", axis=1, tiled=True)[0]
     arrived_hidden = arrived[..., :hidden_units]
     slot_token = jnp.maximum(arrived[..., hidden_units].astype(jnp.int32) - 1, 0)
-    wanted = (
-        jnp.arange(seq_count, dtype=jnp.int32)[:, None, None] * tokens + slot_token
-    ).reshape(-1)
-    arrived_cot = jnp.take(all_cotangent, wanted, axis=0).reshape(
-        seq_count, EXP_DEV, CAP, width
-    )
+    wanted = jnp.arange(seq_count, dtype=jnp.int32)[:, None, None] * tokens + slot_token
 
     query_raw = query[0].reshape(tokens, HEADS, head_dim)
     key_raw = key_in[0].reshape(tokens, HEADS, head_dim)
@@ -90,8 +68,45 @@
     causal = jnp.tril(jnp.ones((tokens, tokens), jnp.float32))
     state_sum = jnp.einsum("thd,the->hde", key_raw, value_raw, preferred_element_type=jnp.float32)
     grad_sum = jnp.einsum("thd,the->hde", query_full * row_scale, grad_out, precision=PRECISE)
-    prefix_state = exclusive_scan(state_sum, "seq", False)
-    after_state = exclusive_scan(grad_sum, "seq", True)
+    state_sum, grad_sum, all_cotangent = lax.optimization_barrier(
+        (state_sum, grad_sum, all_cotangent)
+    )
+    chunks = 4
+    chunk = seq_count // chunks
+    group_term = jnp.zeros((EXP_DEV, hidden_units, width), jnp.float32)
+    prefix_state = jnp.zeros_like(state_sum)
+    after_state = jnp.zeros_like(grad_sum)
+    fwd_window = state_sum
+    bwd_window = grad_sum
+    shift = 1
+    done_chunks = 0
+    while shift < seq_count or done_chunks < chunks:
+        fwd_sent = fwd_window.astype(jnp.bfloat16)
+        bwd_sent = bwd_window.astype(jnp.bfloat16)
+        if done_chunks < chunks:
+            low = done_chunks * chunk
+            part_hidden, part_wanted, fwd_sent, bwd_sent = lax.optimization_barrier(
+                (arrived_hidden[low:low + chunk], wanted[low:low + chunk], fwd_sent, bwd_sent)
+            )
+        if shift < seq_count:
+            fwd_pairs = [(src, src + shift) for src in range(seq_count - shift)]
+            bwd_pairs = [(src, src - shift) for src in range(shift, seq_count)]
+            fwd_arrived = lax.ppermute(fwd_sent, "seq", fwd_pairs)
+            bwd_arrived = lax.ppermute(bwd_sent, "seq", bwd_pairs)
+        if done_chunks < chunks:
+            rows = jnp.take(all_cotangent, part_wanted.reshape(-1), axis=0).reshape(
+                chunk, EXP_DEV, CAP, width
+            )
+            group_term = group_term + jnp.einsum(
+                "sxcf,sxcd->xfd", part_hidden, rows, preferred_element_type=jnp.float32
+            )
+            done_chunks += 1
+        if shift < seq_count:
+            prefix_state = prefix_state + fwd_arrived.astype(jnp.float32)
+            after_state = after_state + bwd_arrived.astype(jnp.float32)
+            fwd_window = state_sum + prefix_state
+            bwd_window = grad_sum + after_state
+            shift *= 2
     scores = (
         jnp.einsum("thd,uhd->htu", query_raw, key_raw, preferred_element_type=jnp.float32) * causal
     )
@@ -117,9 +132,6 @@
     def to_shard(array):
         return array.reshape(1, tokens, width).astype(jnp.bfloat16)
 
-    group_term = jnp.einsum(
-        "sxcf,sxcd->xfd", arrived_hidden, arrived_cot, preferred_element_type=jnp.float32
-    )
     rounded = lax.optimization_barrier(group_term.astype(jnp.bfloat16)).astype(jnp.float32)
     expert_grad = lax.psum_scatter(
         rounded.astype(jnp.bfloat16), "grp", scatter_dimension=1, tiled=True

time: 434 us -> 442 us (1.018)
  the two profiles are of different devices: /device:TPU:88 before, /device:TPU:32 now
where the time goes in v4:
time: 442 us; the launch traced here: 435 us
  waiting for transfers between devices  190 us (43%)
  local copies, waits for them, and re-layouts  93.7 us (21%)
  matrix products  61.9 us (14%)
  starting transfers between devices  46.6 us (11%)
  other arithmetic  27.9 us (6%)
  between operations  14.8 us (3%)
    all_to_all x1, waiting for transfers between devices, per_device(): lax.all_to_all(hidden_slots, 'seq', split_axis=0, concat_axis=0, tiled=True)  87.2 us
    all_gather x1, waiting for transfers between devices, per_device(): all_cotangent = lax.all_gather(cotangent, 'seq', axis=1, tiled=True)[0]  66.9 us
    gather x4, local copies, waits for them, and re-layouts, per_device(): jnp.take(all_cotangent, part_wanted.reshape(-1), axis=0)  52.9 us
    dot_general x4, matrix products, per_device(): jnp.einsum('sxcf,sxcd->xfd', part_hidden, rows, preferred_element_type=jn...  34.2 us
    unnamed x66, local copies, waits for them, and re-layouts  29.1 us
    ppermute x5, starting transfers between devices, per_device(): fwd_arrived = lax.ppermute(fwd_sent, 'seq', fwd_pairs)  26.2 us
    ppermute x5, waiting for transfers between devices, per_device(): bwd_arrived = lax.ppermute(bwd_sent, 'seq', bwd_pairs)  23.4 us
    ppermute x5, waiting for transfers between devices, per_device(): fwd_arrived = lax.ppermute(fwd_sent, 'seq', fwd_pairs)  11.6 us
  transfers between devices with their start and end apart: 13, of which 6 were waited for; matrix products, arithmetic and copies ran while one was open for 28% of the time, Pallas kernels for 0%

profile of v4, /device:TPU:32, one launch (start us, length us, event | category | flops | bytes accessed | tf_op | source)
XLA Modules:
  0.0 434.8 jit_solution(10859678834231267265)
XLA Ops:
  14.4 2.7 reshape.210
  17.6 4.8 %fusion.2 = bf16[2048,768]{1,0:T(8,128)(2,1)} fusion(s32[768]{0:T(1024)S(1)} %multiply_add_fusion, bf16[768,1]{1,0:T(8,128)(2,1)S(1)} %fusion.32, bf16[768,704]{1,0:T(8,128)(2,1)S(1)} %multiply_convert_fusion, bf16[768]{0:T(1024)(128)(2,1)S(1)} %pad.2.clone), kind=kOutput, calls=%fused_computation.10 | convolution fusion | flops 2422603776 | bytes 4233216 | tf_op jit(solution)/shard_map/dot_general | solution.py:47
  22.4 11.5 %all-to-all-start = ((bf16[32,2,32,768]{3,2,1,0:T(8,128)(2,1)}), bf16[32,2,32,768]{3,2,1,0:T(8,128)(2,1)}, u32[]{:S(2)}, u32[]{:S(2)}) async-start(bf16[32,2,32,768]{3,2,1,0:T(8,128)(2,1)} %bitcast.134), calls=%async_computation | async-start | bytes 6291456 | tf_op jit(solution)/shard_map/all_to_all | solution.py:51
  38.1 87.2 %all-to-all-done = bf16[32,2,32,768]{3,2,1,0:T(8,128)(2,1)} async-done(((bf16[32,2,32,768]{3,2,1,0:T(8,128)(2,1)}), bf16[32,2,32,768]{3,2,1,0:T(8,128)(2,1)}, u32[]{:S(2)}, u32[]{:S(2)}) %all-to-all-start) | async-done | bytes 3145760 | tf_op jit(solution)/shard_map/all_to_all | solution.py:51
  127.1 3.6 fusion.47
  130.7 66.9 %all-gather.2.cloned.1.call-done = bf16[1,4096,2048]{2,1,0:T(8,128)(2,1)} async-done(((bf16[1,128,2048]{2,1,0:T(8,128)(2,1)}), bf16[1,4096,2048]{2,1,0:T(8,128)(2,1)}) %all-gather.2.cloned.1.call-update) | async-done | bytes 16777232 | tf_op jit(solution)/shard_map/all_gather | solution.py:52
  199.5 3.5 collective-permute-start
  203.0 2.7 collective-permute-start.1
  205.7 13.1 %gather_fusion = bf16[512,2048]{1,0:T(8,128)(2,1)} fusion(bf16[4096,2048]{1,0:T(8,128)(2,1)} %bitcast.113, s32[1024]{0:T(1024)S(1)} %pad_clamp_fusion.3), kind=kCustom, calls=%fused_computation.clone | custom fusion | bytes 4196352 | tf_op jit(solution)/shard_map/jit(_take)/gather | solution.py:97
  220.8 6.0 %fusion.49 = f32[2,704,2048,1]{2,1,0,3:T(8,128)} fusion(bf16[8,2,32,704]{3,2,1,0:T(8,128)(2,1)S(1)} %copy-done.20, bf16[8,2,32,2048]{3,2,1,0:T(8,128)(2,1)S(1)} %bitcast.141), kind=kOutput, calls=%fused_computation.114 | convolution fusion | flops 1476395008 | bytes 14352384 | tf_op jit(solution)/shard_map/sxcf,sxcd->xfd/dot_general | solution.py:100
  228.8 6.2 %collective-permute-start.2 = (bf16[16,128,128]{2,1,0:T(8,128)(2,1)}, bf16[16,128,128]{2,1,0:T(8,128)(2,1)}, u32[]{:S(2)}, u32[]{:S(2)}) collective-permute-start(bf16[16,128,128]{2,1,0:T(8,128)(2,1)} %fusion.18), channel_id=1, source_target_pairs={{0,16},{8,24},{16,32},{24,40},{32,48},{40,56},{48,64},{56,72},{64,... | collective-permute-start | bytes 1572872 | tf_op jit(solution)/shard_map/ppermute | solution.py:94
  236.8 13.2 %gather_fusion.1 = bf16[512,2048]{1,0:T(8,128)(2,1)} fusion(bf16[4096,2048]{1,0:T(8,128)(2,1)} %bitcast.114, s32[1024]{0:T(1024)S(1)} %pad_clamp_fusion.2), kind=kCustom, calls=%fused_computation.1.clone | custom fusion | bytes 4196352 | tf_op jit(solution)/shard_map/jit(_take)/gather | solution.py:97
  251.9 5.9 %fusion.50 = f32[2,704,2048,1]{2,1,0,3:T(8,128)} fusion(bf16[8,2,32,704]{3,2,1,0:T(8,128)(2,1)S(1)} %copy-done.19, bf16[8,2,32,2048]{3,2,1,0:T(8,128)(2,1)S(1)} %bitcast.142), kind=kOutput, calls=%fused_computation.115 | convolution fusion | flops 1476395008 | bytes 14352384 | tf_op jit(solution)/shard_map/sxcf,sxcd->xfd/dot_general | solution.py:100
  262.0 7.6 %collective-permute-start.4 = (bf16[16,128,128]{2,1,0:T(8,128)(2,1)}, bf16[16,128,128]{2,1,0:T(8,128)(2,1)}, u32[]{:S(2)}, u32[]{:S(2)}) collective-permute-start(bf16[16,128,128]{2,1,0:T(8,128)(2,1)} %add_convert_fusion.5), channel_id=1, source_target_pairs={{0,32},{8,40},{16,48},{24,56},{32,64},{40,72},{48,80},{56,88},{64,... | collective-permute-start | bytes 1572872 | tf_op jit(solution)/shard_map/ppermute | solution.py:94
  271.0 13.4 %gather_fusion.2 = bf16[512,2048]{1,0:T(8,128)(2,1)} fusion(bf16[4096,2048]{1,0:T(8,128)(2,1)} %bitcast.115, s32[1024]{0:T(1024)S(1)} %pad_clamp_fusion.1), kind=kCustom, calls=%fused_computation.2.clone | custom fusion | bytes 4196352 | tf_op jit(solution)/shard_map/jit(_take)/gather | solution.py:97
  286.3 6.0 %fusion.51 = f32[2,704,2048,1]{2,1,0,3:T(8,128)} fusion(bf16[8,2,32,704]{3,2,1,0:T(8,128)(2,1)S(1)} %copy-done.18, bf16[8,2,32,2048]{3,2,1,0:T(8,128)(2,1)S(1)} %bitcast.143), kind=kOutput, calls=%fused_computation.116 | convolution fusion | flops 1476395008 | bytes 14352384 | tf_op jit(solution)/shard_map/sxcf,sxcd->xfd/dot_general | solution.py:100
  294.5 21.9 %collective-permute-done.5 = bf16[16,128,128]{2,1,0:T(8,128)(2,1)} collective-permute-done((bf16[16,128,128]{2,1,0:T(8,128)(2,1)}, bf16[16,128,128]{2,1,0:T(8,128)(2,1)}, u32[]{:S(2)}, u32[]{:S(2)}) %collective-permute-start.5) | collective-permute-done | bytes 524320 | tf_op jit(solution)/shard_map/ppermute | solution.py:95
  318.9 13.2 %gather_fusion.3 = bf16[512,2048]{1,0:T(8,128)(2,1)} fusion(bf16[4096,2048]{1,0:T(8,128)(2,1)} %bitcast.116, s32[1024]{0:T(1024)S(1)} %pad_clamp_fusion), kind=kCustom, calls=%fused_computation.3.clone | custom fusion | bytes 4196352 | tf_op jit(solution)/shard_map/jit(_take)/gather | solution.py:97
  332.0 3.1 broadcast_select_fusion
  335.2 16.4 %fusion = bf16[2,704,2048]{2,1,0:T(8,128)(2,1)} fusion(f32[2,704,2048,1]{2,1,0,3:T(8,128)} %fusion.51, f32[2,704,2048,1]{2,1,0,3:T(8,128)} %fusion.50, f32[2,704,2048,1]{2,1,0,3:T(8,128)} %fusion.49, bf16[8,2,32,704]{3,2,1,0:T(8,128)(2,1)} %get-tuple-element.42, bf16[8,2,32,2048]{3,2,1,0:T(8,128)(2,1)} %bitcast.140), kind=kOutput, calls=%fused_computation.5 | convolution fusion | flops 1487929344 | bytes 43188224 | tf_op jit(solution)/shard_map/sxcf,sxcd->xfd/dot_general | solution.py:100
  351.5 10.4 %copy.128 = bf16[2,704,2048]{2,0,1:T(2,128)(2,1)S(1)} copy(bf16[2,704,2048]{2,1,0:T(8,128)(2,1)} %fusion) | data formatting | bytes 11534336
  362.0 6.2 %copy.135 = bf16[88,8,2,2048]{3,1,2,0:T(8,128)(2,1)} copy(bf16[88,8,2,2048]{3,2,1,0:T(2,128)(2,1)S(1)} %bitcast.118) | data formatting | bytes 11534336
  373.0 3.3 collective-permute-start.6
  380.1 7.6 %collective-permute-done.6 = bf16[16,128,128]{2,1,0:T(8,128)(2,1)S(1)} collective-permute-done((bf16[16,128,128]{2,1,0:T(8,128)(2,1)S(1)}, bf16[16,128,128]{2,1,0:T(8,128)(2,1)S(1)}, u32[]{:S(2)}, u32[]{:S(2)}) %collective-permute-start.6) | collective-permute-done | bytes 524320 | tf_op jit(solution)/shard_map/ppermute | solution.py:94
  389.5 5.5 %collective-permute-start.7 = (bf16[16,128,128]{2,1,0:T(8,128)(2,1)S(1)}, bf16[16,128,128]{2,1,0:T(8,128)(2,1)S(1)}, u32[]{:S(2)}, u32[]{:S(2)}) collective-permute-start(bf16[16,128,128]{2,1,0:T(8,128)(2,1)S(1)} %add_convert_fusion.1), channel_id=1, source_target_pairs={{0,128},{8,136},{16,144},{24,152},{32,160},{40,168},{48,176},{56,1... | collective-permute-start | bytes 1572872 | tf_op jit(solution)/shard_map/ppermute | solution.py:94
  397.3 2.6 add_convert_fusion
  401.6 4.0 collective-permute-done.7
  405.6 2.6 fusion.12
  409.2 3.7 fusion.13
  416.5 2.9 fusion.10
  420.4 2.8 fusion.11
  424.2 2.4 reshape.260
  (141 shorter events, 56.9 us)
Async XLA Ops:
  7.2 4.9 %copy-start.17 = (bf16[1,128,6,704]{1,3,2,0:T(8,128)(2,1)S(1)}, bf16[1,128,6,704]{1,3,2,0:T(8,128)(2,1)}, u32[]{:S(2)}) copy-start(bf16[1,128,6,704]{1,3,2,0:T(8,128)(2,1)} %param.15) | copy-start | bytes 3244036
  7.2 190.5 %all-gather.2.cloned.1.call-start = ((), (), s32[]{:S(2)}) async-start(), calls=%async_computation.2 | async-start | bytes 17301504 | tf_op jit(solution)/shard_map/all_gather | solution.py:52
  22.4 11.6 %copy-start.16 = (bf16[1,128,2048]{2,1,0:T(8,128)(2,1)S(1)}, bf16[1,128,2048]{2,1,0:T(8,128)(2,1)}, u32[]{:S(2)}) copy-start(bf16[1,128,2048]{2,1,0:T(8,128)(2,1)} %param.12) | copy-start | bytes 1572868
  22.4 11.9 %copy-start.21 = (bf16[1,128,2048]{2,1,0:T(8,128)(2,1)S(1)}, bf16[1,128,2048]{2,1,0:T(8,128)(2,1)}, u32[]{:S(2)}) copy-start(bf16[1,128,2048]{2,1,0:T(8,128)(2,1)} %param.9) | copy-start | bytes 1572868
  22.4 102.9 %all-to-all-start = ((bf16[32,2,32,768]{3,2,1,0:T(8,128)(2,1)}), bf16[32,2,32,768]{3,2,1,0:T(8,128)(2,1)}, u32[]{:S(2)}, u32[]{:S(2)}) async-start(bf16[32,2,32,768]{3,2,1,0:T(8,128)(2,1)} %bitcast.134), calls=%async_computation | async-start | bytes 6291456 | tf_op jit(solution)/shard_map/all_to_all | solution.py:51
  34.0 390.2 %reduce-scatter.4.cloned.1.call-start = ((), (), s32[]{:S(2)}) async-start(), calls=%async_computation.3 | async-start | bytes 6488064
  34.3 2.6 copy-start.3
  34.6 2.3 copy-start.6
  199.5 27.3 %collective-permute-start = (bf16[16,128,128]{2,1,0:T(8,128)(2,1)}, bf16[16,128,128]{2,1,0:T(8,128)(2,1)S(1)}, u32[]{:S(2)}, u32[]{:S(2)}) collective-permute-start(bf16[16,128,128]{2,1,0:T(8,128)(2,1)} %convert_element_type.182), channel_id=1, source_target_pairs={{0,8},{8,16},{16,24},{24,32},{32,40},{40,48},{48,56},{56,64},{64,7... | collective-permute-start | bytes 1572872 | tf_op jit(solution)/shard_map/ppermute | solution.py:94
  203.0 24.7 %collective-permute-start.1 = (bf16[16,128,128]{2,1,0:T(8,128)(2,1)}, bf16[16,128,128]{2,1,0:T(8,128)(2,1)S(1)}, u32[]{:S(2)}, u32[]{:S(2)}) collective-permute-start(bf16[16,128,128]{2,1,0:T(8,128)(2,1)} %convert_element_type.183), channel_id=1, source_target_pairs={{8,0},{16,8},{24,16},{32,24},{40,32},{48,40},{56,48},{64,56},{72,6... | collective-permute-start | bytes 1572872 | tf_op jit(solution)/shard_map/ppermute | solution.py:95
  218.9 1.9 copy-start.20
  228.8 29.0 %collective-permute-start.2 = (bf16[16,128,128]{2,1,0:T(8,128)(2,1)}, bf16[16,128,128]{2,1,0:T(8,128)(2,1)}, u32[]{:S(2)}, u32[]{:S(2)}) collective-permute-start(bf16[16,128,128]{2,1,0:T(8,128)(2,1)} %fusion.18), channel_id=1, source_target_pairs={{0,16},{8,24},{16,32},{24,40},{32,48},{40,56},{48,64},{56,72},{64,... | collective-permute-start | bytes 1572872 | tf_op jit(solution)/shard_map/ppermute | solution.py:94
  235.0 24.9 %collective-permute-start.3 = (bf16[16,128,128]{2,1,0:T(8,128)(2,1)}, bf16[16,128,128]{2,1,0:T(8,128)(2,1)}, u32[]{:S(2)}, u32[]{:S(2)}) collective-permute-start(bf16[16,128,128]{2,1,0:T(8,128)(2,1)} %fusion.19), channel_id=1, source_target_pairs={{16,0},{24,8},{32,16},{40,24},{48,32},{56,40},{64,48},{72,56},{80,... | collective-permute-start | bytes 1572872 | tf_op jit(solution)/shard_map/ppermute | solution.py:95
  262.0 30.2 %collective-permute-start.4 = (bf16[16,128,128]{2,1,0:T(8,128)(2,1)}, bf16[16,128,128]{2,1,0:T(8,128)(2,1)}, u32[]{:S(2)}, u32[]{:S(2)}) collective-permute-start(bf16[16,128,128]{2,1,0:T(8,128)(2,1)} %add_convert_fusion.5), channel_id=1, source_target_pairs={{0,32},{8,40},{16,48},{24,56},{32,64},{40,72},{48,80},{56,88},{64,... | collective-permute-start | bytes 1572872 | tf_op jit(solution)/shard_map/ppermute | solution.py:94
  269.7 46.8 %collective-permute-start.5 = (bf16[16,128,128]{2,1,0:T(8,128)(2,1)}, bf16[16,128,128]{2,1,0:T(8,128)(2,1)}, u32[]{:S(2)}, u32[]{:S(2)}) collective-permute-start(bf16[16,128,128]{2,1,0:T(8,128)(2,1)} %add_convert_fusion.4), channel_id=1, source_target_pairs={{32,0},{40,8},{48,16},{56,24},{64,32},{72,40},{80,48},{88,56},{96,... | collective-permute-start | bytes 1572872 | tf_op jit(solution)/shard_map/ppermute | solution.py:95
  284.4 1.9 copy-start.18
  368.2 3.0 copy-start.4
  370.1 3.0 copy-start.25
  371.3 5.6 %copy-start.7 = (bf16[1,128,2048]{1,2,0:T(8,128)(2,1)S(1)}, bf16[1,128,2048]{1,2,0:T(8,128)(2,1)}, u32[]{:S(2)}) copy-start(bf16[1,128,2048]{1,2,0:T(8,128)(2,1)} %copy-done.6) | copy-start | bytes 1572868
  373.0 5.6 %copy-start.24 = (bf16[16,128,128]{2,1,0:T(8,128)(2,1)S(1)}, bf16[16,128,128]{2,1,0:T(8,128)(2,1)}, u32[]{:S(2)}) copy-start(bf16[16,128,128]{2,1,0:T(8,128)(2,1)} %add_convert_fusion.2) | copy-start | bytes 1572868
  373.0 14.7 %collective-permute-start.6 = (bf16[16,128,128]{2,1,0:T(8,128)(2,1)S(1)}, bf16[16,128,128]{2,1,0:T(8,128)(2,1)S(1)}, u32[]{:S(2)}, u32[]{:S(2)}) collective-permute-start(bf16[16,128,128]{2,1,0:T(8,128)(2,1)S(1)} %copy-done.25), channel_id=1, source_target_pairs={{0,64},{8,72},{16,80},{24,88},{32,96},{40,104},{48,112},{56,120},{... | collective-permute-start | bytes 1572872 | tf_op jit(solution)/shard_map/ppermute | solution.py:94
  378.7 16.4 %copy-start.14 = (bf16[128,16,128]{0,2,1:T(8,128)(2,1)S(1)}, bf16[128,16,128]{0,2,1:T(8,128)(2,1)}, u32[]{:S(2)}) copy-start(bf16[128,16,128]{0,2,1:T(8,128)(2,1)} %copy-done.13) | copy-start | bytes 1572868
  378.7 18.7 %collective-permute-start.8 = (bf16[16,128,128]{2,1,0:T(8,128)(2,1)S(1)}, bf16[16,128,128]{2,1,0:T(8,128)(2,1)S(1)}, u32[]{:S(2)}, u32[]{:S(2)}) collective-permute-start(bf16[16,128,128]{2,1,0:T(8,128)(2,1)S(1)} %copy-done.24), channel_id=1, source_target_pairs={{64,0},{72,8},{80,16},{88,24},{96,32},{104,40},{112,48},{120,56},{... | collective-permute-start | bytes 1572872 | tf_op jit(solution)/shard_map/ppermute | solution.py:95
  387.7 17.9 %copy-start.12 = (bf16[16,128,128]{2,1,0:T(8,128)(2,1)}, bf16[16,128,128]{2,1,0:T(8,128)(2,1)S(1)}, u32[]{:S(2)}) copy-start(bf16[16,128,128]{2,1,0:T(8,128)(2,1)S(1)} %collective-permute-done.6) | copy-start | bytes 1572868
  389.5 16.1 %collective-permute-start.7 = (bf16[16,128,128]{2,1,0:T(8,128)(2,1)S(1)}, bf16[16,128,128]{2,1,0:T(8,128)(2,1)S(1)}, u32[]{:S(2)}, u32[]{:S(2)}) collective-permute-start(bf16[16,128,128]{2,1,0:T(8,128)(2,1)S(1)} %add_convert_fusion.1), channel_id=1, source_target_pairs={{0,128},{8,136},{16,144},{24,152},{32,160},{40,168},{48,176},{56,1... | collective-permute-start | bytes 1572872 | tf_op jit(solution)/shard_map/ppermute | solution.py:94
  397.3 2.6 copy-start.10
  399.9 9.3 %copy-start.5 = (bf16[1,128,2048]{1,2,0:T(8,128)(2,1)S(1)}, bf16[1,128,2048]{1,2,0:T(8,128)(2,1)}, u32[]{:S(2)}) copy-start(bf16[1,128,2048]{1,2,0:T(8,128)(2,1)} %copy-done.3) | copy-start | bytes 1572868
  399.9 16.5 %collective-permute-start.9 = (bf16[16,128,128]{2,1,0:T(8,128)(2,1)}, bf16[16,128,128]{2,1,0:T(8,128)(2,1)S(1)}, u32[]{:S(2)}, u32[]{:S(2)}) collective-permute-start(bf16[16,128,128]{2,1,0:T(8,128)(2,1)} %add_convert_fusion), channel_id=1, source_target_pairs={{128,0},{136,8},{144,16},{152,24},{160,32},{168,40},{176,48},{184,... | collective-permute-start | bytes 1572872 | tf_op jit(solution)/shard_map/ppermute | solution.py:95
  405.6 2.6 copy-start.15
  409.2 7.2 %copy-start.2 = (bf16[16,8,16,128]{3,2,1,0:T(8,128)(2,1)S(1)}, bf16[16,8,16,128]{3,2,1,0:T(8,128)(2,1)}, u32[]{:S(2)}) copy-start(bf16[16,8,16,128]{3,2,1,0:T(8,128)(2,1)} %copy-done) | copy-start | bytes 1572868
  409.2 7.2 %copy-start.11 = (bf16[16,128,128]{2,1,0:T(8,128)(2,1)S(1)}, bf16[16,128,128]{2,1,0:T(8,128)(2,1)}, u32[]{:S(2)}) copy-start(bf16[16,128,128]{2,1,0:T(8,128)(2,1)} %copy-done.10) | copy-start | bytes 1572868
  415.0 5.4 %copy-start.9 = (bf16[16,8,16,128]{3,2,1,0:T(8,128)(2,1)S(1)}, bf16[16,8,16,128]{3,2,1,0:T(8,128)(2,1)}, u32[]{:S(2)}) copy-start(bf16[16,8,16,128]{3,2,1,0:T(8,128)(2,1)} %copy-done.8) | copy-start | bytes 1572868
  (7 other events, 9.1 us)
Sparse Core Ops, SparseCore 0:
  10.6 186.9 all-gather.1
  368.3 42.8 reduce-scatter.3

commit v5 on v4

--- a/solution.py
+++ b/solution.py
@@ -68,74 +68,67 @@
     causal = jnp.tril(jnp.ones((tokens, tokens), jnp.float32))
     state_sum = jnp.einsum("thd,the->hde", key_raw, value_raw, preferred_element_type=jnp.float32)
     grad_sum = jnp.einsum("thd,the->hde", query_full * row_scale, grad_out, precision=PRECISE)
-    state_sum, grad_sum, all_cotangent = lax.optimization_barrier(
-        (state_sum, grad_sum, all_cotangent)
+    scores = (
+        jnp.einsum("thd,uhd->htu", query_raw, key_raw, preferred_element_type=jnp.float32) * causal
     )
-    chunks = 4
-    chunk = seq_count // chunks
-    group_term = jnp.zeros((EXP_DEV, hidden_units, width), jnp.float32)
+    grad_scores = (
+        jnp.einsum("the,uhe->htu", grad_raw, value_raw, preferred_element_type=jnp.float32) * causal
+    )
+    col_scale = scaling[None, :, None]
+    out_local = jnp.einsum("htu,uhe->the", scores, value_full, precision=PRECISE)
+    grad_q_local = jnp.einsum("htu,uhd->thd", grad_scores, key_full, precision=PRECISE)
+    grad_k_local = jnp.einsum("htu,thd->uhd", grad_scores * col_scale, query_full, precision=PRECISE)
+    grad_v_local = jnp.einsum("htu,the->uhe", scores * col_scale, grad_out, precision=PRECISE)
+    (
+        state_sum, grad_sum, out_local, grad_q_local, grad_k_local, grad_v_local, all_cotangent
+    ) = lax.optimization_barrier(
+        (state_sum, grad_sum, out_local, grad_q_local, grad_k_local, grad_v_local, all_cotangent)
+    )
+    group_term = None
     prefix_state = jnp.zeros_like(state_sum)
     after_state = jnp.zeros_like(grad_sum)
     fwd_window = state_sum
     bwd_window = grad_sum
     shift = 1
-    done_chunks = 0
-    while shift < seq_count or done_chunks < chunks:
+    while shift < seq_count:
         fwd_sent = fwd_window.astype(jnp.bfloat16)
         bwd_sent = bwd_window.astype(jnp.bfloat16)
-        if done_chunks < chunks:
-            low = done_chunks * chunk
+        if group_term is None and shift > 1:
             part_hidden, part_wanted, fwd_sent, bwd_sent = lax.optimization_barrier(
-                (arrived_hidden[low:low + chunk], wanted[low:low + chunk], fwd_sent, bwd_sent)
+                (arrived_hidden, wanted, fwd_sent, bwd_sent)
             )
-        if shift < seq_count:
-            fwd_pairs = [(src, src + shift) for src in range(seq_count - shift)]
-            bwd_pairs = [(src, src - shift) for src in range(shift, seq_count)]
-            fwd_arrived = lax.ppermute(fwd_sent, "seq", fwd_pairs)
-            bwd_arrived = lax.ppermute(bwd_sent, "seq", bwd_pairs)
-        if done_chunks < chunks:
+        fwd_pairs = [(src, src + shift) for src in range(seq_count - shift)]
+        bwd_pairs = [(src, src - shift) for src in range(shift, seq_count)]
+        fwd_arrived = lax.ppermute(fwd_sent, "seq", fwd_pairs)
+        bwd_arrived = lax.ppermute(bwd_sent, "seq", bwd_pairs)
+        if group_term is None and shift > 1:
             rows = jnp.take(all_cotangent, part_wanted.reshape(-1), axis=0).reshape(
-                chunk, EXP_DEV, CAP, width
+                seq_count, EXP_DEV, CAP, width
             )
-            group_term = group_term + jnp.einsum(
-                "sxcf,sxcd->xfd", part_hidden, rows, preferred_element_type=jnp.float32
+            group_term = jnp.einsum(
+                "sxcf,sxcd->fxd", part_hidden, rows, preferred_element_type=jnp.float32
             )
-            done_chunks += 1
-        if shift < seq_count:
-            prefix_state = prefix_state + fwd_arrived.astype(jnp.float32)
-            after_state = after_state + bwd_arrived.astype(jnp.float32)
-            fwd_window = state_sum + prefix_state
-            bwd_window = grad_sum + after_state
-            shift *= 2
-    scores = (
-        jnp.einsum("thd,uhd->htu", query_raw, key_raw, preferred_element_type=jnp.float32) * causal
-    )
-    outputs = jnp.einsum("htu,uhe->the", scores, value_full, precision=PRECISE)
+        prefix_state = prefix_state + fwd_arrived.astype(jnp.float32)
+        after_state = after_state + bwd_arrived.astype(jnp.float32)
+        fwd_window = state_sum + prefix_state
+        bwd_window = grad_sum + after_state
+        shift *= 2
     outputs = (
-        outputs + jnp.einsum("thd,hde->the", query_full, prefix_state, precision=PRECISE)
+        out_local + jnp.einsum("thd,hde->the", query_full, prefix_state, precision=PRECISE)
     ) * row_scale
-    grad_scores = (
-        jnp.einsum("the,uhe->htu", grad_raw, value_raw, preferred_element_type=jnp.float32) * causal
-    )
-    grad_q = jnp.einsum("htu,uhd->thd", grad_scores, key_full, precision=PRECISE)
     grad_q = (
-        grad_q + jnp.einsum("the,hde->thd", grad_out, prefix_state, precision=PRECISE)
+        grad_q_local + jnp.einsum("the,hde->thd", grad_out, prefix_state, precision=PRECISE)
     ) * row_scale
-    col_scale = scaling[None, :, None]
-    weighted = scores * col_scale
-    grad_weighted = grad_scores * col_scale
-    grad_k = jnp.einsum("htu,thd->uhd", grad_weighted, query_full, precision=PRECISE)
-    grad_k = grad_k + jnp.einsum("uhe,hde->uhd", value_full, after_state, precision=PRECISE)
-    grad_v = jnp.einsum("htu,the->uhe", weighted, grad_out, precision=PRECISE)
-    grad_v = grad_v + jnp.einsum("uhd,hde->uhe", key_full, after_state, precision=PRECISE)
+    grad_k = grad_k_local + jnp.einsum("uhe,hde->uhd", value_full, after_state, precision=PRECISE)
+    grad_v = grad_v_local + jnp.einsum("uhd,hde->uhe", key_full, after_state, precision=PRECISE)
 
     def to_shard(array):
         return array.reshape(1, tokens, width).astype(jnp.bfloat16)
 
     rounded = lax.optimization_barrier(group_term.astype(jnp.bfloat16)).astype(jnp.float32)
     expert_grad = lax.psum_scatter(
-        rounded.astype(jnp.bfloat16), "grp", scatter_dimension=1, tiled=True
-    )
+        rounded.astype(jnp.bfloat16), "grp", scatter_dimension=0, tiled=True
+    ).transpose(1, 0, 2)
     return (to_shard(outputs), to_shard(grad_q), to_shard(grad_k), to_shard(grad_v), expert_grad)
 
 

time: 442 us -> 434 us (0.982); the launches traced: 435 us -> 432 us
  starting transfers between devices: 46.6 us -> 92.2 us
  local copies, waits for them, and re-layouts: 93.7 us -> 51.3 us
  waiting for transfers between devices: 190 us -> 218 us
  other arithmetic: 27.9 us -> 10.2 us
  matrix products: 61.9 us -> 46.3 us
    all_to_all x1, waiting for transfers between devices: 87.2 us -> 0.01 us  [per_device(): lax.all_to_all(hidden_slots, 'seq', split_axis=0, concat_axis=0, tiled=True)]
    all_gather x1, waiting for transfers between devices: 66.9 us -> 150 us  [per_device(): all_cotangent = lax.all_gather(cotangent, 'seq', axis=1, tiled=True)[0]]
    ppermute x5, starting transfers between devices: 26.2 us -> 71.5 us  [per_device(): fwd_arrived = lax.ppermute(fwd_sent, 'seq', fwd_pairs)]
    ppermute x5, waiting for transfers between devices: 11.6 us -> 52.4 us  [per_device(): fwd_arrived = lax.ppermute(fwd_sent, 'seq', fwd_pairs)]
    gather x4 -> x1, local copies, waits for them, and re-layouts: 52.9 us -> 24.3 us  [per_device(): jnp.take(all_cotangent, part_wanted.reshape(-1), axis=0)]
    dot_general x7 -> x4, matrix products: 38.9 us -> 23.6 us  [the longest x1 17.8 us: per_device(): jnp.einsum('sxcf,sxcd->fxd', part_hidden, rows, preferred_element_type=jn...]
    unnamed x66 -> x63, local copies, waits for them, and re-layouts: 29.1 us -> 16.1 us
    ppermute x5, waiting for transfers between devices: 23.4 us -> 14.1 us  [per_device(): bwd_arrived = lax.ppermute(bwd_sent, 'seq', bwd_pairs)]
  transfers between devices with their start and end apart: 13 -> 13, of which waited for: 6 -> 8; matrix products, arithmetic and copies ran while one was open for 28% -> 13% of each run, Pallas kernels for 0% -> 0%
where the time goes in v5:
time: 434 us; the launch traced here: 432 us
  waiting for transfers between devices  218 us (50%)
  starting transfers between devices  92.2 us (21%)
  local copies, waits for them, and re-layouts  51.3 us (12%)
  matrix products  46.3 us (11%)
  between operations  14.6 us (3%)
  other arithmetic  10.2 us (2%)
    all_gather x1, waiting for transfers between devices, per_device(): all_cotangent = lax.all_gather(cotangent, 'seq', axis=1, tiled=True)[0]  150 us
    ppermute x5, starting transfers between devices, per_device(): fwd_arrived = lax.ppermute(fwd_sent, 'seq', fwd_pairs)  71.5 us
    ppermute x5, waiting for transfers between devices, per_device(): fwd_arrived = lax.ppermute(fwd_sent, 'seq', fwd_pairs)  52.4 us
    gather x1, local copies, waits for them, and re-layouts, per_device(): jnp.take(all_cotangent, part_wanted.reshape(-1), axis=0)  24.3 us
    dot_general x1, matrix products, per_device(): jnp.einsum('sxcf,sxcd->fxd', part_hidden, rows, preferred_element_type=jn...  17.8 us
    unnamed x63, local copies, waits for them, and re-layouts  16.1 us
    ppermute x5, waiting for transfers between devices, per_device(): bwd_arrived = lax.ppermute(bwd_sent, 'seq', bwd_pairs)  14.1 us
    all_to_all x1, starting transfers between devices, per_device(): lax.all_to_all(hidden_slots, 'seq', split_axis=0, concat_axis=0, tiled=True)  11.5 us
  transfers between devices with their start and end apart: 13, of which 8 were waited for; matrix products, arithmetic and copies ran while one was open for 13% of the time, Pallas kernels for 0%

profile of v5, /device:TPU:32, one launch (start us, length us, event | category | flops | bytes accessed | tf_op | source)
XLA Modules:
  0.0 432.1 jit_solution(474564009052593477)
XLA Ops:
  9.0 1.8 reduce-window.6
  11.1 2.0 copy.99
  15.4 1.9 multiply_convert_fusion
  17.2 4.7 %fusion.5 = bf16[2048,768]{1,0:T(8,128)(2,1)} fusion(s32[768]{0:T(1024)S(1)} %multiply_add_fusion, bf16[768,1]{1,0:T(8,128)(2,1)S(1)} %fusion.34, bf16[768,704]{1,0:T(8,128)(2,1)S(1)} %multiply_convert_fusion, bf16[768]{0:T(1024)(128)(2,1)S(1)} %pad.2.clone), kind=kOutput, calls=%fused_computation.9 | convolution fusion | flops 2422603776 | bytes 4233216 | tf_op jit(solution)/shard_map/dot_general | solution.py:47
  22.0 11.5 %all-to-all-start = ((bf16[32,2,32,768]{3,2,1,0:T(8,128)(2,1)}), bf16[32,2,32,768]{3,2,1,0:T(8,128)(2,1)}, u32[]{:S(2)}, u32[]{:S(2)}) async-start(bf16[32,2,32,768]{3,2,1,0:T(8,128)(2,1)} %bitcast.7), calls=%async_computation | async-start | bytes 6291456 | tf_op jit(solution)/shard_map/all_to_all | solution.py:51
  36.5 2.3 fusion.26
  40.9 1.6 convolution_bitcast_fusion.7
  42.5 1.7 convolution_bitcast_fusion.6
  44.2 2.1 convolution_bitcast_fusion.5
  46.3 2.1 convolution_bitcast_fusion.4
  48.3 150.4 %all-gather.2.cloned.1.call-done = bf16[1,4096,2048]{2,1,0:T(8,128)(2,1)} async-done(((bf16[1,128,2048]{2,1,0:T(8,128)(2,1)}), bf16[1,4096,2048]{2,1,0:T(8,128)(2,1)}) %all-gather.2.cloned.1.call-update) | async-done | bytes 16777232 | tf_op jit(solution)/shard_map/all_gather | solution.py:52
  199.7 2.3 collective-permute-start
  202.9 3.7 collective-permute-start.1
  206.6 2.0 slice.20
  210.2 5.0 %collective-permute-done = bf16[16,128,128]{2,1,0:T(8,128)(2,1)S(1)} collective-permute-done((bf16[16,128,128]{2,1,0:T(8,128)(2,1)}, bf16[16,128,128]{2,1,0:T(8,128)(2,1)S(1)}, u32[]{:S(2)}, u32[]{:S(2)}) %collective-permute-start) | collective-permute-done | bytes 524320 | tf_op jit(solution)/shard_map/ppermute | solution.py:102
  216.2 3.1 collective-permute-done.1
  220.5 24.3 %gather_fusion = bf16[2048,2048]{1,0:T(8,128)(2,1)} fusion(bf16[4096,2048]{1,0:T(8,128)(2,1)} %bitcast.99, s32[2048]{0:T(1024)S(1)} %broadcast_clamp_fusion), kind=kCustom, calls=%fused_computation | custom fusion | bytes 16785408 | tf_op jit(solution)/shard_map/jit(_take)/gather | solution.py:105
  244.8 17.8 %fusion.3 = bf16[704,2,2048]{2,0,1:T(8,128)(2,1)} fusion(bf16[32,2,32,2048]{3,2,1,0:T(8,128)(2,1)} %bitcast.117, pred[32,2,32]{0,2,1:T(8,128)(4,1)S(1)} %copy.115, bf16[32,2,32,704]{3,2,1,0:T(8,128)(2,1)} %bitcast.98), kind=kOutput, calls=%fused_computation.7 | convolution fusion | flops 5912657920 | bytes 17041408 | tf_op jit(solution)/shard_map/sxcf,sxcd->fxd/dot_general | solution.py:108
  262.6 6.1 %copy.141 = bf16[2,88,8,2048]{3,2,0,1:T(8,128)(2,1)} copy(bf16[2,88,8,2048]{3,2,1,0:T(8,128)(2,1)} %bitcast.118) | data formatting | bytes 11534336
  268.8 4.8 %collective-permute-start.2 = (bf16[16,128,128]{2,1,0:T(8,128)(2,1)}, bf16[16,128,128]{2,1,0:T(8,128)(2,1)S(1)}, u32[]{:S(2)}, u32[]{:S(2)}) collective-permute-start(bf16[16,128,128]{2,1,0:T(8,128)(2,1)} %fusion.22), channel_id=1, source_target_pairs={{0,16},{8,24},{16,32},{24,40},{32,48},{40,56},{48,64},{56,72},{64,... | collective-permute-start | bytes 1572872 | tf_op jit(solution)/shard_map/ppermute | solution.py:102
  274.9 20.2 %collective-permute-done.2 = bf16[16,128,128]{2,1,0:T(8,128)(2,1)S(1)} collective-permute-done((bf16[16,128,128]{2,1,0:T(8,128)(2,1)}, bf16[16,128,128]{2,1,0:T(8,128)(2,1)S(1)}, u32[]{:S(2)}, u32[]{:S(2)}) %collective-permute-start.2) | collective-permute-done | bytes 524320 | tf_op jit(solution)/shard_map/ppermute | solution.py:102
  295.3 6.4 %collective-permute-start.3 = (bf16[16,128,128]{2,1,0:T(8,128)(2,1)S(1)}, bf16[16,128,128]{2,1,0:T(8,128)(2,1)S(1)}, u32[]{:S(2)}, u32[]{:S(2)}) collective-permute-start(bf16[16,128,128]{2,1,0:T(8,128)(2,1)S(1)} %add_convert_fusion.5), channel_id=1, source_target_pairs={{0,32},{8,40},{16,48},{24,56},{32,64},{40,72},{48,80},{56,88},{64,... | collective-permute-start | bytes 1572872 | tf_op jit(solution)/shard_map/ppermute | solution.py:102
  303.3 19.3 %collective-permute-done.3 = bf16[16,128,128]{2,1,0:T(8,128)(2,1)S(1)} collective-permute-done((bf16[16,128,128]{2,1,0:T(8,128)(2,1)S(1)}, bf16[16,128,128]{2,1,0:T(8,128)(2,1)S(1)}, u32[]{:S(2)}, u32[]{:S(2)}) %collective-permute-start.3) | collective-permute-done | bytes 524320 | tf_op jit(solution)/shard_map/ppermute | solution.py:102
  322.9 21.8 %collective-permute-start.4 = (bf16[16,128,128]{2,1,0:T(8,128)(2,1)S(1)}, bf16[16,128,128]{2,1,0:T(8,128)(2,1)S(1)}, u32[]{:S(2)}, u32[]{:S(2)}) collective-permute-start(bf16[16,128,128]{2,1,0:T(8,128)(2,1)S(1)} %add_convert_fusion.4), channel_id=1, source_target_pairs={{0,64},{8,72},{16,80},{24,88},{32,96},{40,104},{48,112},{56,120},{... | collective-permute-start | bytes 1572872 | tf_op jit(solution)/shard_map/ppermute | solution.py:102
  344.7 6.6 %collective-permute-done.7 = bf16[16,128,128]{2,1,0:T(8,128)(2,1)S(1)} collective-permute-done((bf16[16,128,128]{2,1,0:T(8,128)(2,1)S(1)}, bf16[16,128,128]{2,1,0:T(8,128)(2,1)S(1)}, u32[]{:S(2)}, u32[]{:S(2)}) %collective-permute-start.7) | collective-permute-done | bytes 524320 | tf_op jit(solution)/shard_map/ppermute | solution.py:103
  353.5 36.1 %collective-permute-start.5 = (bf16[16,128,128]{2,1,0:T(8,128)(2,1)S(1)}, bf16[16,128,128]{2,1,0:T(8,128)(2,1)S(1)}, u32[]{:S(2)}, u32[]{:S(2)}) collective-permute-start(bf16[16,128,128]{2,1,0:T(8,128)(2,1)S(1)} %add_convert_fusion.3), channel_id=1, source_target_pairs={{0,128},{8,136},{16,144},{24,152},{32,160},{40,168},{48,176},{56,1... | collective-permute-start | bytes 1572872 | tf_op jit(solution)/shard_map/ppermute | solution.py:102
  392.2 7.8 %collective-permute-done.5 = bf16[16,128,128]{2,1,0:T(8,128)(2,1)S(1)} collective-permute-done((bf16[16,128,128]{2,1,0:T(8,128)(2,1)S(1)}, bf16[16,128,128]{2,1,0:T(8,128)(2,1)S(1)}, u32[]{:S(2)}, u32[]{:S(2)}) %collective-permute-start.5) | collective-permute-done | bytes 524320 | tf_op jit(solution)/shard_map/ppermute | solution.py:102
  402.6 4.2 fusion.17
  409.1 4.3 %collective-permute-done.9 = bf16[16,128,128]{2,1,0:T(8,128)(2,1)} collective-permute-done((bf16[16,128,128]{2,1,0:T(8,128)(2,1)}, bf16[16,128,128]{2,1,0:T(8,128)(2,1)}, u32[]{:S(2)}, u32[]{:S(2)}) %collective-permute-start.9) | collective-permute-done | bytes 524320 | tf_op jit(solution)/shard_map/ppermute | solution.py:103
  413.4 3.8 fusion.14
  419.6 2.4 fusion.15
  423.3 2.0 copy.177
  (115 shorter events, 31.0 us)
Async XLA Ops:
  7.2 191.6 %all-gather.2.cloned.1.call-start = ((), (), s32[]{:S(2)}) async-start(), calls=%async_computation.2 | async-start | bytes 17301504 | tf_op jit(solution)/shard_map/all_gather | solution.py:52
  22.0 11.6 %copy-start.21 = (bf16[1,128,2048]{2,1,0:T(8,128)(2,1)S(1)}, bf16[1,128,2048]{2,1,0:T(8,128)(2,1)}, u32[]{:S(2)}) copy-start(bf16[1,128,2048]{2,1,0:T(8,128)(2,1)} %param.8) | copy-start | bytes 1572868
  22.0 11.8 %copy-start.22 = (bf16[1,128,2048]{2,1,0:T(8,128)(2,1)S(1)}, bf16[1,128,2048]{2,1,0:T(8,128)(2,1)}, u32[]{:S(2)}) copy-start(bf16[1,128,2048]{2,1,0:T(8,128)(2,1)} %param.9) | copy-start | bytes 1572868
  22.0 11.9 %copy-start.23 = (bf16[1,128,2048]{2,1,0:T(8,128)(2,1)S(1)}, bf16[1,128,2048]{2,1,0:T(8,128)(2,1)}, u32[]{:S(2)}) copy-start(bf16[1,128,2048]{2,1,0:T(8,128)(2,1)} %param.7) | copy-start | bytes 1572868
  22.0 184.7 %all-to-all-start = ((bf16[32,2,32,768]{3,2,1,0:T(8,128)(2,1)}), bf16[32,2,32,768]{3,2,1,0:T(8,128)(2,1)}, u32[]{:S(2)}, u32[]{:S(2)}) async-start(bf16[32,2,32,768]{3,2,1,0:T(8,128)(2,1)} %bitcast.7), calls=%async_computation | async-start | bytes 6291456 | tf_op jit(solution)/shard_map/all_to_all | solution.py:51
  33.5 389.7 %reduce-scatter.4.cloned.1.call-start = ((), (), s32[]{:S(2)}) async-start(), calls=%async_computation.3 | async-start | bytes 6488064
  33.7 8.8 %copy-start.3 = (bf16[16,8,16,128]{3,2,1,0:T(8,128)(2,1)}, bf16[16,8,16,128]{3,2,1,0:T(8,128)(2,1)S(1)}, u32[]{:S(2)}) copy-start(bf16[16,8,16,128]{3,2,1,0:T(8,128)(2,1)S(1)} %copy.142) | copy-start | bytes 1572868
  33.9 7.0 %copy-start.5 = (bf16[16,8,16,128]{3,2,1,0:T(8,128)(2,1)}, bf16[16,8,16,128]{3,2,1,0:T(8,128)(2,1)S(1)}, u32[]{:S(2)}) copy-start(bf16[16,8,16,128]{3,2,1,0:T(8,128)(2,1)S(1)} %copy.143) | copy-start | bytes 1572868
  36.1 4.3 copy-start.7
  199.7 15.6 %collective-permute-start = (bf16[16,128,128]{2,1,0:T(8,128)(2,1)}, bf16[16,128,128]{2,1,0:T(8,128)(2,1)S(1)}, u32[]{:S(2)}, u32[]{:S(2)}) collective-permute-start(bf16[16,128,128]{2,1,0:T(8,128)(2,1)} %convert_element_type.177), channel_id=1, source_target_pairs={{0,8},{8,16},{16,24},{24,32},{32,40},{40,48},{48,56},{56,64},{64,7... | collective-permute-start | bytes 1572872 | tf_op jit(solution)/shard_map/ppermute | solution.py:102
  202.9 16.4 %collective-permute-start.1 = (bf16[16,128,128]{2,1,0:T(8,128)(2,1)}, bf16[16,128,128]{2,1,0:T(8,128)(2,1)S(1)}, u32[]{:S(2)}, u32[]{:S(2)}) collective-permute-start(bf16[16,128,128]{2,1,0:T(8,128)(2,1)} %convert_element_type.188), channel_id=1, source_target_pairs={{8,0},{16,8},{24,16},{32,24},{40,32},{48,40},{56,48},{64,56},{72,6... | collective-permute-start | bytes 1572872 | tf_op jit(solution)/shard_map/ppermute | solution.py:103
  268.8 26.4 %collective-permute-start.2 = (bf16[16,128,128]{2,1,0:T(8,128)(2,1)}, bf16[16,128,128]{2,1,0:T(8,128)(2,1)S(1)}, u32[]{:S(2)}, u32[]{:S(2)}) collective-permute-start(bf16[16,128,128]{2,1,0:T(8,128)(2,1)} %fusion.22), channel_id=1, source_target_pairs={{0,16},{8,24},{16,32},{24,40},{32,48},{40,56},{48,64},{56,72},{64,... | collective-permute-start | bytes 1572872 | tf_op jit(solution)/shard_map/ppermute | solution.py:102
  273.6 28.2 %collective-permute-start.6 = (bf16[16,128,128]{2,1,0:T(8,128)(2,1)}, bf16[16,128,128]{2,1,0:T(8,128)(2,1)S(1)}, u32[]{:S(2)}, u32[]{:S(2)}) collective-permute-start(bf16[16,128,128]{2,1,0:T(8,128)(2,1)} %fusion.23), channel_id=1, source_target_pairs={{16,0},{24,8},{32,16},{40,24},{48,32},{56,40},{64,48},{72,56},{80,... | collective-permute-start | bytes 1572872 | tf_op jit(solution)/shard_map/ppermute | solution.py:103
  295.1 104.9 %copy-start.2 = (bf16[16,128,128]{2,1,0:T(8,128)(2,1)}, bf16[16,128,128]{2,1,0:T(8,128)(2,1)S(1)}, u32[]{:S(2)}) copy-start(bf16[16,128,128]{2,1,0:T(8,128)(2,1)S(1)} %collective-permute-done.2) | copy-start | bytes 1572868
  295.3 27.2 %collective-permute-start.3 = (bf16[16,128,128]{2,1,0:T(8,128)(2,1)S(1)}, bf16[16,128,128]{2,1,0:T(8,128)(2,1)S(1)}, u32[]{:S(2)}, u32[]{:S(2)}) collective-permute-start(bf16[16,128,128]{2,1,0:T(8,128)(2,1)S(1)} %add_convert_fusion.5), channel_id=1, source_target_pairs={{0,32},{8,40},{16,48},{24,56},{32,64},{40,72},{48,80},{56,88},{64,... | collective-permute-start | bytes 1572872 | tf_op jit(solution)/shard_map/ppermute | solution.py:102
  301.8 87.8 %copy-start = (bf16[16,128,128]{2,1,0:T(8,128)(2,1)}, bf16[16,128,128]{2,1,0:T(8,128)(2,1)S(1)}, u32[]{:S(2)}) copy-start(bf16[16,128,128]{2,1,0:T(8,128)(2,1)S(1)} %collective-permute-done.6) | copy-start | bytes 1572868
  302.0 49.3 %collective-permute-start.7 = (bf16[16,128,128]{2,1,0:T(8,128)(2,1)S(1)}, bf16[16,128,128]{2,1,0:T(8,128)(2,1)S(1)}, u32[]{:S(2)}, u32[]{:S(2)}) collective-permute-start(bf16[16,128,128]{2,1,0:T(8,128)(2,1)S(1)} %add_convert_fusion.2), channel_id=1, source_target_pairs={{32,0},{40,8},{48,16},{56,24},{64,32},{72,40},{80,48},{88,56},{96,... | collective-permute-start | bytes 1572872 | tf_op jit(solution)/shard_map/ppermute | solution.py:103
  322.6 77.5 %copy-start.14 = (bf16[16,128,128]{2,1,0:T(8,128)(2,1)}, bf16[16,128,128]{2,1,0:T(8,128)(2,1)S(1)}, u32[]{:S(2)}) copy-start(bf16[16,128,128]{2,1,0:T(8,128)(2,1)S(1)} %collective-permute-done.3) | copy-start | bytes 1572868
  322.9 30.2 %collective-permute-start.4 = (bf16[16,128,128]{2,1,0:T(8,128)(2,1)S(1)}, bf16[16,128,128]{2,1,0:T(8,128)(2,1)S(1)}, u32[]{:S(2)}, u32[]{:S(2)}) collective-permute-start(bf16[16,128,128]{2,1,0:T(8,128)(2,1)S(1)} %add_convert_fusion.4), channel_id=1, source_target_pairs={{0,64},{8,72},{16,80},{24,88},{32,96},{40,104},{48,112},{56,120},{... | collective-permute-start | bytes 1572872 | tf_op jit(solution)/shard_map/ppermute | solution.py:102
  351.3 38.3 %copy-start.12 = (bf16[16,128,128]{2,1,0:T(8,128)(2,1)}, bf16[16,128,128]{2,1,0:T(8,128)(2,1)S(1)}, u32[]{:S(2)}) copy-start(bf16[16,128,128]{2,1,0:T(8,128)(2,1)S(1)} %collective-permute-done.7) | copy-start | bytes 1572868
  351.6 48.4 %copy-start.11 = (bf16[1,128,2048]{1,2,0:T(8,128)(2,1)S(1)}, bf16[1,128,2048]{1,2,0:T(8,128)(2,1)}, u32[]{:S(2)}) copy-start(bf16[1,128,2048]{1,2,0:T(8,128)(2,1)} %copy-done.9) | copy-start | bytes 1572868
  351.6 48.4 %copy-start.18 = (f32[128,16,128]{2,0,1:T(8,128)S(1)}, f32[128,16,128]{2,0,1:T(8,128)}, u32[]{:S(2)}) copy-start(f32[128,16,128]{2,0,1:T(8,128)} %convolution_bitcast_fusion.7) | copy-start | bytes 3145732
  351.6 37.9 %collective-permute-start.8 = (bf16[16,128,128]{2,1,0:T(8,128)(2,1)S(1)}, bf16[16,128,128]{2,1,0:T(8,128)(2,1)S(1)}, u32[]{:S(2)}, u32[]{:S(2)}) collective-permute-start(bf16[16,128,128]{2,1,0:T(8,128)(2,1)S(1)} %add_convert_fusion.1), channel_id=1, source_target_pairs={{64,0},{72,8},{80,16},{88,24},{96,32},{104,40},{112,48},{120,56},{... | collective-permute-start | bytes 1572872 | tf_op jit(solution)/shard_map/ppermute | solution.py:103
  353.1 47.0 %copy-start.17 = (bf16[16,128,128]{2,1,0:T(8,128)(2,1)}, bf16[16,128,128]{2,1,0:T(8,128)(2,1)S(1)}, u32[]{:S(2)}) copy-start(bf16[16,128,128]{2,1,0:T(8,128)(2,1)S(1)} %collective-permute-done.4) | copy-start | bytes 1572868
  353.5 46.6 %collective-permute-start.5 = (bf16[16,128,128]{2,1,0:T(8,128)(2,1)S(1)}, bf16[16,128,128]{2,1,0:T(8,128)(2,1)S(1)}, u32[]{:S(2)}, u32[]{:S(2)}) collective-permute-start(bf16[16,128,128]{2,1,0:T(8,128)(2,1)S(1)} %add_convert_fusion.3), channel_id=1, source_target_pairs={{0,128},{8,136},{16,144},{24,152},{32,160},{40,168},{48,176},{56,1... | collective-permute-start | bytes 1572872 | tf_op jit(solution)/shard_map/ppermute | solution.py:102
  390.8 11.7 %copy-start.8 = (bf16[16,8,16,128]{3,2,1,0:T(8,128)(2,1)S(1)}, bf16[16,8,16,128]{3,2,1,0:T(8,128)(2,1)}, u32[]{:S(2)}) copy-start(bf16[16,8,16,128]{3,2,1,0:T(8,128)(2,1)} %copy.144) | copy-start | bytes 1572868
  390.8 22.6 %collective-permute-start.9 = (bf16[16,128,128]{2,1,0:T(8,128)(2,1)}, bf16[16,128,128]{2,1,0:T(8,128)(2,1)}, u32[]{:S(2)}, u32[]{:S(2)}) collective-permute-start(bf16[16,128,128]{2,1,0:T(8,128)(2,1)} %add_convert_fusion), channel_id=1, source_target_pairs={{128,0},{136,8},{144,16},{152,24},{160,32},{168,40},{176,48},{184,... | collective-permute-start | bytes 1572872 | tf_op jit(solution)/shard_map/ppermute | solution.py:103
  402.5 10.9 %copy-start.1 = (bf16[16,128,128]{2,1,0:T(8,128)(2,1)S(1)}, bf16[16,128,128]{2,1,0:T(8,128)(2,1)}, u32[]{:S(2)}) copy-start(bf16[16,128,128]{2,1,0:T(8,128)(2,1)} %copy-done) | copy-start | bytes 1572868
  402.5 10.9 %copy-start.6 = (bf16[16,8,16,128]{3,2,1,0:T(8,128)(2,1)S(1)}, bf16[16,8,16,128]{3,2,1,0:T(8,128)(2,1)}, u32[]{:S(2)}) copy-start(bf16[16,8,16,128]{3,2,1,0:T(8,128)(2,1)} %copy-done.5) | copy-start | bytes 1572868
  402.5 10.9 %copy-start.13 = (bf16[16,128,128]{2,1,0:T(8,128)(2,1)S(1)}, bf16[16,128,128]{2,1,0:T(8,128)(2,1)}, u32[]{:S(2)}) copy-start(bf16[16,128,128]{2,1,0:T(8,128)(2,1)} %copy-done.12) | copy-start | bytes 1572868
  409.1 10.5 %copy-start.4 = (bf16[16,8,16,128]{3,2,1,0:T(8,128)(2,1)S(1)}, bf16[16,8,16,128]{3,2,1,0:T(8,128)(2,1)}, u32[]{:S(2)}) copy-start(bf16[16,8,16,128]{3,2,1,0:T(8,128)(2,1)} %copy-done.3) | copy-start | bytes 1572868
  409.1 10.5 %copy-start.16 = (bf16[16,128,128]{2,1,0:T(8,128)(2,1)S(1)}, bf16[16,128,128]{2,1,0:T(8,128)(2,1)}, u32[]{:S(2)}) copy-start(bf16[16,128,128]{2,1,0:T(8,128)(2,1)} %copy-done.15) | copy-start | bytes 1572868
  (6 other events, 11.6 us)
Sparse Core Ops, SparseCore 0:
  10.6 188.1 all-gather.1
  268.9 43.3 reduce-scatter.3

commit v6 on v5

--- a/solution.py
+++ b/solution.py
@@ -49,7 +49,6 @@
     ).astype(jnp.bfloat16)
     hidden_slots = hidden_slots.reshape(seq_count, EXP_DEV, CAP, lanes)
     arrived = lax.all_to_all(hidden_slots, "seq", split_axis=0, concat_axis=0, tiled=True)
-    all_cotangent = lax.all_gather(cotangent, "seq", axis=1, tiled=True)[0]
     arrived_hidden = arrived[..., :hidden_units]
     slot_token = jnp.maximum(arrived[..., hidden_units].astype(jnp.int32) - 1, 0)
     wanted = jnp.arange(seq_count, dtype=jnp.int32)[:, None, None] * tokens + slot_token
@@ -79,40 +78,40 @@
     grad_q_local = jnp.einsum("htu,uhd->thd", grad_scores, key_full, precision=PRECISE)
     grad_k_local = jnp.einsum("htu,thd->uhd", grad_scores * col_scale, query_full, precision=PRECISE)
     grad_v_local = jnp.einsum("htu,the->uhe", scores * col_scale, grad_out, precision=PRECISE)
-    (
-        state_sum, grad_sum, out_local, grad_q_local, grad_k_local, grad_v_local, all_cotangent
-    ) = lax.optimization_barrier(
-        (state_sum, grad_sum, out_local, grad_q_local, grad_k_local, grad_v_local, all_cotangent)
-    )
-    group_term = None
     prefix_state = jnp.zeros_like(state_sum)
     after_state = jnp.zeros_like(grad_sum)
     fwd_window = state_sum
     bwd_window = grad_sum
     shift = 1
     while shift < seq_count:
-        fwd_sent = fwd_window.astype(jnp.bfloat16)
-        bwd_sent = bwd_window.astype(jnp.bfloat16)
-        if group_term is None and shift > 1:
-            part_hidden, part_wanted, fwd_sent, bwd_sent = lax.optimization_barrier(
-                (arrived_hidden, wanted, fwd_sent, bwd_sent)
-            )
         fwd_pairs = [(src, src + shift) for src in range(seq_count - shift)]
         bwd_pairs = [(src, src - shift) for src in range(shift, seq_count)]
-        fwd_arrived = lax.ppermute(fwd_sent, "seq", fwd_pairs)
-        bwd_arrived = lax.ppermute(bwd_sent, "seq", bwd_pairs)
-        if group_term is None and shift > 1:
-            rows = jnp.take(all_cotangent, part_wanted.reshape(-1), axis=0).reshape(
-                seq_count, EXP_DEV, CAP, width
-            )
-            group_term = jnp.einsum(
-                "sxcf,sxcd->fxd", part_hidden, rows, preferred_element_type=jnp.float32
-            )
+        fwd_arrived = lax.ppermute(fwd_window.astype(jnp.bfloat16), "seq", fwd_pairs)
+        bwd_arrived = lax.ppermute(bwd_window.astype(jnp.bfloat16), "seq", bwd_pairs)
         prefix_state = prefix_state + fwd_arrived.astype(jnp.float32)
         after_state = after_state + bwd_arrived.astype(jnp.float32)
         fwd_window = state_sum + prefix_state
         bwd_window = grad_sum + after_state
         shift *= 2
+    late_cotangent, prefix_state, after_state = lax.optimization_barrier(
+        (cotangent, prefix_state, after_state)
+    )
+    halves = 2
+    cols = width // halves
+    scattered = []
+    for half in range(halves):
+        gathered = lax.all_gather(
+            late_cotangent[:, :, half * cols:(half + 1) * cols], "seq", axis=1, tiled=True
+        )[0]
+        rows = jnp.take(gathered, wanted.reshape(-1), axis=0).reshape(
+            seq_count, EXP_DEV, CAP, cols
+        )
+        group_term = jnp.einsum(
+            "sxcf,sxcd->fxd", arrived_hidden, rows, preferred_element_type=jnp.float32
+        )
+        rounded = lax.optimization_barrier(group_term.astype(jnp.bfloat16))
+        scattered.append(lax.psum_scatter(rounded, "grp", scatter_dimension=0, tiled=True))
+    expert_grad = jnp.concatenate(scattered, axis=2).transpose(1, 0, 2)
     outputs = (
         out_local + jnp.einsum("thd,hde->the", query_full, prefix_state, precision=PRECISE)
     ) * row_scale
@@ -125,10 +124,6 @@
     def to_shard(array):
         return array.reshape(1, tokens, width).astype(jnp.bfloat16)
 
-    rounded = lax.optimization_barrier(group_term.astype(jnp.bfloat16)).astype(jnp.float32)
-    expert_grad = lax.psum_scatter(
-        rounded.astype(jnp.bfloat16), "grp", scatter_dimension=0, tiled=True
-    ).transpose(1, 0, 2)
     return (to_shard(outputs), to_shard(grad_q), to_shard(grad_k), to_shard(grad_v), expert_grad)
 
 

time: 434 us -> 507 us (1.17)
  waiting for transfers between devices: 218 us -> 310 us
  starting transfers between devices: 92.2 us -> 71.7 us
  matrix products: 46.3 us -> 35.7 us
  local copies, waits for them, and re-layouts: 51.3 us -> 57.7 us
  other arithmetic: 10.2 us -> 16.4 us
    all_to_all x1, waiting for transfers between devices: 0.01 us -> 94.3 us  [per_device(): lax.all_to_all(hidden_slots, 'seq', split_axis=0, concat_axis=0, tiled=True)]
    all_gather x1 -> x2, waiting for transfers between devices: 150 us -> 99.1 us  [per_device(): lax.all_gather(late_cotangent[:, :, half * cols:(half + 1) * cols], 'seq'...]
    unnamed x3 -> x6, waiting for transfers between devices: 0.7 us -> 42.6 us
    ppermute x10, starting transfers between devices: 80.6 us -> 50.4 us  [the longest x5 43.1 us: per_device(): lax.ppermute(fwd_window.astype(jnp.bfloat16), 'seq', fwd_pairs)]
    all_to_all x1, starting transfers between devices: 11.5 us -> 20.8 us  [per_device(): lax.all_to_all(hidden_slots, 'seq', split_axis=0, concat_axis=0, tiled=True)]
    ppermute x10, waiting for transfers between devices: 66.4 us -> 74.1 us  [the longest x5 46.6 us: per_device(): lax.ppermute(fwd_window.astype(jnp.bfloat16), 'seq', fwd_pairs)]
    gather x1 -> x2, local copies, waits for them, and re-layouts: 24.3 us -> 30.9 us  [per_device(): jnp.take(gathered, wanted.reshape(-1), axis=0)]
    dot_general x1 -> x2, matrix products: 17.8 us -> 11.7 us  [per_device(): jnp.einsum('sxcf,sxcd->fxd', arrived_hidden, rows, preferred_element_type...]
  transfers between devices with their start and end apart: 13 -> 15, of which waited for: 8 -> 14; matrix products, arithmetic and copies ran while one was open for 13% -> 15% of each run, Pallas kernels for 0% -> 0%
where the time goes in v6:
time: 507 us; the launch traced here: 506 us
  waiting for transfers between devices  310 us (61%)
  starting transfers between devices  71.7 us (14%)
  local copies, waits for them, and re-layouts  57.7 us (11%)
  matrix products  35.7 us (7%)
  other arithmetic  16.4 us (3%)
  between operations  14.2 us (3%)
    all_gather x2, waiting for transfers between devices, per_device(): lax.all_gather(late_cotangent[:, :, half * cols:(half + 1) * cols], 'seq'...  99.1 us
    all_to_all x1, waiting for transfers between devices, per_device(): lax.all_to_all(hidden_slots, 'seq', split_axis=0, concat_axis=0, tiled=True)  94.3 us
    ppermute x5, waiting for transfers between devices, per_device(): lax.ppermute(fwd_window.astype(jnp.bfloat16), 'seq', fwd_pairs)  46.6 us
    ppermute x5, starting transfers between devices, per_device(): lax.ppermute(fwd_window.astype(jnp.bfloat16), 'seq', fwd_pairs)  43.1 us
    unnamed x6, waiting for transfers between devices  42.6 us
    gather x2, local copies, waits for them, and re-layouts, per_device(): jnp.take(gathered, wanted.reshape(-1), axis=0)  30.9 us
    ppermute x5, waiting for transfers between devices, per_device(): lax.ppermute(bwd_window.astype(jnp.bfloat16), 'seq', bwd_pairs)  27.5 us
    all_to_all x1, starting transfers between devices, per_device(): lax.all_to_all(hidden_slots, 'seq', split_axis=0, concat_axis=0, tiled=True)  20.8 us
  transfers between devices with their start and end apart: 15, of which 14 were waited for; matrix products, arithmetic and copies ran while one was open for 15% of the time, Pallas kernels for 0%

profile of v6, /device:TPU:32, one launch (start us, length us, event | category | flops | bytes accessed | tf_op | source)
XLA Modules:
  0.0 505.9 jit_solution(6941453071797649256)
XLA Ops:
  11.4 3.8 collective-permute-start
  20.1 7.0 %collective-permute-done = bf16[16,128,128]{2,1,0:T(8,128)(2,1)S(1)} collective-permute-done((bf16[16,128,128]{2,1,0:T(8,128)(2,1)}, bf16[16,128,128]{2,1,0:T(8,128)(2,1)S(1)}, u32[]{:S(2)}, u32[]{:S(2)}) %collective-permute-start) | collective-permute-done | bytes 524320 | tf_op jit(solution)/shard_map/ppermute | solution.py:89
  27.3 6.0 %collective-permute-start.1 = (bf16[16,128,128]{2,1,0:T(8,128)(2,1)S(1)}, bf16[16,128,128]{2,1,0:T(8,128)(2,1)S(1)}, u32[]{:S(2)}, u32[]{:S(2)}) collective-permute-start(bf16[16,128,128]{2,1,0:T(8,128)(2,1)S(1)} %fusion.27), channel_id=1, source_target_pairs={{0,16},{8,24},{16,32},{24,40},{32,48},{40,56},{48,64},{56,72},{64,... | collective-permute-start | bytes 1572872 | tf_op jit(solution)/shard_map/ppermute | solution.py:89
  34.9 12.0 %collective-permute-done.1 = bf16[16,128,128]{2,1,0:T(8,128)(2,1)S(1)} collective-permute-done((bf16[16,128,128]{2,1,0:T(8,128)(2,1)S(1)}, bf16[16,128,128]{2,1,0:T(8,128)(2,1)S(1)}, u32[]{:S(2)}, u32[]{:S(2)}) %collective-permute-start.1) | collective-permute-done | bytes 524320 | tf_op jit(solution)/shard_map/ppermute | solution.py:89
  47.2 7.7 %collective-permute-start.2 = (bf16[16,128,128]{2,1,0:T(8,128)(2,1)S(1)}, bf16[16,128,128]{2,1,0:T(8,128)(2,1)S(1)}, u32[]{:S(2)}, u32[]{:S(2)}) collective-permute-start(bf16[16,128,128]{2,1,0:T(8,128)(2,1)S(1)} %add_convert_fusion.5), channel_id=1, source_target_pairs={{0,32},{8,40},{16,48},{24,56},{32,64},{40,72},{48,80},{56,88},{64,... | collective-permute-start | bytes 1572872 | tf_op jit(solution)/shard_map/ppermute | solution.py:89
  56.4 25.9 %collective-permute-done.2 = bf16[16,128,128]{2,1,0:T(8,128)(2,1)S(1)} collective-permute-done((bf16[16,128,128]{2,1,0:T(8,128)(2,1)S(1)}, bf16[16,128,128]{2,1,0:T(8,128)(2,1)S(1)}, u32[]{:S(2)}, u32[]{:S(2)}) %collective-permute-start.2) | collective-permute-done | bytes 524320 | tf_op jit(solution)/shard_map/ppermute | solution.py:89
  82.5 20.8 %collective-permute-start.3 = (bf16[16,128,128]{2,1,0:T(8,128)(2,1)S(1)}, bf16[16,128,128]{2,1,0:T(8,128)(2,1)S(1)}, u32[]{:S(2)}, u32[]{:S(2)}) collective-permute-start(bf16[16,128,128]{2,1,0:T(8,128)(2,1)S(1)} %add_convert_fusion.4), channel_id=1, source_target_pairs={{0,64},{8,72},{16,80},{24,88},{32,96},{40,104},{48,112},{56,120},{... | collective-permute-start | bytes 1572872 | tf_op jit(solution)/shard_map/ppermute | solution.py:89
  103.4 6.8 %collective-permute-done.7 = bf16[16,128,128]{2,1,0:T(8,128)(2,1)S(1)} collective-permute-done((bf16[16,128,128]{2,1,0:T(8,128)(2,1)S(1)}, bf16[16,128,128]{2,1,0:T(8,128)(2,1)S(1)}, u32[]{:S(2)}, u32[]{:S(2)}) %collective-permute-start.7) | collective-permute-done | bytes 524320 | tf_op jit(solution)/shard_map/ppermute | solution.py:90
  113.7 4.8 collective-permute-start.4
  118.4 8.8 %collective-permute-done.8 = bf16[16,128,128]{2,1,0:T(8,128)(2,1)S(1)} collective-permute-done((bf16[16,128,128]{2,1,0:T(8,128)(2,1)S(1)}, bf16[16,128,128]{2,1,0:T(8,128)(2,1)S(1)}, u32[]{:S(2)}, u32[]{:S(2)}) %collective-permute-start.8) | collective-permute-done | bytes 524320 | tf_op jit(solution)/shard_map/ppermute | solution.py:90
  130.6 11.7 %collective-permute-done.9 = bf16[16,128,128]{2,1,0:T(8,128)(2,1)S(1)} collective-permute-done((bf16[16,128,128]{2,1,0:T(8,128)(2,1)S(1)}, bf16[16,128,128]{2,1,0:T(8,128)(2,1)S(1)}, u32[]{:S(2)}, u32[]{:S(2)}) %collective-permute-start.9) | collective-permute-done | bytes 524320 | tf_op jit(solution)/shard_map/ppermute | solution.py:90
  146.9 3.2 copy.87
  150.1 3.9 reshape.190
  156.4 4.7 fusion.1
  161.1 20.8 %all-to-all-start = ((bf16[32,2,32,768]{3,2,1,0:T(8,128)(2,1)}), bf16[32,2,32,768]{3,2,1,0:T(8,128)(2,1)}, u32[]{:S(2)}, u32[]{:S(2)}) async-start(bf16[32,2,32,768]{3,2,1,0:T(8,128)(2,1)} %bitcast.139), calls=%async_computation | async-start | bytes 6291456 | tf_op jit(solution)/shard_map/all_to_all | solution.py:51
  182.4 94.3 %all-to-all-done = bf16[32,2,32,768]{3,2,1,0:T(8,128)(2,1)} async-done(((bf16[32,2,32,768]{3,2,1,0:T(8,128)(2,1)}), bf16[32,2,32,768]{3,2,1,0:T(8,128)(2,1)}, u32[]{:S(2)}, u32[]{:S(2)}) %all-to-all-start) | async-done | bytes 3145760 | tf_op jit(solution)/shard_map/all_to_all | solution.py:51
  276.7 2.4 maximum_reduce_fusion
  279.2 14.9 %all-gather.3.cloned.1.call-done = bf16[1,4096,1024]{2,1,0:T(8,128)(2,1)} async-done(((bf16[1,128,1024]{2,1,0:T(8,128)(2,1)}), bf16[1,4096,1024]{2,1,0:T(8,128)(2,1)}) %all-gather.3.cloned.1.call-update) | async-done | bytes 8388624 | tf_op jit(solution)/shard_map/all_gather | solution.py:103
  294.1 15.4 %gather_fusion = bf16[2048,1024]{1,0:T(8,128)(2,1)} fusion(bf16[4096,1024]{1,0:T(8,128)(2,1)} %bitcast.118, s32[2048]{0:T(1024)S(1)} %broadcast_clamp_fusion), kind=kCustom, calls=%fused_computation.clone | custom fusion | bytes 8396800 | tf_op jit(solution)/shard_map/jit(_take)/gather | solution.py:106
  309.5 84.2 %all-gather.5.cloned.1.call-done = bf16[1,4096,1024]{2,1,0:T(8,128)(2,1)} async-done(((bf16[1,128,1024]{2,1,0:T(8,128)(2,1)}), bf16[1,4096,1024]{2,1,0:T(8,128)(2,1)}) %all-gather.5.cloned.1.call-update) | async-done | bytes 8388624 | tf_op jit(solution)/shard_map/all_gather | solution.py:103
  393.7 15.5 %gather_fusion.1 = bf16[2048,1024]{1,0:T(8,128)(2,1)} fusion(bf16[4096,1024]{1,0:T(8,128)(2,1)} %bitcast.119, s32[2048]{0:T(1024)S(1)} %broadcast_clamp_fusion), kind=kCustom, calls=%fused_computation.1.clone | custom fusion | bytes 8396800 | tf_op jit(solution)/shard_map/jit(_take)/gather | solution.py:106
  409.2 5.2 %broadcast_select_fusion.1 = (bf16[2048,1024]{1,0:T(8,128)(2,1)}, bf16[2048,1024]{1,0:T(8,128)(2,1)S(1)}) fusion(bf16[2048,1024]{1,0:T(8,128)(2,1)} %gather_fusion, pred[2048]{0:T(1024)(128)(4,1)S(1)} %compare_and_fusion, bf16[2048,1024]{1,0:T(8,128)(2,1)} %gather_fusion.1), kind=kLoop, calls=%fused_computation.7 | loop fusion | flops 4194304 | bytes 16779264 | tf_op jit(solution)/shard_map/jit(_take)/select_n | solution.py:106
  414.4 5.3 %fusion.4 = bf16[704,2,1024]{2,0,1:T(8,128)(2,1)S(1)} fusion(bf16[32,2,32,1024]{3,2,1,0:T(8,128)(2,1)S(1)} %bitcast.138, bf16[32,2,32,768]{3,2,1,0:T(8,128)(2,1)} %all-to-all-done), kind=kOutput, calls=%fused_computation.11 | convolution fusion | flops 2954231808 | bytes 10223616 | tf_op jit(solution)/shard_map/sxcf,sxcd->fxd/dot_general | solution.py:109
  422.0 6.4 %fusion.3 = bf16[704,2,1024]{2,0,1:T(8,128)(2,1)S(1)} fusion(bf16[32,2,32,1024]{3,2,1,0:T(8,128)(2,1)} %bitcast.137, bf16[32,2,32,768]{3,2,1,0:T(8,128)(2,1)} %all-to-all-done), kind=kOutput, calls=%fused_computation.10 | convolution fusion | flops 2954231808 | bytes 10223616 | tf_op jit(solution)/shard_map/sxcf,sxcd->fxd/dot_general | solution.py:109
  432.6 2.2 convolution_bitcast_fusion.5
  440.1 2.0 copy.88
  442.2 3.0 fusion.22
  445.2 2.1 copy.89
  447.3 3.2 fusion.19
  450.5 2.1 copy.90
  454.6 3.8 reduce-scatter.9.cloned.1.call-done
  459.4 38.1 %reduce-scatter.7.cloned.1.call-done = bf16[88,2048]{1,0:T(8,128)(2,1)} async-done(((bf16[704,2048]{1,0:T(8,128)(2,1)}), bf16[88,2048]{1,0:T(8,128)(2,1)}) %reduce-scatter.7.cloned.1.call-update) | async-done | bytes 360464
  (91 shorter events, 43.7 us)
Async XLA Ops:
  7.2 8.0 %copy-start.7 = (bf16[1,128,2048]{2,1,0:T(8,128)(2,1)S(1)}, bf16[1,128,2048]{2,1,0:T(8,128)(2,1)}, u32[]{:S(2)}) copy-start(bf16[1,128,2048]{2,1,0:T(8,128)(2,1)} %param.9) | copy-start | bytes 1572868
  7.2 286.9 %all-gather.3.cloned.1.call-start = ((), (), s32[]{:S(2)}) async-start(), calls=%async_computation.3 | async-start | bytes 8650752 | tf_op jit(solution)/shard_map/all_gather | solution.py:103
  8.4 1.8 copy-start.1
  10.3 1.1 copy-start.3
  11.4 15.8 %collective-permute-start = (bf16[16,128,128]{2,1,0:T(8,128)(2,1)}, bf16[16,128,128]{2,1,0:T(8,128)(2,1)S(1)}, u32[]{:S(2)}, u32[]{:S(2)}) collective-permute-start(bf16[16,128,128]{2,1,0:T(8,128)(2,1)} %get-tuple-element.31), channel_id=1, source_target_pairs={{0,8},{8,16},{16,24},{24,32},{32,40},{40,48},{48,56},{56,64},{64,7... | collective-permute-start | bytes 1572872 | tf_op jit(solution)/shard_map/ppermute | solution.py:89
  18.0 15.5 %collective-permute-start.5 = (bf16[16,128,128]{2,1,0:T(8,128)(2,1)S(1)}, bf16[16,128,128]{2,1,0:T(8,128)(2,1)S(1)}, u32[]{:S(2)}, u32[]{:S(2)}) collective-permute-start(bf16[16,128,128]{2,1,0:T(8,128)(2,1)S(1)} %get-tuple-element.33), channel_id=1, source_target_pairs={{8,0},{16,8},{24,16},{32,24},{40,32},{48,40},{56,48},{64,56},{72,6... | collective-permute-start | bytes 1572872 | tf_op jit(solution)/shard_map/ppermute | solution.py:90
  27.3 19.7 %collective-permute-start.1 = (bf16[16,128,128]{2,1,0:T(8,128)(2,1)S(1)}, bf16[16,128,128]{2,1,0:T(8,128)(2,1)S(1)}, u32[]{:S(2)}, u32[]{:S(2)}) collective-permute-start(bf16[16,128,128]{2,1,0:T(8,128)(2,1)S(1)} %fusion.27), channel_id=1, source_target_pairs={{0,16},{8,24},{16,32},{24,40},{32,48},{40,56},{48,64},{56,72},{64,... | collective-permute-start | bytes 1572872 | tf_op jit(solution)/shard_map/ppermute | solution.py:89
  33.6 21.2 %collective-permute-start.6 = (bf16[16,128,128]{2,1,0:T(8,128)(2,1)S(1)}, bf16[16,128,128]{2,1,0:T(8,128)(2,1)S(1)}, u32[]{:S(2)}, u32[]{:S(2)}) collective-permute-start(bf16[16,128,128]{2,1,0:T(8,128)(2,1)S(1)} %fusion.28), channel_id=1, source_target_pairs={{16,0},{24,8},{32,16},{40,24},{48,32},{56,40},{64,48},{72,56},{80,... | collective-permute-start | bytes 1572872 | tf_op jit(solution)/shard_map/ppermute | solution.py:90
  47.2 35.1 %collective-permute-start.2 = (bf16[16,128,128]{2,1,0:T(8,128)(2,1)S(1)}, bf16[16,128,128]{2,1,0:T(8,128)(2,1)S(1)}, u32[]{:S(2)}, u32[]{:S(2)}) collective-permute-start(bf16[16,128,128]{2,1,0:T(8,128)(2,1)S(1)} %add_convert_fusion.5), channel_id=1, source_target_pairs={{0,32},{8,40},{16,48},{24,56},{32,64},{40,72},{48,80},{56,88},{64,... | collective-permute-start | bytes 1572872 | tf_op jit(solution)/shard_map/ppermute | solution.py:89
  55.1 55.1 %collective-permute-start.7 = (bf16[16,128,128]{2,1,0:T(8,128)(2,1)S(1)}, bf16[16,128,128]{2,1,0:T(8,128)(2,1)S(1)}, u32[]{:S(2)}, u32[]{:S(2)}) collective-permute-start(bf16[16,128,128]{2,1,0:T(8,128)(2,1)S(1)} %add_convert_fusion.2), channel_id=1, source_target_pairs={{32,0},{40,8},{48,16},{56,24},{64,32},{72,40},{80,48},{88,56},{96,... | collective-permute-start | bytes 1572872 | tf_op jit(solution)/shard_map/ppermute | solution.py:90
  82.5 30.8 %collective-permute-start.3 = (bf16[16,128,128]{2,1,0:T(8,128)(2,1)S(1)}, bf16[16,128,128]{2,1,0:T(8,128)(2,1)S(1)}, u32[]{:S(2)}, u32[]{:S(2)}) collective-permute-start(bf16[16,128,128]{2,1,0:T(8,128)(2,1)S(1)} %add_convert_fusion.4), channel_id=1, source_target_pairs={{0,64},{8,72},{16,80},{24,88},{32,96},{40,104},{48,112},{56,120},{... | collective-permute-start | bytes 1572872 | tf_op jit(solution)/shard_map/ppermute | solution.py:89
  110.5 16.7 %collective-permute-start.8 = (bf16[16,128,128]{2,1,0:T(8,128)(2,1)S(1)}, bf16[16,128,128]{2,1,0:T(8,128)(2,1)S(1)}, u32[]{:S(2)}, u32[]{:S(2)}) collective-permute-start(bf16[16,128,128]{2,1,0:T(8,128)(2,1)S(1)} %add_convert_fusion.1), channel_id=1, source_target_pairs={{64,0},{72,8},{80,16},{88,24},{96,32},{104,40},{112,48},{120,56},{... | collective-permute-start | bytes 1572872 | tf_op jit(solution)/shard_map/ppermute | solution.py:90
  113.7 15.5 %collective-permute-start.4 = (bf16[16,128,128]{2,1,0:T(8,128)(2,1)S(1)}, bf16[16,128,128]{2,1,0:T(8,128)(2,1)S(1)}, u32[]{:S(2)}, u32[]{:S(2)}) collective-permute-start(bf16[16,128,128]{2,1,0:T(8,128)(2,1)S(1)} %add_convert_fusion.3), channel_id=1, source_target_pairs={{0,128},{8,136},{16,144},{24,152},{32,160},{40,168},{48,176},{56,1... | collective-permute-start | bytes 1572872 | tf_op jit(solution)/shard_map/ppermute | solution.py:89
  127.6 15.1 %copy-start.6 = (bf16[1,128,2048]{2,1,0:T(8,128)(2,1)S(1)}, bf16[1,128,2048]{2,1,0:T(8,128)(2,1)}, u32[]{:S(2)}) copy-start(bf16[1,128,2048]{2,1,0:T(8,128)(2,1)} %param.12) | copy-start | bytes 1572868
  127.6 14.7 %collective-permute-start.9 = (bf16[16,128,128]{2,1,0:T(8,128)(2,1)S(1)}, bf16[16,128,128]{2,1,0:T(8,128)(2,1)S(1)}, u32[]{:S(2)}, u32[]{:S(2)}) collective-permute-start(bf16[16,128,128]{2,1,0:T(8,128)(2,1)S(1)} %add_convert_fusion), channel_id=1, source_target_pairs={{128,0},{136,8},{144,16},{152,24},{160,32},{168,40},{176,48},{184,... | collective-permute-start | bytes 1572872 | tf_op jit(solution)/shard_map/ppermute | solution.py:90
  130.6 13.7 %copy-start.8 = (s32[1,128,6]{1,0,2:T(1,128)S(1)}, s32[1,128,6]{1,0,2:T(1,128)}, u32[]{:S(2)}) copy-start(s32[1,128,6]{1,0,2:T(1,128)} %param.13) | copy-start | bytes 9220
  143.6 250.1 %all-gather.5.cloned.1.call-start = ((), (), s32[]{:S(2)}) async-start(), calls=%async_computation.4 | async-start | bytes 8650752 | tf_op jit(solution)/shard_map/all_gather | solution.py:103
  150.1 3.9 copy-start.9
  161.1 115.5 %all-to-all-start = ((bf16[32,2,32,768]{3,2,1,0:T(8,128)(2,1)}), bf16[32,2,32,768]{3,2,1,0:T(8,128)(2,1)}, u32[]{:S(2)}, u32[]{:S(2)}) async-start(bf16[32,2,32,768]{3,2,1,0:T(8,128)(2,1)} %bitcast.139), calls=%async_computation | async-start | bytes 6291456 | tf_op jit(solution)/shard_map/all_to_all | solution.py:51
  181.9 276.5 %reduce-scatter.9.cloned.1.call-start = ((), (), s32[]{:S(2)}) async-start(), calls=%async_computation.6 | async-start | bytes 3244032
  421.7 75.7 %reduce-scatter.7.cloned.1.call-start = ((), (), s32[]{:S(2)}) async-start(), calls=%async_computation.5 | async-start | bytes 3244032
  428.3 2.0 copy-start.2
  430.3 2.2 copy-start.4
  434.8 3.5 copy-start
  445.2 7.4 %copy-start.5 = (f32[128,16,128]{0,2,1:T(8,128)S(1)}, f32[128,16,128]{0,2,1:T(8,128)}, u32[]{:S(2)}) copy-start(f32[128,16,128]{0,2,1:T(8,128)} %convolution_bitcast_fusion.1) | copy-start | bytes 3145732
Sparse Core Ops, SparseCore 0:
  143.7 150.3 all-gather.2
  297.3 96.4 all-gather.4
  421.8 36.5 reduce-scatter.8
  460.8 36.5 reduce-scatter.6

commit v7 on v6

--- a/solution.py
+++ b/solution.py
@@ -49,6 +49,7 @@
     ).astype(jnp.bfloat16)
     hidden_slots = hidden_slots.reshape(seq_count, EXP_DEV, CAP, lanes)
     arrived = lax.all_to_all(hidden_slots, "seq", split_axis=0, concat_axis=0, tiled=True)
+    all_cotangent = lax.all_gather(cotangent, "seq", axis=1, tiled=True)[0]
     arrived_hidden = arrived[..., :hidden_units]
     slot_token = jnp.maximum(arrived[..., hidden_units].astype(jnp.int32) - 1, 0)
     wanted = jnp.arange(seq_count, dtype=jnp.int32)[:, None, None] * tokens + slot_token
@@ -93,25 +94,15 @@
         fwd_window = state_sum + prefix_state
         bwd_window = grad_sum + after_state
         shift *= 2
-    late_cotangent, prefix_state, after_state = lax.optimization_barrier(
-        (cotangent, prefix_state, after_state)
+    all_cotangent, prefix_state, after_state = lax.optimization_barrier(
+        (all_cotangent, prefix_state, after_state)
     )
-    halves = 2
-    cols = width // halves
-    scattered = []
-    for half in range(halves):
-        gathered = lax.all_gather(
-            late_cotangent[:, :, half * cols:(half + 1) * cols], "seq", axis=1, tiled=True
-        )[0]
-        rows = jnp.take(gathered, wanted.reshape(-1), axis=0).reshape(
-            seq_count, EXP_DEV, CAP, cols
-        )
-        group_term = jnp.einsum(
-            "sxcf,sxcd->fxd", arrived_hidden, rows, preferred_element_type=jnp.float32
-        )
-        rounded = lax.optimization_barrier(group_term.astype(jnp.bfloat16))
-        scattered.append(lax.psum_scatter(rounded, "grp", scatter_dimension=0, tiled=True))
-    expert_grad = jnp.concatenate(scattered, axis=2).transpose(1, 0, 2)
+    rows = jnp.take(all_cotangent, wanted.reshape(-1), axis=0).reshape(
+        seq_count, EXP_DEV, CAP, width
+    )
+    group_term = jnp.einsum(
+        "sxcf,sxcd->fxd", arrived_hidden, rows, preferred_element_type=jnp.float32
+    )
     outputs = (
         out_local + jnp.einsum("thd,hde->the", query_full, prefix_state, precision=PRECISE)
     ) * row_scale
@@ -124,6 +115,10 @@
     def to_shard(array):
         return array.reshape(1, tokens, width).astype(jnp.bfloat16)
 
+    rounded = lax.optimization_barrier(group_term.astype(jnp.bfloat16)).astype(jnp.float32)
+    expert_grad = lax.psum_scatter(
+        rounded.astype(jnp.bfloat16), "grp", scatter_dimension=0, tiled=True
+    ).transpose(1, 0, 2)
     return (to_shard(outputs), to_shard(grad_q), to_shard(grad_k), to_shard(grad_v), expert_grad)
 
 

time: 507 us -> 398 us (0.79)
  waiting for transfers between devices: 310 us -> 225 us
  starting transfers between devices: 71.7 us -> 51.3 us
  local copies, waits for them, and re-layouts: 57.7 us -> 51.1 us
  matrix products: 35.7 us -> 41.8 us
    ppermute x5, waiting for transfers between devices: 46.6 us -> 166 us  [per_device(): lax.ppermute(fwd_window.astype(jnp.bfloat16), 'seq', fwd_pairs)]
    all_gather x2 -> x1, waiting for transfers between devices: 99.1 us -> 0.02 us  [per_device(): all_cotangent = lax.all_gather(cotangent, 'seq', axis=1, tiled=True)[0]]
    all_to_all x1, waiting for transfers between devices: 94.3 us -> 0.01 us  [per_device(): lax.all_to_all(hidden_slots, 'seq', split_axis=0, concat_axis=0, tiled=True)]
    unnamed x6 -> x3, waiting for transfers between devices: 42.6 us -> 14.3 us
    ppermute x5, waiting for transfers between devices: 27.5 us -> 44.8 us  [per_device(): lax.ppermute(bwd_window.astype(jnp.bfloat16), 'seq', bwd_pairs)]
    ppermute x5, starting transfers between devices: 43.1 us -> 31.7 us  [per_device(): lax.ppermute(fwd_window.astype(jnp.bfloat16), 'seq', fwd_pairs)]
    all_to_all x1, starting transfers between devices: 20.8 us -> 11.5 us  [per_device(): lax.all_to_all(hidden_slots, 'seq', split_axis=0, concat_axis=0, tiled=True)]
    gather x2 -> x1, local copies, waits for them, and re-layouts: 30.9 us -> 24.3 us  [per_device(): jnp.take(all_cotangent, wanted.reshape(-1), axis=0)]
  transfers between devices with their start and end apart: 15 -> 13, of which waited for: 14 -> 7; matrix products, arithmetic and copies ran while one was open for 15% -> 14% of each run, Pallas kernels for 0% -> 0%
where the time goes in v7:
time: 398 us; the launch traced here: 396 us
  waiting for transfers between devices  225 us (57%)
  starting transfers between devices  51.3 us (13%)
  local copies, waits for them, and re-layouts  51.1 us (13%)
  matrix products  41.8 us (11%)
  between operations  14.6 us (4%)
  other arithmetic  13 us (3%)
    ppermute x5, waiting for transfers between devices, per_device(): lax.ppermute(fwd_window.astype(jnp.bfloat16), 'seq', fwd_pairs)  166 us
    ppermute x5, waiting for transfers between devices, per_device(): lax.ppermute(bwd_window.astype(jnp.bfloat16), 'seq', bwd_pairs)  44.8 us
    ppermute x5, starting transfers between devices, per_device(): lax.ppermute(fwd_window.astype(jnp.bfloat16), 'seq', fwd_pairs)  31.7 us
    gather x1, local copies, waits for them, and re-layouts, per_device(): jnp.take(all_cotangent, wanted.reshape(-1), axis=0)  24.3 us
    unnamed x58, local copies, waits for them, and re-layouts  20 us
    dot_general x1, matrix products, per_device(): jnp.einsum('sxcf,sxcd->fxd', arrived_hidden, rows, preferred_element_type...  17.8 us
    unnamed x3, waiting for transfers between devices  14.3 us
    all_to_all x1, starting transfers between devices, per_device(): lax.all_to_all(hidden_slots, 'seq', split_axis=0, concat_axis=0, tiled=True)  11.5 us
  transfers between devices with their start and end apart: 13, of which 7 were waited for; matrix products, arithmetic and copies ran while one was open for 14% of the time, Pallas kernels for 0%

profile of v7, /device:TPU:32, one launch (start us, length us, event | category | flops | bytes accessed | tf_op | source)
XLA Modules:
  0.0 396.5 jit_solution(18339225223019535254)
XLA Ops:
  9.9 1.8 reduce-window.6
  12.0 2.0 copy.88
  16.0 1.9 multiply_convert_fusion
  17.9 4.7 %fusion.5 = bf16[2048,768]{1,0:T(8,128)(2,1)} fusion(s32[768]{0:T(1024)S(1)} %multiply_add_fusion, bf16[768,1]{1,0:T(8,128)(2,1)S(1)} %fusion.36, bf16[768,704]{1,0:T(8,128)(2,1)S(1)} %multiply_convert_fusion, bf16[768]{0:T(1024)(128)(2,1)S(1)} %pad.2.clone), kind=kOutput, calls=%fused_computation.9 | convolution fusion | flops 2422603776 | bytes 4233216 | tf_op jit(solution)/shard_map/dot_general | solution.py:47
  22.6 11.5 %all-to-all-start = ((bf16[32,2,32,768]{3,2,1,0:T(8,128)(2,1)}), bf16[32,2,32,768]{3,2,1,0:T(8,128)(2,1)}, u32[]{:S(2)}, u32[]{:S(2)}) async-start(bf16[32,2,32,768]{3,2,1,0:T(8,128)(2,1)} %bitcast.15), calls=%async_computation | async-start | bytes 6291456 | tf_op jit(solution)/shard_map/all_to_all | solution.py:51
  36.3 3.4 collective-permute-start
  42.5 2.5 collective-permute-start.5
  45.0 102.1 %collective-permute-done = bf16[16,128,128]{2,1,0:T(8,128)(2,1)S(1)} collective-permute-done((bf16[16,128,128]{2,1,0:T(8,128)(2,1)}, bf16[16,128,128]{2,1,0:T(8,128)(2,1)S(1)}, u32[]{:S(2)}, u32[]{:S(2)}) %collective-permute-start) | collective-permute-done | bytes 524320 | tf_op jit(solution)/shard_map/ppermute | solution.py:90
  147.2 4.2 %collective-permute-start.1 = (bf16[16,128,128]{2,1,0:T(8,128)(2,1)S(1)}, bf16[16,128,128]{2,1,0:T(8,128)(2,1)S(1)}, u32[]{:S(2)}, u32[]{:S(2)}) collective-permute-start(bf16[16,128,128]{2,1,0:T(8,128)(2,1)S(1)} %fusion.22), channel_id=1, source_target_pairs={{0,16},{8,24},{16,32},{24,40},{32,48},{40,56},{48,64},{56,72},{64,... | collective-permute-start | bytes 1572872 | tf_op jit(solution)/shard_map/ppermute | solution.py:90
  152.9 32.0 %collective-permute-done.1 = bf16[16,128,128]{2,1,0:T(8,128)(2,1)S(1)} collective-permute-done((bf16[16,128,128]{2,1,0:T(8,128)(2,1)S(1)}, bf16[16,128,128]{2,1,0:T(8,128)(2,1)S(1)}, u32[]{:S(2)}, u32[]{:S(2)}) %collective-permute-start.1) | collective-permute-done | bytes 524320 | tf_op jit(solution)/shard_map/ppermute | solution.py:90
  185.1 9.3 %collective-permute-start.2 = (bf16[16,128,128]{2,1,0:T(8,128)(2,1)S(1)}, bf16[16,128,128]{2,1,0:T(8,128)(2,1)S(1)}, u32[]{:S(2)}, u32[]{:S(2)}) collective-permute-start(bf16[16,128,128]{2,1,0:T(8,128)(2,1)S(1)} %add_convert_fusion.5), channel_id=1, source_target_pairs={{0,32},{8,40},{16,48},{24,56},{32,64},{40,72},{48,80},{56,88},{64,... | collective-permute-start | bytes 1572872 | tf_op jit(solution)/shard_map/ppermute | solution.py:90
  195.9 31.5 %collective-permute-done.2 = bf16[16,128,128]{2,1,0:T(8,128)(2,1)S(1)} collective-permute-done((bf16[16,128,128]{2,1,0:T(8,128)(2,1)S(1)}, bf16[16,128,128]{2,1,0:T(8,128)(2,1)S(1)}, u32[]{:S(2)}, u32[]{:S(2)}) %collective-permute-start.2) | collective-permute-done | bytes 524320 | tf_op jit(solution)/shard_map/ppermute | solution.py:90
  227.7 9.1 %collective-permute-start.3 = (bf16[16,128,128]{2,1,0:T(8,128)(2,1)S(1)}, bf16[16,128,128]{2,1,0:T(8,128)(2,1)S(1)}, u32[]{:S(2)}, u32[]{:S(2)}) collective-permute-start(bf16[16,128,128]{2,1,0:T(8,128)(2,1)S(1)} %add_convert_fusion.4), channel_id=1, source_target_pairs={{0,64},{8,72},{16,80},{24,88},{32,96},{40,104},{48,112},{56,120},{... | collective-permute-start | bytes 1572872 | tf_op jit(solution)/shard_map/ppermute | solution.py:90
  236.8 27.5 %collective-permute-done.7 = bf16[16,128,128]{2,1,0:T(8,128)(2,1)S(1)} collective-permute-done((bf16[16,128,128]{2,1,0:T(8,128)(2,1)S(1)}, bf16[16,128,128]{2,1,0:T(8,128)(2,1)S(1)}, u32[]{:S(2)}, u32[]{:S(2)}) %collective-permute-start.7) | collective-permute-done | bytes 524320 | tf_op jit(solution)/shard_map/ppermute | solution.py:91
  267.1 5.7 %collective-permute-start.4 = (bf16[16,128,128]{2,1,0:T(8,128)(2,1)}, bf16[16,128,128]{2,1,0:T(8,128)(2,1)}, u32[]{:S(2)}, u32[]{:S(2)}) collective-permute-start(bf16[16,128,128]{2,1,0:T(8,128)(2,1)} %add_convert_fusion.3), channel_id=1, source_target_pairs={{0,128},{8,136},{16,144},{24,152},{32,160},{40,168},{48,176},{56,1... | collective-permute-start | bytes 1572872 | tf_op jit(solution)/shard_map/ppermute | solution.py:90
  272.8 8.6 %collective-permute-done.8 = bf16[16,128,128]{2,1,0:T(8,128)(2,1)S(1)} collective-permute-done((bf16[16,128,128]{2,1,0:T(8,128)(2,1)S(1)}, bf16[16,128,128]{2,1,0:T(8,128)(2,1)S(1)}, u32[]{:S(2)}, u32[]{:S(2)}) %collective-permute-start.8) | collective-permute-done | bytes 524320 | tf_op jit(solution)/shard_map/ppermute | solution.py:91
  284.4 2.8 convert_add_fusion.7
  287.3 8.8 %collective-permute-done.9 = bf16[16,128,128]{2,1,0:T(8,128)(2,1)} collective-permute-done((bf16[16,128,128]{2,1,0:T(8,128)(2,1)}, bf16[16,128,128]{2,1,0:T(8,128)(2,1)}, u32[]{:S(2)}, u32[]{:S(2)}) %collective-permute-start.9) | collective-permute-done | bytes 524320 | tf_op jit(solution)/shard_map/ppermute | solution.py:91
  296.0 2.5 convert_add_fusion.4
  300.6 24.3 %gather_fusion = bf16[2048,2048]{1,0:T(8,128)(2,1)} fusion(bf16[4096,2048]{1,0:T(8,128)(2,1)} %bitcast.113, s32[2048]{0:T(1024)S(1)} %broadcast_clamp_fusion), kind=kCustom, calls=%fused_computation | custom fusion | bytes 16785408 | tf_op jit(solution)/shard_map/jit(_take)/gather | solution.py:100
  324.9 17.8 %fusion.3 = bf16[704,2,2048]{2,0,1:T(8,128)(2,1)} fusion(bf16[32,2,32,2048]{3,2,1,0:T(8,128)(2,1)} %bitcast.127, pred[32,2,32]{0,2,1:T(8,128)(4,1)S(1)} %copy.90, bf16[32,2,32,704]{3,2,1,0:T(8,128)(2,1)} %bitcast.112), kind=kOutput, calls=%fused_computation.7 | convolution fusion | flops 5912657920 | bytes 17041408 | tf_op jit(solution)/shard_map/sxcf,sxcd->fxd/dot_general | solution.py:103
  342.7 6.1 %copy.111 = bf16[2,88,8,2048]{3,2,0,1:T(8,128)(2,1)} copy(bf16[2,88,8,2048]{3,2,1,0:T(8,128)(2,1)} %bitcast.131) | data formatting | bytes 11534336
  352.0 2.2 convolution_bitcast_fusion.5
  356.0 1.8 convolution_bitcast_fusion.3
  357.8 1.8 fusion.16
  359.6 2.1 copy.95
  361.7 2.7 fusion.17
  364.4 2.2 copy.96
  366.6 3.3 fusion.14
  369.9 2.1 copy.97
  373.9 13.6 %reduce-scatter.4.cloned.1.call-done = bf16[88,4096]{1,0:T(8,128)(2,1)} async-done(((bf16[704,4096]{1,0:T(8,128)(2,1)}), bf16[88,4096]{1,0:T(8,128)(2,1)}) %reduce-scatter.4.cloned.1.call-update) | async-done | bytes 720912
  387.6 2.0 copy.136
  (109 shorter events, 28.1 us)
Async XLA Ops:
  7.2 293.5 %all-gather.2.cloned.1.call-start = ((), (), s32[]{:S(2)}) async-start(), calls=%async_computation.2 | async-start | bytes 17301504 | tf_op jit(solution)/shard_map/all_gather | solution.py:52
  22.6 11.6 %copy-start.21 = (bf16[1,128,2048]{2,1,0:T(8,128)(2,1)S(1)}, bf16[1,128,2048]{2,1,0:T(8,128)(2,1)}, u32[]{:S(2)}) copy-start(bf16[1,128,2048]{2,1,0:T(8,128)(2,1)} %param.8) | copy-start | bytes 1572868
  22.6 12.2 %copy-start.22 = (bf16[1,128,2048]{2,1,0:T(8,128)(2,1)S(1)}, bf16[1,128,2048]{2,1,0:T(8,128)(2,1)}, u32[]{:S(2)}) copy-start(bf16[1,128,2048]{2,1,0:T(8,128)(2,1)} %param.9) | copy-start | bytes 1572868
  22.6 275.9 %all-to-all-start = ((bf16[32,2,32,768]{3,2,1,0:T(8,128)(2,1)}), bf16[32,2,32,768]{3,2,1,0:T(8,128)(2,1)}, u32[]{:S(2)}, u32[]{:S(2)}) async-start(bf16[32,2,32,768]{3,2,1,0:T(8,128)(2,1)} %bitcast.15), calls=%async_computation | async-start | bytes 6291456 | tf_op jit(solution)/shard_map/all_to_all | solution.py:51
  34.2 5.5 %copy-start.20 = (bf16[1,128,2048]{2,1,0:T(8,128)(2,1)S(1)}, bf16[1,128,2048]{2,1,0:T(8,128)(2,1)}, u32[]{:S(2)}) copy-start(bf16[1,128,2048]{2,1,0:T(8,128)(2,1)} %param.10) | copy-start | bytes 1572868
  34.2 353.4 %reduce-scatter.4.cloned.1.call-start = ((), (), s32[]{:S(2)}) async-start(), calls=%async_computation.3 | async-start | bytes 6488064
  34.8 1.4 copy-start.11
  36.3 110.8 %collective-permute-start = (bf16[16,128,128]{2,1,0:T(8,128)(2,1)}, bf16[16,128,128]{2,1,0:T(8,128)(2,1)S(1)}, u32[]{:S(2)}, u32[]{:S(2)}) collective-permute-start(bf16[16,128,128]{2,1,0:T(8,128)(2,1)} %get-tuple-element.26), channel_id=1, source_target_pairs={{0,8},{8,16},{16,24},{24,32},{32,40},{40,48},{48,56},{56,64},{64,7... | collective-permute-start | bytes 1572872 | tf_op jit(solution)/shard_map/ppermute | solution.py:90
  41.3 1.2 copy-start
  42.5 109.0 %collective-permute-start.5 = (bf16[16,128,128]{2,1,0:T(8,128)(2,1)S(1)}, bf16[16,128,128]{2,1,0:T(8,128)(2,1)S(1)}, u32[]{:S(2)}, u32[]{:S(2)}) collective-permute-start(bf16[16,128,128]{2,1,0:T(8,128)(2,1)S(1)} %get-tuple-element.28), channel_id=1, source_target_pairs={{8,0},{16,8},{24,16},{32,24},{40,32},{48,40},{56,48},{64,56},{72,6... | collective-permute-start | bytes 1572872 | tf_op jit(solution)/shard_map/ppermute | solution.py:91
  147.2 37.7 %collective-permute-start.1 = (bf16[16,128,128]{2,1,0:T(8,128)(2,1)S(1)}, bf16[16,128,128]{2,1,0:T(8,128)(2,1)S(1)}, u32[]{:S(2)}, u32[]{:S(2)}) collective-permute-start(bf16[16,128,128]{2,1,0:T(8,128)(2,1)S(1)} %fusion.22), channel_id=1, source_target_pairs={{0,16},{8,24},{16,32},{24,40},{32,48},{40,56},{48,64},{56,72},{64,... | collective-permute-start | bytes 1572872 | tf_op jit(solution)/shard_map/ppermute | solution.py:90
  151.6 42.8 %collective-permute-start.6 = (bf16[16,128,128]{2,1,0:T(8,128)(2,1)S(1)}, bf16[16,128,128]{2,1,0:T(8,128)(2,1)S(1)}, u32[]{:S(2)}, u32[]{:S(2)}) collective-permute-start(bf16[16,128,128]{2,1,0:T(8,128)(2,1)S(1)} %fusion.23), channel_id=1, source_target_pairs={{16,0},{24,8},{32,16},{40,24},{48,32},{56,40},{64,48},{72,56},{80,... | collective-permute-start | bytes 1572872 | tf_op jit(solution)/shard_map/ppermute | solution.py:91
  184.9 81.1 %copy-start.4 = (bf16[16,128,128]{2,1,0:T(8,128)(2,1)}, bf16[16,128,128]{2,1,0:T(8,128)(2,1)S(1)}, u32[]{:S(2)}) copy-start(bf16[16,128,128]{2,1,0:T(8,128)(2,1)S(1)} %collective-permute-done.1) | copy-start | bytes 1572868
  185.1 42.3 %collective-permute-start.2 = (bf16[16,128,128]{2,1,0:T(8,128)(2,1)S(1)}, bf16[16,128,128]{2,1,0:T(8,128)(2,1)S(1)}, u32[]{:S(2)}, u32[]{:S(2)}) collective-permute-start(bf16[16,128,128]{2,1,0:T(8,128)(2,1)S(1)} %add_convert_fusion.5), channel_id=1, source_target_pairs={{0,32},{8,40},{16,48},{24,56},{32,64},{40,72},{48,80},{56,88},{64,... | collective-permute-start | bytes 1572872 | tf_op jit(solution)/shard_map/ppermute | solution.py:90
  194.4 87.0 %copy-start.6 = (bf16[16,128,128]{2,1,0:T(8,128)(2,1)}, bf16[16,128,128]{2,1,0:T(8,128)(2,1)S(1)}, u32[]{:S(2)}) copy-start(bf16[16,128,128]{2,1,0:T(8,128)(2,1)S(1)} %collective-permute-done.6) | copy-start | bytes 1572868
  194.6 69.7 %collective-permute-start.7 = (bf16[16,128,128]{2,1,0:T(8,128)(2,1)S(1)}, bf16[16,128,128]{2,1,0:T(8,128)(2,1)S(1)}, u32[]{:S(2)}, u32[]{:S(2)}) collective-permute-start(bf16[16,128,128]{2,1,0:T(8,128)(2,1)S(1)} %add_convert_fusion.2), channel_id=1, source_target_pairs={{32,0},{40,8},{48,16},{56,24},{64,32},{72,40},{80,48},{88,56},{96,... | collective-permute-start | bytes 1572872 | tf_op jit(solution)/shard_map/ppermute | solution.py:91
  227.4 38.5 %copy-start.15 = (bf16[16,128,128]{2,1,0:T(8,128)(2,1)}, bf16[16,128,128]{2,1,0:T(8,128)(2,1)S(1)}, u32[]{:S(2)}) copy-start(bf16[16,128,128]{2,1,0:T(8,128)(2,1)S(1)} %collective-permute-done.2) | copy-start | bytes 1572868
  227.7 38.2 %collective-permute-start.3 = (bf16[16,128,128]{2,1,0:T(8,128)(2,1)S(1)}, bf16[16,128,128]{2,1,0:T(8,128)(2,1)S(1)}, u32[]{:S(2)}, u32[]{:S(2)}) collective-permute-start(bf16[16,128,128]{2,1,0:T(8,128)(2,1)S(1)} %add_convert_fusion.4), channel_id=1, source_target_pairs={{0,64},{8,72},{16,80},{24,88},{32,96},{40,104},{48,112},{56,120},{... | collective-permute-start | bytes 1572872 | tf_op jit(solution)/shard_map/ppermute | solution.py:90
  264.3 17.0 %copy-start.13 = (bf16[16,128,128]{2,1,0:T(8,128)(2,1)}, bf16[16,128,128]{2,1,0:T(8,128)(2,1)S(1)}, u32[]{:S(2)}) copy-start(bf16[16,128,128]{2,1,0:T(8,128)(2,1)S(1)} %collective-permute-done.7) | copy-start | bytes 1572868
  264.6 16.8 %collective-permute-start.8 = (bf16[16,128,128]{2,1,0:T(8,128)(2,1)S(1)}, bf16[16,128,128]{2,1,0:T(8,128)(2,1)S(1)}, u32[]{:S(2)}, u32[]{:S(2)}) collective-permute-start(bf16[16,128,128]{2,1,0:T(8,128)(2,1)S(1)} %add_convert_fusion.1), channel_id=1, source_target_pairs={{64,0},{72,8},{80,16},{88,24},{96,32},{104,40},{112,48},{120,56},{... | collective-permute-start | bytes 1572872 | tf_op jit(solution)/shard_map/ppermute | solution.py:91
  266.0 16.6 %copy-start.19 = (bf16[16,128,128]{2,1,0:T(8,128)(2,1)}, bf16[16,128,128]{2,1,0:T(8,128)(2,1)S(1)}, u32[]{:S(2)}) copy-start(bf16[16,128,128]{2,1,0:T(8,128)(2,1)S(1)} %collective-permute-done.3) | copy-start | bytes 1572868
  267.1 17.3 %copy-start.5 = (bf16[16,128,128]{2,1,0:T(8,128)(2,1)S(1)}, bf16[16,128,128]{2,1,0:T(8,128)(2,1)}, u32[]{:S(2)}) copy-start(bf16[16,128,128]{2,1,0:T(8,128)(2,1)} %copy-done.4) | copy-start | bytes 1572868
  267.1 17.3 %collective-permute-start.4 = (bf16[16,128,128]{2,1,0:T(8,128)(2,1)}, bf16[16,128,128]{2,1,0:T(8,128)(2,1)}, u32[]{:S(2)}, u32[]{:S(2)}) collective-permute-start(bf16[16,128,128]{2,1,0:T(8,128)(2,1)} %add_convert_fusion.3), channel_id=1, source_target_pairs={{0,128},{8,136},{16,144},{24,152},{32,160},{40,168},{48,176},{56,1... | collective-permute-start | bytes 1572872 | tf_op jit(solution)/shard_map/ppermute | solution.py:90
  282.6 13.5 %copy-start.7 = (bf16[16,128,128]{2,1,0:T(8,128)(2,1)S(1)}, bf16[16,128,128]{2,1,0:T(8,128)(2,1)}, u32[]{:S(2)}) copy-start(bf16[16,128,128]{2,1,0:T(8,128)(2,1)} %copy-done.6) | copy-start | bytes 1572868
  282.6 13.5 %collective-permute-start.9 = (bf16[16,128,128]{2,1,0:T(8,128)(2,1)}, bf16[16,128,128]{2,1,0:T(8,128)(2,1)}, u32[]{:S(2)}, u32[]{:S(2)}) collective-permute-start(bf16[16,128,128]{2,1,0:T(8,128)(2,1)} %add_convert_fusion), channel_id=1, source_target_pairs={{128,0},{136,8},{144,16},{152,24},{160,32},{168,40},{176,48},{184,... | collective-permute-start | bytes 1572872 | tf_op jit(solution)/shard_map/ppermute | solution.py:91
  284.4 11.6 %copy-start.14 = (bf16[16,128,128]{2,1,0:T(8,128)(2,1)S(1)}, bf16[16,128,128]{2,1,0:T(8,128)(2,1)}, u32[]{:S(2)}) copy-start(bf16[16,128,128]{2,1,0:T(8,128)(2,1)} %copy-done.13) | copy-start | bytes 1572868
  284.4 11.6 %copy-start.18 = (bf16[16,128,128]{2,1,0:T(8,128)(2,1)S(1)}, bf16[16,128,128]{2,1,0:T(8,128)(2,1)}, u32[]{:S(2)}) copy-start(bf16[16,128,128]{2,1,0:T(8,128)(2,1)} %copy-done.17) | copy-start | bytes 1572868
  348.9 3.1 copy-start.12
  354.2 3.6 copy-start.3
  359.6 7.0 %copy-start.2 = (f32[16,128,128]{2,1,0:T(8,128)S(1)}, f32[16,128,128]{2,1,0:T(8,128)}, u32[]{:S(2)}) copy-start(f32[16,128,128]{2,1,0:T(8,128)} %convert_add_fusion.4) | copy-start | bytes 3145732
  364.4 7.5 %copy-start.10 = (bf16[16,8,16,128]{3,2,1,0:T(8,128)(2,1)S(1)}, bf16[16,8,16,128]{3,2,1,0:T(8,128)(2,1)}, u32[]{:S(2)}) copy-start(bf16[16,8,16,128]{3,2,1,0:T(8,128)(2,1)} %copy-done.8) | copy-start | bytes 1572868
  364.4 7.5 %copy-start.16 = (f32[128,16,128]{0,2,1:T(8,128)S(1)}, f32[128,16,128]{0,2,1:T(8,128)}, u32[]{:S(2)}) copy-start(f32[128,16,128]{0,2,1:T(8,128)} %convolution_bitcast_fusion.1) | copy-start | bytes 3145732
  (4 other events, 4.2 us)
Sparse Core Ops, SparseCore 0:
  10.6 260.5 all-gather.1
  349.0 38.5 reduce-scatter.3

commit v8 on v7

--- a/solution.py
+++ b/solution.py
@@ -51,8 +51,13 @@
     arrived = lax.all_to_all(hidden_slots, "seq", split_axis=0, concat_axis=0, tiled=True)
     all_cotangent = lax.all_gather(cotangent, "seq", axis=1, tiled=True)[0]
     arrived_hidden = arrived[..., :hidden_units]
-    slot_token = jnp.maximum(arrived[..., hidden_units].astype(jnp.int32) - 1, 0)
-    wanted = jnp.arange(seq_count, dtype=jnp.int32)[:, None, None] * tokens + slot_token
+    slot_token = arrived[..., hidden_units].astype(jnp.int32) - 1
+    token_pick = (
+        slot_token[:, :, None, :] == jnp.arange(tokens, dtype=jnp.int32)[None, None, :, None]
+    ).astype(jnp.bfloat16)
+    token_weights = jnp.einsum(
+        "sxtc,sxcf->fxst", token_pick, arrived_hidden, preferred_element_type=jnp.float32
+    ).astype(jnp.bfloat16).reshape(hidden_units * EXP_DEV, seq_count * tokens)
 
     query_raw = query[0].reshape(tokens, HEADS, head_dim)
     key_raw = key_in[0].reshape(tokens, HEADS, head_dim)
@@ -97,12 +102,9 @@
     all_cotangent, prefix_state, after_state = lax.optimization_barrier(
         (all_cotangent, prefix_state, after_state)
     )
-    rows = jnp.take(all_cotangent, wanted.reshape(-1), axis=0).reshape(
-        seq_count, EXP_DEV, CAP, width
-    )
-    group_term = jnp.einsum(
-        "sxcf,sxcd->fxd", arrived_hidden, rows, preferred_element_type=jnp.float32
-    )
+    group_term = jnp.dot(
+        token_weights, all_cotangent, preferred_element_type=jnp.float32
+    ).reshape(hidden_units, EXP_DEV, width)
     outputs = (
         out_local + jnp.einsum("thd,hde->the", query_full, prefix_state, precision=PRECISE)
     ) * row_scale

time: 398 us -> 387 us (0.972)
  local copies, waits for them, and re-layouts: 51.1 us -> 23 us
  matrix products: 41.8 us -> 62.4 us
  other arithmetic: 13 us -> 7.74 us
    gather x1 -> x0, local copies, waits for them, and re-layouts: 24.3 us -> none  [per_device(): jnp.take(all_cotangent, wanted.reshape(-1), axis=0)]
    dot_general x1 -> x2, matrix products: 17.8 us -> 38.3 us  [the longest x1 30.4 us: per_device(): jnp.dot(token_weights, all_cotangent, preferred_element_type=jnp.float32)]
    unnamed x58 -> x30, local copies, waits for them, and re-layouts: 20 us -> 16.6 us
  transfers between devices with their start and end apart: 13 -> 13, of which waited for: 7 -> 7; matrix products, arithmetic and copies ran while one was open for 14% -> 15% of each run, Pallas kernels for 0% -> 0%
where the time goes in v8:
time: 387 us; the launch traced here: 386 us
  waiting for transfers between devices  228 us (59%)
  matrix products  62.4 us (16%)
  starting transfers between devices  50.6 us (13%)
  local copies, waits for them, and re-layouts  23 us (6%)
  between operations  14.5 us (4%)
  other arithmetic  7.74 us (2%)
    ppermute x5, waiting for transfers between devices, per_device(): lax.ppermute(fwd_window.astype(jnp.bfloat16), 'seq', fwd_pairs)  166 us
    ppermute x5, waiting for transfers between devices, per_device(): lax.ppermute(bwd_window.astype(jnp.bfloat16), 'seq', bwd_pairs)  47.5 us
    ppermute x5, starting transfers between devices, per_device(): lax.ppermute(fwd_window.astype(jnp.bfloat16), 'seq', fwd_pairs)  31.1 us
    dot_general x1, matrix products, per_device(): jnp.dot(token_weights, all_cotangent, preferred_element_type=jnp.float32)  30.4 us
    unnamed x30, local copies, waits for them, and re-layouts  16.6 us
    unnamed x3, waiting for transfers between devices  14.7 us
    all_to_all x1, starting transfers between devices, per_device(): lax.all_to_all(hidden_slots, 'seq', split_axis=0, concat_axis=0, tiled=True)  11.5 us
    dot_general x1, matrix products, per_device(): jnp.einsum('sxtc,sxcf->fxst', token_pick, arrived_hidden, preferred_eleme...  7.92 us
  transfers between devices with their start and end apart: 13, of which 7 were waited for; matrix products, arithmetic and copies ran while one was open for 15% of the time, Pallas kernels for 0%

profile of v8, /device:TPU:32, one launch (start us, length us, event | category | flops | bytes accessed | tf_op | source)
XLA Modules:
  0.0 386.0 jit_solution(618042712283653103)
XLA Ops:
  9.9 1.8 reduce-window.6
  12.0 2.0 copy.83
  14.1 1.6 reshape.176
  16.0 1.9 multiply_convert_fusion
  17.9 4.7 %fusion.10 = bf16[2048,768]{1,0:T(8,128)(2,1)} fusion(s32[768]{0:T(1024)S(1)} %multiply_add_fusion, bf16[768,1]{1,0:T(8,128)(2,1)S(1)} %fusion.42, bf16[768,704]{1,0:T(8,128)(2,1)S(1)} %multiply_convert_fusion, bf16[768]{0:T(1024)(128)(2,1)S(1)} %pad.2.clone), kind=kOutput, calls=%fused_computation.8 | convolution fusion | flops 2422603776 | bytes 4233216 | tf_op jit(solution)/shard_map/dot_general | solution.py:47
  22.6 11.5 %all-to-all-start = ((bf16[32,2,32,768]{3,2,1,0:T(8,128)(2,1)}), bf16[32,2,32,768]{3,2,1,0:T(8,128)(2,1)}, u32[]{:S(2)}, u32[]{:S(2)}) async-start(bf16[32,2,32,768]{3,2,1,0:T(8,128)(2,1)} %bitcast.15), calls=%async_computation | async-start | bytes 6291456 | tf_op jit(solution)/shard_map/all_to_all | solution.py:51
  36.2 3.4 collective-permute-start
  42.5 2.5 collective-permute-start.5
  45.0 102.1 %collective-permute-done = bf16[16,128,128]{2,1,0:T(8,128)(2,1)S(1)} collective-permute-done((bf16[16,128,128]{2,1,0:T(8,128)(2,1)}, bf16[16,128,128]{2,1,0:T(8,128)(2,1)S(1)}, u32[]{:S(2)}, u32[]{:S(2)}) %collective-permute-start) | collective-permute-done | bytes 524320 | tf_op jit(solution)/shard_map/ppermute | solution.py:95
  147.2 4.2 %collective-permute-start.1 = (bf16[16,128,128]{2,1,0:T(8,128)(2,1)S(1)}, bf16[16,128,128]{2,1,0:T(8,128)(2,1)S(1)}, u32[]{:S(2)}, u32[]{:S(2)}) collective-permute-start(bf16[16,128,128]{2,1,0:T(8,128)(2,1)S(1)} %fusion.27), channel_id=1, source_target_pairs={{0,16},{8,24},{16,32},{24,40},{32,48},{40,56},{48,64},{56,72},{64,... | collective-permute-start | bytes 1572872 | tf_op jit(solution)/shard_map/ppermute | solution.py:95
  152.9 32.0 %collective-permute-done.1 = bf16[16,128,128]{2,1,0:T(8,128)(2,1)S(1)} collective-permute-done((bf16[16,128,128]{2,1,0:T(8,128)(2,1)S(1)}, bf16[16,128,128]{2,1,0:T(8,128)(2,1)S(1)}, u32[]{:S(2)}, u32[]{:S(2)}) %collective-permute-start.1) | collective-permute-done | bytes 524320 | tf_op jit(solution)/shard_map/ppermute | solution.py:95
  185.1 9.3 %collective-permute-start.2 = (bf16[16,128,128]{2,1,0:T(8,128)(2,1)S(1)}, bf16[16,128,128]{2,1,0:T(8,128)(2,1)S(1)}, u32[]{:S(2)}, u32[]{:S(2)}) collective-permute-start(bf16[16,128,128]{2,1,0:T(8,128)(2,1)S(1)} %add_convert_fusion.5), channel_id=1, source_target_pairs={{0,32},{8,40},{16,48},{24,56},{32,64},{40,72},{48,80},{56,88},{64,... | collective-permute-start | bytes 1572872 | tf_op jit(solution)/shard_map/ppermute | solution.py:95
  195.9 31.5 %collective-permute-done.2 = bf16[16,128,128]{2,1,0:T(8,128)(2,1)S(1)} collective-permute-done((bf16[16,128,128]{2,1,0:T(8,128)(2,1)S(1)}, bf16[16,128,128]{2,1,0:T(8,128)(2,1)S(1)}, u32[]{:S(2)}, u32[]{:S(2)}) %collective-permute-start.2) | collective-permute-done | bytes 524320 | tf_op jit(solution)/shard_map/ppermute | solution.py:95
  227.7 9.3 %collective-permute-start.3 = (bf16[16,128,128]{2,1,0:T(8,128)(2,1)S(1)}, bf16[16,128,128]{2,1,0:T(8,128)(2,1)S(1)}, u32[]{:S(2)}, u32[]{:S(2)}) collective-permute-start(bf16[16,128,128]{2,1,0:T(8,128)(2,1)S(1)} %add_convert_fusion.4), channel_id=1, source_target_pairs={{0,64},{8,72},{16,80},{24,88},{32,96},{40,104},{48,112},{56,120},{... | collective-permute-start | bytes 1572872 | tf_op jit(solution)/shard_map/ppermute | solution.py:95
  237.0 27.3 %collective-permute-done.7 = bf16[16,128,128]{2,1,0:T(8,128)(2,1)S(1)} collective-permute-done((bf16[16,128,128]{2,1,0:T(8,128)(2,1)S(1)}, bf16[16,128,128]{2,1,0:T(8,128)(2,1)S(1)}, u32[]{:S(2)}, u32[]{:S(2)}) %collective-permute-start.7) | collective-permute-done | bytes 524320 | tf_op jit(solution)/shard_map/ppermute | solution.py:96
  266.3 4.9 %collective-permute-start.4 = (bf16[16,128,128]{2,1,0:T(8,128)(2,1)S(1)}, bf16[16,128,128]{2,1,0:T(8,128)(2,1)S(1)}, u32[]{:S(2)}, u32[]{:S(2)}) collective-permute-start(bf16[16,128,128]{2,1,0:T(8,128)(2,1)S(1)} %add_convert_fusion.3), channel_id=1, source_target_pairs={{0,128},{8,136},{16,144},{24,152},{32,160},{40,168},{48,176},{56,1... | collective-permute-start | bytes 1572872 | tf_op jit(solution)/shard_map/ppermute | solution.py:95
  271.2 10.1 %collective-permute-done.8 = bf16[16,128,128]{2,1,0:T(8,128)(2,1)S(1)} collective-permute-done((bf16[16,128,128]{2,1,0:T(8,128)(2,1)S(1)}, bf16[16,128,128]{2,1,0:T(8,128)(2,1)S(1)}, u32[]{:S(2)}, u32[]{:S(2)}) %collective-permute-start.8) | collective-permute-done | bytes 524320 | tf_op jit(solution)/shard_map/ppermute | solution.py:96
  284.6 10.1 %collective-permute-done.9 = bf16[16,128,128]{2,1,0:T(8,128)(2,1)S(1)} collective-permute-done((bf16[16,128,128]{2,1,0:T(8,128)(2,1)S(1)}, bf16[16,128,128]{2,1,0:T(8,128)(2,1)S(1)}, u32[]{:S(2)}, u32[]{:S(2)}) %collective-permute-start.9) | collective-permute-done | bytes 524320 | tf_op jit(solution)/shard_map/ppermute | solution.py:96
  296.9 7.9 %convert_bitcast_fusion = bf16[2,32,88,8,128]{4,3,2,1,0:T(8,128)(2,1)} fusion(s32[32,2,32]{2,0,1:T(8,128)S(1)} %add_bitcast_fusion.1, bf16[32,2,32,768]{3,2,1,0:T(8,128)(2,1)} %all-to-all-done), kind=kOutput, calls=%fused_computation.4 | convolution fusion | flops 375128064 | bytes 14688256 | tf_op jit(solution)/shard_map/sxtc,sxcf->fxst/dot_general | solution.py:58
  304.8 30.4 %fusion.5 = bf16[704,2,2048]{2,0,1:T(8,128)(2,1)S(1)} fusion(bf16[4096,2048]{1,0:T(8,128)(2,1)} %bitcast.136, bf16[2,32,88,8,128]{4,3,2,1,0:T(8,128)(2,1)} %convert_bitcast_fusion), kind=kOutput, calls=%fused_computation.7 | convolution fusion | flops 23625203712 | bytes 34078720 | tf_op jit(solution)/shard_map/dot_general | solution.py:105
  335.2 3.0 copy.103
  340.9 2.2 convolution_bitcast_fusion.5
  343.1 1.7 convolution_bitcast_fusion.1
  344.9 1.8 convolution_bitcast_fusion.3
  346.6 1.8 fusion.21
  348.5 2.0 copy.87
  350.5 3.0 fusion.22
  353.6 2.1 copy.88
  355.7 3.3 fusion.19
  359.0 2.1 copy.89
  363.0 14.0 %reduce-scatter.4.cloned.1.call-done = bf16[88,4096]{1,0:T(8,128)(2,1)} async-done(((bf16[704,4096]{1,0:T(8,128)(2,1)}), bf16[88,4096]{1,0:T(8,128)(2,1)}) %reduce-scatter.4.cloned.1.call-update) | async-done | bytes 720912
  377.1 2.0 copy.130
  (72 shorter events, 23.8 us)
Async XLA Ops:
  7.2 297.6 %all-gather.2.cloned.1.call-start = ((), (), s32[]{:S(2)}) async-start(), calls=%async_computation.2 | async-start | bytes 17301504 | tf_op jit(solution)/shard_map/all_gather | solution.py:52
  22.6 11.6 %copy-start.7 = (bf16[1,128,2048]{2,1,0:T(8,128)(2,1)S(1)}, bf16[1,128,2048]{2,1,0:T(8,128)(2,1)}, u32[]{:S(2)}) copy-start(bf16[1,128,2048]{2,1,0:T(8,128)(2,1)} %param.8) | copy-start | bytes 1572868
  22.6 12.2 %copy-start.8 = (bf16[1,128,2048]{2,1,0:T(8,128)(2,1)S(1)}, bf16[1,128,2048]{2,1,0:T(8,128)(2,1)}, u32[]{:S(2)}) copy-start(bf16[1,128,2048]{2,1,0:T(8,128)(2,1)} %param.9) | copy-start | bytes 1572868
  22.6 272.5 %all-to-all-start = ((bf16[32,2,32,768]{3,2,1,0:T(8,128)(2,1)}), bf16[32,2,32,768]{3,2,1,0:T(8,128)(2,1)}, u32[]{:S(2)}, u32[]{:S(2)}) async-start(bf16[32,2,32,768]{3,2,1,0:T(8,128)(2,1)} %bitcast.15), calls=%async_computation | async-start | bytes 6291456 | tf_op jit(solution)/shard_map/all_to_all | solution.py:51
  34.2 5.5 %copy-start.6 = (bf16[1,128,2048]{2,1,0:T(8,128)(2,1)S(1)}, bf16[1,128,2048]{2,1,0:T(8,128)(2,1)}, u32[]{:S(2)}) copy-start(bf16[1,128,2048]{2,1,0:T(8,128)(2,1)} %param.10) | copy-start | bytes 1572868
  34.2 342.9 %reduce-scatter.4.cloned.1.call-start = ((), (), s32[]{:S(2)}) async-start(), calls=%async_computation.3 | async-start | bytes 6488064
  34.3 0.8 copy-start.1
  34.8 1.4 copy-start.3
  36.2 110.8 %collective-permute-start = (bf16[16,128,128]{2,1,0:T(8,128)(2,1)}, bf16[16,128,128]{2,1,0:T(8,128)(2,1)S(1)}, u32[]{:S(2)}, u32[]{:S(2)}) collective-permute-start(bf16[16,128,128]{2,1,0:T(8,128)(2,1)} %get-tuple-element.26), channel_id=1, source_target_pairs={{0,8},{8,16},{16,24},{24,32},{32,40},{40,48},{48,56},{56,64},{64,7... | collective-permute-start | bytes 1572872 | tf_op jit(solution)/shard_map/ppermute | solution.py:95
  42.5 109.0 %collective-permute-start.5 = (bf16[16,128,128]{2,1,0:T(8,128)(2,1)S(1)}, bf16[16,128,128]{2,1,0:T(8,128)(2,1)S(1)}, u32[]{:S(2)}, u32[]{:S(2)}) collective-permute-start(bf16[16,128,128]{2,1,0:T(8,128)(2,1)S(1)} %get-tuple-element.28), channel_id=1, source_target_pairs={{8,0},{16,8},{24,16},{32,24},{40,32},{48,40},{56,48},{64,56},{72,6... | collective-permute-start | bytes 1572872 | tf_op jit(solution)/shard_map/ppermute | solution.py:96
  147.2 37.7 %collective-permute-start.1 = (bf16[16,128,128]{2,1,0:T(8,128)(2,1)S(1)}, bf16[16,128,128]{2,1,0:T(8,128)(2,1)S(1)}, u32[]{:S(2)}, u32[]{:S(2)}) collective-permute-start(bf16[16,128,128]{2,1,0:T(8,128)(2,1)S(1)} %fusion.27), channel_id=1, source_target_pairs={{0,16},{8,24},{16,32},{24,40},{32,48},{40,56},{48,64},{56,72},{64,... | collective-permute-start | bytes 1572872 | tf_op jit(solution)/shard_map/ppermute | solution.py:95
  151.6 42.8 %collective-permute-start.6 = (bf16[16,128,128]{2,1,0:T(8,128)(2,1)S(1)}, bf16[16,128,128]{2,1,0:T(8,128)(2,1)S(1)}, u32[]{:S(2)}, u32[]{:S(2)}) collective-permute-start(bf16[16,128,128]{2,1,0:T(8,128)(2,1)S(1)} %fusion.28), channel_id=1, source_target_pairs={{16,0},{24,8},{32,16},{40,24},{48,32},{56,40},{64,48},{72,56},{80,... | collective-permute-start | bytes 1572872 | tf_op jit(solution)/shard_map/ppermute | solution.py:96
  185.1 42.3 %collective-permute-start.2 = (bf16[16,128,128]{2,1,0:T(8,128)(2,1)S(1)}, bf16[16,128,128]{2,1,0:T(8,128)(2,1)S(1)}, u32[]{:S(2)}, u32[]{:S(2)}) collective-permute-start(bf16[16,128,128]{2,1,0:T(8,128)(2,1)S(1)} %add_convert_fusion.5), channel_id=1, source_target_pairs={{0,32},{8,40},{16,48},{24,56},{32,64},{40,72},{48,80},{56,88},{64,... | collective-permute-start | bytes 1572872 | tf_op jit(solution)/shard_map/ppermute | solution.py:95
  194.6 69.7 %collective-permute-start.7 = (bf16[16,128,128]{2,1,0:T(8,128)(2,1)S(1)}, bf16[16,128,128]{2,1,0:T(8,128)(2,1)S(1)}, u32[]{:S(2)}, u32[]{:S(2)}) collective-permute-start(bf16[16,128,128]{2,1,0:T(8,128)(2,1)S(1)} %add_convert_fusion.2), channel_id=1, source_target_pairs={{32,0},{40,8},{48,16},{56,24},{64,32},{72,40},{80,48},{88,56},{96,... | collective-permute-start | bytes 1572872 | tf_op jit(solution)/shard_map/ppermute | solution.py:96
  227.7 38.2 %collective-permute-start.3 = (bf16[16,128,128]{2,1,0:T(8,128)(2,1)S(1)}, bf16[16,128,128]{2,1,0:T(8,128)(2,1)S(1)}, u32[]{:S(2)}, u32[]{:S(2)}) collective-permute-start(bf16[16,128,128]{2,1,0:T(8,128)(2,1)S(1)} %add_convert_fusion.4), channel_id=1, source_target_pairs={{0,64},{8,72},{16,80},{24,88},{32,96},{40,104},{48,112},{56,120},{... | collective-permute-start | bytes 1572872 | tf_op jit(solution)/shard_map/ppermute | solution.py:95
  264.6 16.8 %collective-permute-start.8 = (bf16[16,128,128]{2,1,0:T(8,128)(2,1)S(1)}, bf16[16,128,128]{2,1,0:T(8,128)(2,1)S(1)}, u32[]{:S(2)}, u32[]{:S(2)}) collective-permute-start(bf16[16,128,128]{2,1,0:T(8,128)(2,1)S(1)} %add_convert_fusion.1), channel_id=1, source_target_pairs={{64,0},{72,8},{80,16},{88,24},{96,32},{104,40},{112,48},{120,56},{... | collective-permute-start | bytes 1572872 | tf_op jit(solution)/shard_map/ppermute | solution.py:96
  266.3 17.0 %collective-permute-start.4 = (bf16[16,128,128]{2,1,0:T(8,128)(2,1)S(1)}, bf16[16,128,128]{2,1,0:T(8,128)(2,1)S(1)}, u32[]{:S(2)}, u32[]{:S(2)}) collective-permute-start(bf16[16,128,128]{2,1,0:T(8,128)(2,1)S(1)} %add_convert_fusion.3), channel_id=1, source_target_pairs={{0,128},{8,136},{16,144},{24,152},{32,160},{40,168},{48,176},{56,1... | collective-permute-start | bytes 1572872 | tf_op jit(solution)/shard_map/ppermute | solution.py:95
  281.8 12.9 %collective-permute-start.9 = (bf16[16,128,128]{2,1,0:T(8,128)(2,1)S(1)}, bf16[16,128,128]{2,1,0:T(8,128)(2,1)S(1)}, u32[]{:S(2)}, u32[]{:S(2)}) collective-permute-start(bf16[16,128,128]{2,1,0:T(8,128)(2,1)S(1)} %add_convert_fusion), channel_id=1, source_target_pairs={{128,0},{136,8},{144,16},{152,24},{160,32},{168,40},{176,48},{184,... | collective-permute-start | bytes 1572872 | tf_op jit(solution)/shard_map/ppermute | solution.py:96
  338.2 1.0 copy-start.2
  338.2 2.7 copy-start.4
  343.1 3.5 copy-start
  353.6 7.5 %copy-start.5 = (f32[128,16,128]{0,2,1:T(8,128)S(1)}, f32[128,16,128]{0,2,1:T(8,128)}, u32[]{:S(2)}) copy-start(f32[128,16,128]{0,2,1:T(8,128)} %convolution_bitcast_fusion.1) | copy-start | bytes 3145732
Sparse Core Ops, SparseCore 0:
  10.6 260.5 all-gather.1
  338.3 38.7 reduce-scatter.3

commit v9 on v8

--- a/solution.py
+++ b/solution.py
@@ -92,8 +92,14 @@
     while shift < seq_count:
         fwd_pairs = [(src, src + shift) for src in range(seq_count - shift)]
         bwd_pairs = [(src, src - shift) for src in range(shift, seq_count)]
-        fwd_arrived = lax.ppermute(fwd_window.astype(jnp.bfloat16), "seq", fwd_pairs)
-        bwd_arrived = lax.ppermute(bwd_window.astype(jnp.bfloat16), "seq", bwd_pairs)
+        fwd_sent = fwd_window.astype(jnp.bfloat16)
+        bwd_sent = bwd_window.astype(jnp.bfloat16)
+        if shift == 8:
+            token_weights, fwd_sent, bwd_sent = lax.optimization_barrier(
+                (token_weights, fwd_sent, bwd_sent)
+            )
+        fwd_arrived = lax.ppermute(fwd_sent, "seq", fwd_pairs)
+        bwd_arrived = lax.ppermute(bwd_sent, "seq", bwd_pairs)
         prefix_state = prefix_state + fwd_arrived.astype(jnp.float32)
         after_state = after_state + bwd_arrived.astype(jnp.float32)
         fwd_window = state_sum + prefix_state

time: 387 us -> 452 us (1.17)
  local copies, waits for them, and re-layouts: 23 us -> 83.1 us
  starting transfers between devices: 50.6 us -> 75.2 us
  waiting for transfers between devices: 228 us -> 206 us
    convert_element_type x0 -> x2, local copies, waits for them, and re-layouts: none -> 35.6 us  [the longest x1 25.4 us: per_device(): token_weights = jnp.einsum('sxtc,sxcf->fxst', token_pick, arrived_hidden,...]
    ppermute x10, waiting for transfers between devices: 213 us -> 181 us  [the longest x5 179 us: per_device(): bwd_arrived = lax.ppermute(bwd_sent, 'seq', bwd_pairs)]
    ppermute x10, starting transfers between devices: 38.9 us -> 63.5 us  [the longest x5 56 us: per_device(): fwd_arrived = lax.ppermute(fwd_sent, 'seq', fwd_pairs)]
    unnamed x30 -> x59, local copies, waits for them, and re-layouts: 16.6 us -> 39.5 us
    unnamed x3, waiting for transfers between devices: 14.7 us -> 25.5 us
  transfers between devices with their start and end apart: 13 -> 13, of which waited for: 7 -> 8; matrix products, arithmetic and copies ran while one was open for 15% -> 22% of each run, Pallas kernels for 0% -> 0%
where the time goes in v9:
time: 452 us; the launch traced here: 450 us
  waiting for transfers between devices  206 us (46%)
  local copies, waits for them, and re-layouts  83.1 us (18%)
  starting transfers between devices  75.2 us (17%)
  matrix products  61.6 us (14%)
  between operations  14.6 us (3%)
  other arithmetic  9.43 us (2%)
    ppermute x5, waiting for transfers between devices, per_device(): bwd_arrived = lax.ppermute(bwd_sent, 'seq', bwd_pairs)  179 us
    ppermute x5, starting transfers between devices, per_device(): fwd_arrived = lax.ppermute(fwd_sent, 'seq', fwd_pairs)  56 us
    unnamed x59, local copies, waits for them, and re-layouts  39.5 us
    dot_general x1, matrix products, per_device(): jnp.dot(token_weights, all_cotangent, preferred_element_type=jnp.float32)  31.4 us
    unnamed x3, waiting for transfers between devices  25.5 us
    convert_element_type x1, local copies, waits for them, and re-layouts, per_device(): token_weights = jnp.einsum('sxtc,sxcf->fxst', token_pick, arrived_hidden,...  25.4 us
    all_to_all x1, starting transfers between devices, per_device(): lax.all_to_all(hidden_slots, 'seq', split_axis=0, concat_axis=0, tiled=True)  11.5 us
    convert_element_type x1, local copies, waits for them, and re-layouts, per_device(): group_term.astype(jnp.bfloat16)  10.2 us
  transfers between devices with their start and end apart: 13, of which 8 were waited for; matrix products, arithmetic and copies ran while one was open for 22% of the time, Pallas kernels for 0%

profile of v9, /device:TPU:32, one launch (start us, length us, event | category | flops | bytes accessed | tf_op | source)
XLA Modules:
  0.0 450.2 jit_solution(11235588941327033525)
XLA Ops:
  11.1 2.0 copy.74
  15.4 1.9 multiply_convert_fusion
  17.2 4.8 %fusion.1 = bf16[2048,768]{1,0:T(8,128)(2,1)} fusion(s32[768]{0:T(1024)S(1)} %multiply_add_fusion, bf16[768,1]{1,0:T(8,128)(2,1)S(1)} %fusion.33, bf16[768,704]{1,0:T(8,128)(2,1)S(1)} %multiply_convert_fusion, bf16[768]{0:T(1024)(128)(2,1)S(1)} %pad.2.clone), kind=kOutput, calls=%fused_computation.5 | convolution fusion | flops 2422603776 | bytes 4233216 | tf_op jit(solution)/shard_map/dot_general | solution.py:47
  22.0 11.5 %all-to-all-start = ((bf16[32,2,32,768]{3,2,1,0:T(8,128)(2,1)}), bf16[32,2,32,768]{3,2,1,0:T(8,128)(2,1)}, u32[]{:S(2)}, u32[]{:S(2)}) async-start(bf16[32,2,32,768]{3,2,1,0:T(8,128)(2,1)} %bitcast.4), calls=%async_computation | async-start | bytes 6291456 | tf_op jit(solution)/shard_map/all_to_all | solution.py:51
  34.2 2.0 fusion.49
  36.2 2.2 collective-permute-start.3
  43.4 3.6 collective-permute-start
  47.0 96.6 %collective-permute-done.3 = bf16[16,128,128]{2,1,0:T(8,128)(2,1)S(1)} collective-permute-done((bf16[16,128,128]{2,1,0:T(8,128)(2,1)}, bf16[16,128,128]{2,1,0:T(8,128)(2,1)S(1)}, u32[]{:S(2)}, u32[]{:S(2)}) %collective-permute-start.3) | collective-permute-done | bytes 524320 | tf_op jit(solution)/shard_map/ppermute | solution.py:102
  146.7 4.4 collective-permute-start.1
  151.2 32.2 %collective-permute-done.4 = bf16[16,128,128]{2,1,0:T(8,128)(2,1)S(1)} collective-permute-done((bf16[16,128,128]{2,1,0:T(8,128)(2,1)S(1)}, bf16[16,128,128]{2,1,0:T(8,128)(2,1)S(1)}, u32[]{:S(2)}, u32[]{:S(2)}) %collective-permute-start.4) | collective-permute-done | bytes 524320 | tf_op jit(solution)/shard_map/ppermute | solution.py:102
  185.2 9.7 %collective-permute-start.2 = (bf16[16,128,128]{2,1,0:T(8,128)(2,1)S(1)}, bf16[16,128,128]{2,1,0:T(8,128)(2,1)S(1)}, u32[]{:S(2)}, u32[]{:S(2)}) collective-permute-start(bf16[16,128,128]{2,1,0:T(8,128)(2,1)S(1)} %add_convert_fusion.5), channel_id=1, source_target_pairs={{0,32},{8,40},{16,48},{24,56},{32,64},{40,72},{48,80},{56,88},{64,... | collective-permute-start | bytes 1572872 | tf_op jit(solution)/shard_map/ppermute | solution.py:101
  194.8 35.4 %collective-permute-done.5 = bf16[16,128,128]{2,1,0:T(8,128)(2,1)S(1)} collective-permute-done((bf16[16,128,128]{2,1,0:T(8,128)(2,1)S(1)}, bf16[16,128,128]{2,1,0:T(8,128)(2,1)S(1)}, u32[]{:S(2)}, u32[]{:S(2)}) %collective-permute-start.5) | collective-permute-done | bytes 524320 | tf_op jit(solution)/shard_map/ppermute | solution.py:102
  233.2 2.1 slice.18
  236.8 5.4 %convert_bitcast_fusion = bf16[704,2,32,128]{3,0,2,1:T(8,128)(2,1)S(1)} fusion(s32[32,2,32]{2,0,1:T(8,128)S(1)} %add_bitcast_fusion.1, bf16[32,2,32,768]{3,2,1,0:T(8,128)(2,1)} %all-to-all-done), kind=kOutput, calls=%fused_computation.1 | convolution fusion | flops 375128064 | bytes 14688256 | tf_op jit(solution)/shard_map/sxtc,sxcf->fxst/dot_general | solution.py:58
  242.2 25.4 %copy.77 = bf16[704,2,32,128]{3,2,1,0:T(8,128)(2,1)S(1)} copy(bf16[704,2,32,128]{3,0,2,1:T(8,128)(2,1)S(1)} %convert_bitcast_fusion) | data formatting | bytes 23068672 | tf_op jit(solution)/shard_map/convert_element_type | solution.py:60
  267.6 16.8 %copy.128 = bf16[176,8,32,128]{3,1,2,0:T(8,128)(2,1)} copy(bf16[176,8,32,128]{3,2,1,0:T(8,128)(2,1)S(1)} %bitcast.106) | data formatting | bytes 23068672
  285.9 32.2 %collective-permute-start.6 = (bf16[16,128,128]{2,1,0:T(8,128)(2,1)S(1)}, bf16[16,128,128]{2,1,0:T(8,128)(2,1)S(1)}, u32[]{:S(2)}, u32[]{:S(2)}) collective-permute-start(bf16[16,128,128]{2,1,0:T(8,128)(2,1)S(1)} %copy-done.20), channel_id=1, source_target_pairs={{0,64},{8,72},{16,80},{24,88},{32,96},{40,104},{48,112},{56,120},{... | collective-permute-start | bytes 1572872 | tf_op jit(solution)/shard_map/ppermute | solution.py:101
  318.1 7.6 %collective-permute-done.8 = bf16[16,128,128]{2,1,0:T(8,128)(2,1)S(1)} collective-permute-done((bf16[16,128,128]{2,1,0:T(8,128)(2,1)S(1)}, bf16[16,128,128]{2,1,0:T(8,128)(2,1)S(1)}, u32[]{:S(2)}, u32[]{:S(2)}) %collective-permute-start.8) | collective-permute-done | bytes 524320 | tf_op jit(solution)/shard_map/ppermute | solution.py:102
  327.9 6.1 %collective-permute-start.7 = (bf16[16,128,128]{2,1,0:T(8,128)(2,1)S(1)}, bf16[16,128,128]{2,1,0:T(8,128)(2,1)S(1)}, u32[]{:S(2)}, u32[]{:S(2)}) collective-permute-start(bf16[16,128,128]{2,1,0:T(8,128)(2,1)S(1)} %add_convert_fusion.1), channel_id=1, source_target_pairs={{0,128},{8,136},{16,144},{24,152},{32,160},{40,168},{48,176},{56,1... | collective-permute-start | bytes 1572872 | tf_op jit(solution)/shard_map/ppermute | solution.py:101
  334.0 6.8 %collective-permute-done.9 = bf16[16,128,128]{2,1,0:T(8,128)(2,1)S(1)} collective-permute-done((bf16[16,128,128]{2,1,0:T(8,128)(2,1)S(1)}, bf16[16,128,128]{2,1,0:T(8,128)(2,1)S(1)}, u32[]{:S(2)}, u32[]{:S(2)}) %collective-permute-start.9) | collective-permute-done | bytes 524320 | tf_op jit(solution)/shard_map/ppermute | solution.py:102
  343.3 31.4 %convolution_convert_fusion = bf16[1408,2048]{1,0:T(8,128)(2,1)} fusion(bf16[1408,4096]{1,0:T(8,128)(2,1)} %bitcast.121, bf16[4096,2048]{1,0:T(8,128)(2,1)} %bitcast.134), kind=kOutput, calls=%fused_computation.2 | convolution fusion | flops 23625203712 | bytes 34078720 | tf_op jit(solution)/shard_map/dot_general | solution.py:111
  374.7 10.2 %convert_element_type.227 = bf16[704,2,2048]{2,1,0:T(2,128)(2,1)} reshape(bf16[1408,2048]{1,0:T(8,128)(2,1)} %convolution_convert_fusion) | data formatting | bytes 11534336 | tf_op jit(solution)/shard_map/convert_element_type | solution.py:126
  384.9 8.8 %copy.108 = bf16[88,8,2,2048]{3,1,2,0:T(8,128)(2,1)} copy(bf16[88,8,2,2048]{3,2,1,0:T(2,128)(2,1)} %bitcast.108) | data formatting | bytes 11534336
  395.8 2.2 convolution_bitcast_fusion.5
  398.0 2.2 convolution_bitcast_fusion.7
  402.7 2.0 fusion.10
  404.7 2.0 copy.92
  406.8 2.2 fusion.11
  410.0 2.2 fusion.13
  413.3 2.2 fusion.12
  416.5 24.8 %reduce-scatter.4.cloned.1.call-done = bf16[88,4096]{1,0:T(8,128)(2,1)} async-done(((bf16[704,4096]{1,0:T(8,128)(2,1)}), bf16[88,4096]{1,0:T(8,128)(2,1)}) %reduce-scatter.4.cloned.1.call-update) | async-done | bytes 720912
  441.3 2.0 copy.129
  (103 shorter events, 34.5 us)
Async XLA Ops:
  7.2 336.1 %all-gather.2.cloned.1.call-start = ((), (), s32[]{:S(2)}) async-start(), calls=%async_computation.2 | async-start | bytes 17301504 | tf_op jit(solution)/shard_map/all_gather | solution.py:52
  13.1 1.6 copy-start.22
  22.0 11.6 %copy-start.18 = (bf16[1,128,2048]{2,1,0:T(8,128)(2,1)S(1)}, bf16[1,128,2048]{2,1,0:T(8,128)(2,1)}, u32[]{:S(2)}) copy-start(bf16[1,128,2048]{2,1,0:T(8,128)(2,1)} %param.10) | copy-start | bytes 1572868
  22.0 11.9 %copy-start.19 = (bf16[1,128,2048]{2,1,0:T(8,128)(2,1)S(1)}, bf16[1,128,2048]{2,1,0:T(8,128)(2,1)}, u32[]{:S(2)}) copy-start(bf16[1,128,2048]{2,1,0:T(8,128)(2,1)} %param.7) | copy-start | bytes 1572868
  22.0 211.2 %all-to-all-start = ((bf16[32,2,32,768]{3,2,1,0:T(8,128)(2,1)}), bf16[32,2,32,768]{3,2,1,0:T(8,128)(2,1)}, u32[]{:S(2)}, u32[]{:S(2)}) async-start(bf16[32,2,32,768]{3,2,1,0:T(8,128)(2,1)} %bitcast.4), calls=%async_computation | async-start | bytes 6291456 | tf_op jit(solution)/shard_map/all_to_all | solution.py:51
  33.6 407.8 %reduce-scatter.4.cloned.1.call-start = ((), (), s32[]{:S(2)}) async-start(), calls=%async_computation.3 | async-start | bytes 6488064
  33.9 8.1 %copy-start.2 = (bf16[1,128,2048]{1,2,0:T(8,128)(2,1)}, bf16[1,128,2048]{1,2,0:T(8,128)(2,1)S(1)}, u32[]{:S(2)}) copy-start(bf16[1,128,2048]{1,2,0:T(8,128)(2,1)S(1)} %copy.102) | copy-start | bytes 1572868
  34.2 7.8 %copy-start.4 = (bf16[1,128,2048]{1,2,0:T(8,128)(2,1)}, bf16[1,128,2048]{1,2,0:T(8,128)(2,1)S(1)}, u32[]{:S(2)}) copy-start(bf16[1,128,2048]{1,2,0:T(8,128)(2,1)S(1)} %copy.64) | copy-start | bytes 1572868
  36.2 107.4 %collective-permute-start.3 = (bf16[16,128,128]{2,1,0:T(8,128)(2,1)}, bf16[16,128,128]{2,1,0:T(8,128)(2,1)S(1)}, u32[]{:S(2)}, u32[]{:S(2)}) collective-permute-start(bf16[16,128,128]{2,1,0:T(8,128)(2,1)} %get-tuple-element.34), channel_id=1, source_target_pairs={{8,0},{16,8},{24,16},{32,24},{40,32},{48,40},{56,48},{64,56},{72,6... | collective-permute-start | bytes 1572872 | tf_op jit(solution)/shard_map/ppermute | solution.py:102
  43.4 103.2 %collective-permute-start = (bf16[16,128,128]{2,1,0:T(8,128)(2,1)S(1)}, bf16[16,128,128]{2,1,0:T(8,128)(2,1)S(1)}, u32[]{:S(2)}, u32[]{:S(2)}) collective-permute-start(bf16[16,128,128]{2,1,0:T(8,128)(2,1)S(1)} %get-tuple-element.32), channel_id=1, source_target_pairs={{0,8},{8,16},{16,24},{24,32},{32,40},{40,48},{48,56},{56,64},{64,7... | collective-permute-start | bytes 1572872 | tf_op jit(solution)/shard_map/ppermute | solution.py:101
  143.7 39.7 %collective-permute-start.4 = (bf16[16,128,128]{2,1,0:T(8,128)(2,1)S(1)}, bf16[16,128,128]{2,1,0:T(8,128)(2,1)S(1)}, u32[]{:S(2)}, u32[]{:S(2)}) collective-permute-start(bf16[16,128,128]{2,1,0:T(8,128)(2,1)S(1)} %fusion.19), channel_id=1, source_target_pairs={{16,0},{24,8},{32,16},{40,24},{48,32},{56,40},{64,48},{72,56},{80,... | collective-permute-start | bytes 1572872 | tf_op jit(solution)/shard_map/ppermute | solution.py:102
  146.6 84.7 %copy-start = (bf16[16,128,128]{2,1,0:T(8,128)(2,1)}, bf16[16,128,128]{2,1,0:T(8,128)(2,1)S(1)}, u32[]{:S(2)}) copy-start(bf16[16,128,128]{2,1,0:T(8,128)(2,1)S(1)} %collective-permute-done) | copy-start | bytes 1572868
  146.7 38.2 %collective-permute-start.1 = (bf16[16,128,128]{2,1,0:T(8,128)(2,1)S(1)}, bf16[16,128,128]{2,1,0:T(8,128)(2,1)S(1)}, u32[]{:S(2)}, u32[]{:S(2)}) collective-permute-start(bf16[16,128,128]{2,1,0:T(8,128)(2,1)S(1)} %fusion.18), channel_id=1, source_target_pairs={{0,16},{8,24},{16,32},{24,40},{32,48},{40,56},{48,64},{56,72},{64,... | collective-permute-start | bytes 1572872 | tf_op jit(solution)/shard_map/ppermute | solution.py:101
  183.4 47.9 %copy-start.7 = (bf16[16,128,128]{2,1,0:T(8,128)(2,1)}, bf16[16,128,128]{2,1,0:T(8,128)(2,1)S(1)}, u32[]{:S(2)}) copy-start(bf16[16,128,128]{2,1,0:T(8,128)(2,1)S(1)} %collective-permute-done.4) | copy-start | bytes 1572868
  183.6 46.6 %collective-permute-start.5 = (bf16[16,128,128]{2,1,0:T(8,128)(2,1)S(1)}, bf16[16,128,128]{2,1,0:T(8,128)(2,1)S(1)}, u32[]{:S(2)}, u32[]{:S(2)}) collective-permute-start(bf16[16,128,128]{2,1,0:T(8,128)(2,1)S(1)} %add_convert_fusion.3), channel_id=1, source_target_pairs={{32,0},{40,8},{48,16},{56,24},{64,32},{72,40},{80,48},{88,56},{96,... | collective-permute-start | bytes 1572872 | tf_op jit(solution)/shard_map/ppermute | solution.py:102
  184.9 46.4 %copy-start.9 = (bf16[16,128,128]{2,1,0:T(8,128)(2,1)}, bf16[16,128,128]{2,1,0:T(8,128)(2,1)S(1)}, u32[]{:S(2)}) copy-start(bf16[16,128,128]{2,1,0:T(8,128)(2,1)S(1)} %collective-permute-done.1) | copy-start | bytes 1572868
  185.2 46.1 %collective-permute-start.2 = (bf16[16,128,128]{2,1,0:T(8,128)(2,1)S(1)}, bf16[16,128,128]{2,1,0:T(8,128)(2,1)S(1)}, u32[]{:S(2)}, u32[]{:S(2)}) collective-permute-start(bf16[16,128,128]{2,1,0:T(8,128)(2,1)S(1)} %add_convert_fusion.5), channel_id=1, source_target_pairs={{0,32},{8,40},{16,48},{24,56},{32,64},{40,72},{48,80},{56,88},{64,... | collective-permute-start | bytes 1572872 | tf_op jit(solution)/shard_map/ppermute | solution.py:101
  267.6 16.9 %copy-start.21 = (bf16[16,128,128]{2,1,0:T(8,128)(2,1)S(1)}, bf16[16,128,128]{2,1,0:T(8,128)(2,1)}, u32[]{:S(2)}) copy-start(bf16[16,128,128]{2,1,0:T(8,128)(2,1)} %add_convert_fusion.2) | copy-start | bytes 1572868
  267.6 18.3 %copy-start.20 = (bf16[16,128,128]{2,1,0:T(8,128)(2,1)S(1)}, bf16[16,128,128]{2,1,0:T(8,128)(2,1)}, u32[]{:S(2)}) copy-start(bf16[16,128,128]{2,1,0:T(8,128)(2,1)} %add_convert_fusion.4) | copy-start | bytes 1572868
  267.6 58.1 %copy-start.8 = (bf16[16,128,128]{2,1,0:T(8,128)(2,1)S(1)}, bf16[16,128,128]{2,1,0:T(8,128)(2,1)}, u32[]{:S(2)}) copy-start(bf16[16,128,128]{2,1,0:T(8,128)(2,1)} %copy-done.7) | copy-start | bytes 1572868
  267.6 58.1 %copy-start.17 = (bf16[16,128,128]{2,1,0:T(8,128)(2,1)S(1)}, bf16[16,128,128]{2,1,0:T(8,128)(2,1)}, u32[]{:S(2)}) copy-start(bf16[16,128,128]{2,1,0:T(8,128)(2,1)} %copy-done.16) | copy-start | bytes 1572868
  284.5 43.0 %copy-start.1 = (bf16[16,128,128]{2,1,0:T(8,128)(2,1)S(1)}, bf16[16,128,128]{2,1,0:T(8,128)(2,1)}, u32[]{:S(2)}) copy-start(bf16[16,128,128]{2,1,0:T(8,128)(2,1)} %copy-done) | copy-start | bytes 1572868
  284.5 43.0 %copy-start.10 = (bf16[16,128,128]{2,1,0:T(8,128)(2,1)S(1)}, bf16[16,128,128]{2,1,0:T(8,128)(2,1)}, u32[]{:S(2)}) copy-start(bf16[16,128,128]{2,1,0:T(8,128)(2,1)} %copy-done.9) | copy-start | bytes 1572868
  284.5 43.0 %copy-start.15 = (bf16[16,128,128]{2,1,0:T(8,128)(2,1)S(1)}, bf16[16,128,128]{2,1,0:T(8,128)(2,1)}, u32[]{:S(2)}) copy-start(bf16[16,128,128]{2,1,0:T(8,128)(2,1)} %copy-done.14) | copy-start | bytes 1572868
  284.5 41.3 %collective-permute-start.8 = (bf16[16,128,128]{2,1,0:T(8,128)(2,1)S(1)}, bf16[16,128,128]{2,1,0:T(8,128)(2,1)S(1)}, u32[]{:S(2)}, u32[]{:S(2)}) collective-permute-start(bf16[16,128,128]{2,1,0:T(8,128)(2,1)S(1)} %copy-done.21), channel_id=1, source_target_pairs={{64,0},{72,8},{80,16},{88,24},{96,32},{104,40},{112,48},{120,56},{... | collective-permute-start | bytes 1572872 | tf_op jit(solution)/shard_map/ppermute | solution.py:102
  285.9 41.5 %collective-permute-start.6 = (bf16[16,128,128]{2,1,0:T(8,128)(2,1)S(1)}, bf16[16,128,128]{2,1,0:T(8,128)(2,1)S(1)}, u32[]{:S(2)}, u32[]{:S(2)}) collective-permute-start(bf16[16,128,128]{2,1,0:T(8,128)(2,1)S(1)} %copy-done.20), channel_id=1, source_target_pairs={{0,64},{8,72},{16,80},{24,88},{32,96},{40,104},{48,112},{56,120},{... | collective-permute-start | bytes 1572872 | tf_op jit(solution)/shard_map/ppermute | solution.py:101
  326.1 14.7 %collective-permute-start.9 = (bf16[16,128,128]{2,1,0:T(8,128)(2,1)S(1)}, bf16[16,128,128]{2,1,0:T(8,128)(2,1)S(1)}, u32[]{:S(2)}, u32[]{:S(2)}) collective-permute-start(bf16[16,128,128]{2,1,0:T(8,128)(2,1)S(1)} %add_convert_fusion), channel_id=1, source_target_pairs={{128,0},{136,8},{144,16},{152,24},{160,32},{168,40},{176,48},{184,... | collective-permute-start | bytes 1572872 | tf_op jit(solution)/shard_map/ppermute | solution.py:102
  327.9 14.0 %collective-permute-start.7 = (bf16[16,128,128]{2,1,0:T(8,128)(2,1)S(1)}, bf16[16,128,128]{2,1,0:T(8,128)(2,1)S(1)}, u32[]{:S(2)}, u32[]{:S(2)}) collective-permute-start(bf16[16,128,128]{2,1,0:T(8,128)(2,1)S(1)} %add_convert_fusion.1), channel_id=1, source_target_pairs={{0,128},{8,136},{16,144},{24,152},{32,160},{40,168},{48,176},{56,1... | collective-permute-start | bytes 1572872 | tf_op jit(solution)/shard_map/ppermute | solution.py:101
  393.7 1.6 copy-start.5
  393.7 1.6 copy-start.12
  393.7 2.1 copy-start.13
  409.0 4.2 copy-start.6
  (4 other events, 4.2 us)
Sparse Core Ops, SparseCore 0:
  10.6 260.4 all-gather.1
  393.8 47.4 reduce-scatter.3

commit v10 on v8

--- a/solution.py
+++ b/solution.py
@@ -94,14 +94,15 @@
         bwd_pairs = [(src, src - shift) for src in range(shift, seq_count)]
         fwd_arrived = lax.ppermute(fwd_window.astype(jnp.bfloat16), "seq", fwd_pairs)
         bwd_arrived = lax.ppermute(bwd_window.astype(jnp.bfloat16), "seq", bwd_pairs)
+        if 2 * shift == seq_count // 2:
+            all_cotangent, fwd_arrived, bwd_arrived = lax.optimization_barrier(
+                (all_cotangent, fwd_arrived, bwd_arrived)
+            )
         prefix_state = prefix_state + fwd_arrived.astype(jnp.float32)
         after_state = after_state + bwd_arrived.astype(jnp.float32)
         fwd_window = state_sum + prefix_state
         bwd_window = grad_sum + after_state
         shift *= 2
-    all_cotangent, prefix_state, after_state = lax.optimization_barrier(
-        (all_cotangent, prefix_state, after_state)
-    )
     group_term = jnp.dot(
         token_weights, all_cotangent, preferred_element_type=jnp.float32
     ).reshape(hidden_units, EXP_DEV, width)

time: 387 us -> 365 us (0.943)
  waiting for transfers between devices: 228 us -> 198 us
  matrix products: 62.4 us -> 68.7 us
    ppermute x5, waiting for transfers between devices: 47.5 us -> 29.1 us  [per_device(): lax.ppermute(bwd_window.astype(jnp.bfloat16), 'seq', bwd_pairs)]
    unnamed x3, waiting for transfers between devices: 14.7 us -> 0.7 us
    unnamed x30 -> x66, local copies, waits for them, and re-layouts: 16.6 us -> 15.3 us
  transfers between devices with their start and end apart: 13 -> 13, of which waited for: 7 -> 7; matrix products, arithmetic and copies ran while one was open for 15% -> 18% of each run, Pallas kernels for 0% -> 0%
where the time goes in v10:
time: 365 us; the launch traced here: 364 us
  waiting for transfers between devices  198 us (54%)
  matrix products  68.7 us (19%)
  starting transfers between devices  50 us (14%)
  local copies, waits for them, and re-layouts  22.5 us (6%)
  between operations  14.5 us (4%)
  other arithmetic  10.5 us (3%)
    ppermute x5, waiting for transfers between devices, per_device(): lax.ppermute(fwd_window.astype(jnp.bfloat16), 'seq', fwd_pairs)  168 us
    ppermute x5, starting transfers between devices, per_device(): lax.ppermute(fwd_window.astype(jnp.bfloat16), 'seq', fwd_pairs)  30.2 us
    dot_general x1, matrix products, per_device(): jnp.dot(token_weights, all_cotangent, preferred_element_type=jnp.float32)  30.2 us
    ppermute x5, waiting for transfers between devices, per_device(): lax.ppermute(bwd_window.astype(jnp.bfloat16), 'seq', bwd_pairs)  29.1 us
    unnamed x66, local copies, waits for them, and re-layouts  15.3 us
    all_to_all x1, starting transfers between devices, per_device(): lax.all_to_all(hidden_slots, 'seq', split_axis=0, concat_axis=0, tiled=True)  11.5 us
    ppermute x5, starting transfers between devices, per_device(): lax.ppermute(bwd_window.astype(jnp.bfloat16), 'seq', bwd_pairs)  8.18 us
    dot_general x1, matrix products, per_device(): jnp.einsum('sxtc,sxcf->fxst', token_pick, arrived_hidden, preferred_eleme...  7.9 us
  transfers between devices with their start and end apart: 13, of which 7 were waited for; matrix products, arithmetic and copies ran while one was open for 18% of the time, Pallas kernels for 0%

profile of v10, /device:TPU:32, one launch (start us, length us, event | category | flops | bytes accessed | tf_op | source)
XLA Modules:
  0.0 364.0 jit_solution(9282743357650406712)
XLA Ops:
  9.9 1.8 reduce-window.6
  12.0 2.0 copy.83
  16.0 1.9 multiply_convert_fusion
  17.9 4.7 %fusion.10 = bf16[2048,768]{1,0:T(8,128)(2,1)} fusion(s32[768]{0:T(1024)S(1)} %multiply_add_fusion, bf16[768,1]{1,0:T(8,128)(2,1)S(1)} %fusion.42, bf16[768,704]{1,0:T(8,128)(2,1)S(1)} %multiply_convert_fusion, bf16[768]{0:T(1024)(128)(2,1)S(1)} %pad.2.clone), kind=kOutput, calls=%fused_computation.8 | convolution fusion | flops 2422603776 | bytes 4233216 | tf_op jit(solution)/shard_map/dot_general | solution.py:47
  22.6 11.5 %all-to-all-start = ((bf16[32,2,32,768]{3,2,1,0:T(8,128)(2,1)}), bf16[32,2,32,768]{3,2,1,0:T(8,128)(2,1)}, u32[]{:S(2)}, u32[]{:S(2)}) async-start(bf16[32,2,32,768]{3,2,1,0:T(8,128)(2,1)} %bitcast.15), calls=%async_computation | async-start | bytes 6291456 | tf_op jit(solution)/shard_map/all_to_all | solution.py:51
  36.1 3.4 collective-permute-start
  40.8 2.2 fusion.58
  43.1 2.5 collective-permute-start.4
  45.6 101.5 %collective-permute-done = bf16[16,128,128]{2,1,0:T(8,128)(2,1)S(1)} collective-permute-done((bf16[16,128,128]{2,1,0:T(8,128)(2,1)}, bf16[16,128,128]{2,1,0:T(8,128)(2,1)S(1)}, u32[]{:S(2)}, u32[]{:S(2)}) %collective-permute-start) | collective-permute-done | bytes 524320 | tf_op jit(solution)/shard_map/ppermute | solution.py:95
  147.2 4.2 %collective-permute-start.1 = (bf16[16,128,128]{2,1,0:T(8,128)(2,1)S(1)}, bf16[16,128,128]{2,1,0:T(8,128)(2,1)S(1)}, u32[]{:S(2)}, u32[]{:S(2)}) collective-permute-start(bf16[16,128,128]{2,1,0:T(8,128)(2,1)S(1)} %fusion.27), channel_id=1, source_target_pairs={{0,16},{8,24},{16,32},{24,40},{32,48},{40,56},{48,64},{56,72},{64,... | collective-permute-start | bytes 1572872 | tf_op jit(solution)/shard_map/ppermute | solution.py:95
  152.9 32.0 %collective-permute-done.1 = bf16[16,128,128]{2,1,0:T(8,128)(2,1)S(1)} collective-permute-done((bf16[16,128,128]{2,1,0:T(8,128)(2,1)S(1)}, bf16[16,128,128]{2,1,0:T(8,128)(2,1)S(1)}, u32[]{:S(2)}, u32[]{:S(2)}) %collective-permute-start.1) | collective-permute-done | bytes 524320 | tf_op jit(solution)/shard_map/ppermute | solution.py:95
  185.1 9.3 %collective-permute-start.2 = (bf16[16,128,128]{2,1,0:T(8,128)(2,1)S(1)}, bf16[16,128,128]{2,1,0:T(8,128)(2,1)S(1)}, u32[]{:S(2)}, u32[]{:S(2)}) collective-permute-start(bf16[16,128,128]{2,1,0:T(8,128)(2,1)S(1)} %add_convert_fusion.5), channel_id=1, source_target_pairs={{0,32},{8,40},{16,48},{24,56},{32,64},{40,72},{48,80},{56,88},{64,... | collective-permute-start | bytes 1572872 | tf_op jit(solution)/shard_map/ppermute | solution.py:95
  195.9 31.5 %collective-permute-done.2 = bf16[16,128,128]{2,1,0:T(8,128)(2,1)S(1)} collective-permute-done((bf16[16,128,128]{2,1,0:T(8,128)(2,1)S(1)}, bf16[16,128,128]{2,1,0:T(8,128)(2,1)S(1)}, u32[]{:S(2)}, u32[]{:S(2)}) %collective-permute-start.2) | collective-permute-done | bytes 524320 | tf_op jit(solution)/shard_map/ppermute | solution.py:95
  228.5 10.1 %collective-permute-start.3 = (bf16[16,128,128]{2,1,0:T(8,128)(2,1)}, bf16[16,128,128]{2,1,0:T(8,128)(2,1)}, u32[]{:S(2)}, u32[]{:S(2)}) collective-permute-start(bf16[16,128,128]{2,1,0:T(8,128)(2,1)} %add_convert_fusion.4), channel_id=1, source_target_pairs={{0,64},{8,72},{16,80},{24,88},{32,96},{40,104},{48,112},{56,120},{... | collective-permute-start | bytes 1572872 | tf_op jit(solution)/shard_map/ppermute | solution.py:95
  238.6 25.7 %collective-permute-done.6 = bf16[16,128,128]{2,1,0:T(8,128)(2,1)S(1)} collective-permute-done((bf16[16,128,128]{2,1,0:T(8,128)(2,1)S(1)}, bf16[16,128,128]{2,1,0:T(8,128)(2,1)S(1)}, u32[]{:S(2)}, u32[]{:S(2)}) %collective-permute-start.6) | collective-permute-done | bytes 524320 | tf_op jit(solution)/shard_map/ppermute | solution.py:96
  267.7 2.1 slice.18
  271.3 7.9 %convert_bitcast_fusion = bf16[2,32,88,8,128]{4,3,2,1,0:T(8,128)(2,1)} fusion(s32[32,2,32]{2,0,1:T(8,128)S(1)} %add_bitcast_fusion.1, bf16[32,2,32,768]{3,2,1,0:T(8,128)(2,1)} %all-to-all-done), kind=kOutput, calls=%fused_computation.4 | convolution fusion | flops 375128064 | bytes 14688256 | tf_op jit(solution)/shard_map/sxtc,sxcf->fxst/dot_general | solution.py:58
  279.2 1.9 collective-permute-done.7
  281.1 30.2 %fusion.5 = bf16[704,2,2048]{2,0,1:T(8,128)(2,1)S(1)} fusion(bf16[4096,2048]{1,0:T(8,128)(2,1)} %bitcast.132, bf16[2,32,88,8,128]{4,3,2,1,0:T(8,128)(2,1)} %convert_bitcast_fusion), kind=kOutput, calls=%fused_computation.7 | convolution fusion | flops 23625203712 | bytes 34078720 | tf_op jit(solution)/shard_map/dot_general | solution.py:106
  311.2 3.0 copy.103
  314.3 1.8 convolution_multiply_fusion
  319.1 1.8 convolution_bitcast_fusion.1
  324.1 3.2 collective-permute-start.8
  327.3 2.3 convolution_bitcast_fusion.5
  329.6 2.2 add_convert_fusion
  333.5 3.0 collective-permute-done.8
  336.5 2.4 fusion.21
  340.0 3.6 fusion.22
  343.5 2.1 copy.88
  347.1 3.1 fusion.19
  351.3 2.8 fusion.20
  355.1 2.0 copy.130
  (106 shorter events, 29.7 us)
Async XLA Ops:
  7.2 273.9 %all-gather.2.cloned.1.call-start = ((), (), s32[]{:S(2)}) async-start(), calls=%async_computation.2 | async-start | bytes 17301504 | tf_op jit(solution)/shard_map/all_gather | solution.py:52
  22.6 11.6 %copy-start.24 = (bf16[1,128,2048]{2,1,0:T(8,128)(2,1)S(1)}, bf16[1,128,2048]{2,1,0:T(8,128)(2,1)}, u32[]{:S(2)}) copy-start(bf16[1,128,2048]{2,1,0:T(8,128)(2,1)} %param.8) | copy-start | bytes 1572868
  22.6 12.2 %copy-start.25 = (bf16[1,128,2048]{2,1,0:T(8,128)(2,1)S(1)}, bf16[1,128,2048]{2,1,0:T(8,128)(2,1)}, u32[]{:S(2)}) copy-start(bf16[1,128,2048]{2,1,0:T(8,128)(2,1)} %param.9) | copy-start | bytes 1572868
  22.6 245.1 %all-to-all-start = ((bf16[32,2,32,768]{3,2,1,0:T(8,128)(2,1)}), bf16[32,2,32,768]{3,2,1,0:T(8,128)(2,1)}, u32[]{:S(2)}, u32[]{:S(2)}) async-start(bf16[32,2,32,768]{3,2,1,0:T(8,128)(2,1)} %bitcast.15), calls=%async_computation | async-start | bytes 6291456 | tf_op jit(solution)/shard_map/all_to_all | solution.py:51
  34.2 5.3 %copy-start.23 = (bf16[1,128,2048]{2,1,0:T(8,128)(2,1)S(1)}, bf16[1,128,2048]{2,1,0:T(8,128)(2,1)}, u32[]{:S(2)}) copy-start(bf16[1,128,2048]{2,1,0:T(8,128)(2,1)} %param.10) | copy-start | bytes 1572868
  34.2 321.0 %reduce-scatter.4.cloned.1.call-start = ((), (), s32[]{:S(2)}) async-start(), calls=%async_computation.3 | async-start | bytes 6488064
  34.4 5.4 %copy-start.26 = (bf16[1,128,2048]{2,1,0:T(8,128)(2,1)S(1)}, bf16[1,128,2048]{2,1,0:T(8,128)(2,1)}, u32[]{:S(2)}) copy-start(bf16[1,128,2048]{2,1,0:T(8,128)(2,1)} %param.7) | copy-start | bytes 1572868
  34.8 4.6 %copy-start.20 = (bf16[128,16,128]{0,2,1:T(8,128)(2,1)}, bf16[128,16,128]{0,2,1:T(8,128)(2,1)S(1)}, u32[]{:S(2)}) copy-start(bf16[128,16,128]{0,2,1:T(8,128)(2,1)S(1)} %copy.66) | copy-start | bytes 1572868
  36.1 111.0 %collective-permute-start = (bf16[16,128,128]{2,1,0:T(8,128)(2,1)}, bf16[16,128,128]{2,1,0:T(8,128)(2,1)S(1)}, u32[]{:S(2)}, u32[]{:S(2)}) collective-permute-start(bf16[16,128,128]{2,1,0:T(8,128)(2,1)} %get-tuple-element.26), channel_id=1, source_target_pairs={{0,8},{8,16},{16,24},{24,32},{32,40},{40,48},{48,56},{56,64},{64,7... | collective-permute-start | bytes 1572872 | tf_op jit(solution)/shard_map/ppermute | solution.py:95
  43.1 108.4 %collective-permute-start.4 = (bf16[16,128,128]{2,1,0:T(8,128)(2,1)S(1)}, bf16[16,128,128]{2,1,0:T(8,128)(2,1)S(1)}, u32[]{:S(2)}, u32[]{:S(2)}) collective-permute-start(bf16[16,128,128]{2,1,0:T(8,128)(2,1)S(1)} %get-tuple-element.28), channel_id=1, source_target_pairs={{8,0},{16,8},{24,16},{32,24},{40,32},{48,40},{56,48},{64,56},{72,6... | collective-permute-start | bytes 1572872 | tf_op jit(solution)/shard_map/ppermute | solution.py:96
  147.2 37.7 %collective-permute-start.1 = (bf16[16,128,128]{2,1,0:T(8,128)(2,1)S(1)}, bf16[16,128,128]{2,1,0:T(8,128)(2,1)S(1)}, u32[]{:S(2)}, u32[]{:S(2)}) collective-permute-start(bf16[16,128,128]{2,1,0:T(8,128)(2,1)S(1)} %fusion.27), channel_id=1, source_target_pairs={{0,16},{8,24},{16,32},{24,40},{32,48},{40,56},{48,64},{56,72},{64,... | collective-permute-start | bytes 1572872 | tf_op jit(solution)/shard_map/ppermute | solution.py:95
  151.6 42.8 %collective-permute-start.5 = (bf16[16,128,128]{2,1,0:T(8,128)(2,1)S(1)}, bf16[16,128,128]{2,1,0:T(8,128)(2,1)S(1)}, u32[]{:S(2)}, u32[]{:S(2)}) collective-permute-start(bf16[16,128,128]{2,1,0:T(8,128)(2,1)S(1)} %fusion.28), channel_id=1, source_target_pairs={{16,0},{24,8},{32,16},{40,24},{48,32},{56,40},{64,48},{72,56},{80,... | collective-permute-start | bytes 1572872 | tf_op jit(solution)/shard_map/ppermute | solution.py:96
  184.9 43.6 %copy-start.3 = (bf16[16,128,128]{2,1,0:T(8,128)(2,1)}, bf16[16,128,128]{2,1,0:T(8,128)(2,1)S(1)}, u32[]{:S(2)}) copy-start(bf16[16,128,128]{2,1,0:T(8,128)(2,1)S(1)} %collective-permute-done.1) | copy-start | bytes 1572868
  185.1 42.3 %collective-permute-start.2 = (bf16[16,128,128]{2,1,0:T(8,128)(2,1)S(1)}, bf16[16,128,128]{2,1,0:T(8,128)(2,1)S(1)}, u32[]{:S(2)}, u32[]{:S(2)}) collective-permute-start(bf16[16,128,128]{2,1,0:T(8,128)(2,1)S(1)} %add_convert_fusion.5), channel_id=1, source_target_pairs={{0,32},{8,40},{16,48},{24,56},{32,64},{40,72},{48,80},{56,88},{64,... | collective-permute-start | bytes 1572872 | tf_op jit(solution)/shard_map/ppermute | solution.py:95
  194.4 71.9 %copy-start = (bf16[16,128,128]{2,1,0:T(8,128)(2,1)}, bf16[16,128,128]{2,1,0:T(8,128)(2,1)S(1)}, u32[]{:S(2)}) copy-start(bf16[16,128,128]{2,1,0:T(8,128)(2,1)S(1)} %collective-permute-done.5) | copy-start | bytes 1572868
  194.6 69.7 %collective-permute-start.6 = (bf16[16,128,128]{2,1,0:T(8,128)(2,1)S(1)}, bf16[16,128,128]{2,1,0:T(8,128)(2,1)S(1)}, u32[]{:S(2)}, u32[]{:S(2)}) collective-permute-start(bf16[16,128,128]{2,1,0:T(8,128)(2,1)S(1)} %add_convert_fusion.3), channel_id=1, source_target_pairs={{32,0},{40,8},{48,16},{56,24},{64,32},{72,40},{80,48},{88,56},{96,... | collective-permute-start | bytes 1572872 | tf_op jit(solution)/shard_map/ppermute | solution.py:96
  227.4 38.8 %copy-start.16 = (bf16[16,128,128]{2,1,0:T(8,128)(2,1)}, bf16[16,128,128]{2,1,0:T(8,128)(2,1)S(1)}, u32[]{:S(2)}) copy-start(bf16[16,128,128]{2,1,0:T(8,128)(2,1)S(1)} %collective-permute-done.2) | copy-start | bytes 1572868
  228.5 50.7 %collective-permute-start.3 = (bf16[16,128,128]{2,1,0:T(8,128)(2,1)}, bf16[16,128,128]{2,1,0:T(8,128)(2,1)}, u32[]{:S(2)}, u32[]{:S(2)}) collective-permute-start(bf16[16,128,128]{2,1,0:T(8,128)(2,1)} %add_convert_fusion.4), channel_id=1, source_target_pairs={{0,64},{8,72},{16,80},{24,88},{32,96},{40,104},{48,112},{56,120},{... | collective-permute-start | bytes 1572872 | tf_op jit(solution)/shard_map/ppermute | solution.py:95
  266.2 14.9 %collective-permute-start.7 = (bf16[16,128,128]{2,1,0:T(8,128)(2,1)}, bf16[16,128,128]{2,1,0:T(8,128)(2,1)}, u32[]{:S(2)}, u32[]{:S(2)}) collective-permute-start(bf16[16,128,128]{2,1,0:T(8,128)(2,1)} %add_convert_fusion.2), channel_id=1, source_target_pairs={{64,0},{72,8},{80,16},{88,24},{96,32},{104,40},{112,48},{120,56},{... | collective-permute-start | bytes 1572872 | tf_op jit(solution)/shard_map/ppermute | solution.py:96
  314.3 3.6 copy-start.7
  314.3 4.7 %copy-start.10 = (bf16[1,128,2048]{1,2,0:T(8,128)(2,1)S(1)}, bf16[1,128,2048]{1,2,0:T(8,128)(2,1)}, u32[]{:S(2)}) copy-start(bf16[1,128,2048]{1,2,0:T(8,128)(2,1)} %copy-done.9) | copy-start | bytes 1572868
  320.8 6.5 %copy-start.21 = (bf16[128,16,128]{0,2,1:T(8,128)(2,1)S(1)}, bf16[128,16,128]{0,2,1:T(8,128)(2,1)}, u32[]{:S(2)}) copy-start(bf16[128,16,128]{0,2,1:T(8,128)(2,1)} %copy-done.20) | copy-start | bytes 1572868
  322.6 7.1 %copy-start.1 = (bf16[16,128,128]{2,1,0:T(8,128)(2,1)S(1)}, bf16[16,128,128]{2,1,0:T(8,128)(2,1)}, u32[]{:S(2)}) copy-start(bf16[16,128,128]{2,1,0:T(8,128)(2,1)} %copy-done) | copy-start | bytes 1572868
  322.6 7.1 %copy-start.14 = (bf16[16,128,128]{2,1,0:T(8,128)(2,1)S(1)}, bf16[16,128,128]{2,1,0:T(8,128)(2,1)}, u32[]{:S(2)}) copy-start(bf16[16,128,128]{2,1,0:T(8,128)(2,1)} %copy-done.13) | copy-start | bytes 1572868
  324.1 12.4 %collective-permute-start.8 = (bf16[16,128,128]{2,1,0:T(8,128)(2,1)S(1)}, bf16[16,128,128]{2,1,0:T(8,128)(2,1)S(1)}, u32[]{:S(2)}, u32[]{:S(2)}) collective-permute-start(bf16[16,128,128]{2,1,0:T(8,128)(2,1)S(1)} %add_convert_fusion.1), channel_id=1, source_target_pairs={{0,128},{8,136},{16,144},{24,152},{32,160},{40,168},{48,176},{56,1... | collective-permute-start | bytes 1572872 | tf_op jit(solution)/shard_map/ppermute | solution.py:95
  331.9 8.1 %copy-start.5 = (bf16[16,128,128]{2,1,0:T(8,128)(2,1)S(1)}, bf16[16,128,128]{2,1,0:T(8,128)(2,1)}, u32[]{:S(2)}) copy-start(bf16[16,128,128]{2,1,0:T(8,128)(2,1)} %copy-done.3) | copy-start | bytes 1572868
  331.9 8.1 %copy-start.11 = (bf16[1,128,2048]{1,2,0:T(8,128)(2,1)S(1)}, bf16[1,128,2048]{1,2,0:T(8,128)(2,1)}, u32[]{:S(2)}) copy-start(bf16[1,128,2048]{1,2,0:T(8,128)(2,1)} %copy-done.9) | copy-start | bytes 1572868
  331.9 15.2 %collective-permute-start.9 = (bf16[16,128,128]{2,1,0:T(8,128)(2,1)}, bf16[16,128,128]{2,1,0:T(8,128)(2,1)}, u32[]{:S(2)}, u32[]{:S(2)}) collective-permute-start(bf16[16,128,128]{2,1,0:T(8,128)(2,1)} %add_convert_fusion), channel_id=1, source_target_pairs={{128,0},{136,8},{144,16},{152,24},{160,32},{168,40},{176,48},{184,... | collective-permute-start | bytes 1572872 | tf_op jit(solution)/shard_map/ppermute | solution.py:96
  340.0 7.2 %copy-start.2 = (bf16[16,128,128]{2,1,0:T(8,128)(2,1)S(1)}, bf16[16,128,128]{2,1,0:T(8,128)(2,1)}, u32[]{:S(2)}) copy-start(bf16[16,128,128]{2,1,0:T(8,128)(2,1)} %copy-done) | copy-start | bytes 1572868
  340.0 7.2 %copy-start.8 = (bf16[16,8,16,128]{3,2,1,0:T(8,128)(2,1)S(1)}, bf16[16,8,16,128]{3,2,1,0:T(8,128)(2,1)}, u32[]{:S(2)}) copy-start(bf16[16,8,16,128]{3,2,1,0:T(8,128)(2,1)} %copy-done.6) | copy-start | bytes 1572868
  345.6 5.7 %copy-start.15 = (bf16[16,128,128]{2,1,0:T(8,128)(2,1)S(1)}, bf16[16,128,128]{2,1,0:T(8,128)(2,1)}, u32[]{:S(2)}) copy-start(bf16[16,128,128]{2,1,0:T(8,128)(2,1)} %copy-done.13) | copy-start | bytes 1572868
  345.6 5.7 %copy-start.19 = (bf16[16,8,16,128]{3,2,1,0:T(8,128)(2,1)S(1)}, bf16[16,8,16,128]{3,2,1,0:T(8,128)(2,1)}, u32[]{:S(2)}) copy-start(bf16[16,8,16,128]{3,2,1,0:T(8,128)(2,1)} %copy-done.18) | copy-start | bytes 1572868
  (8 other events, 19.4 us)
Sparse Core Ops, SparseCore 0:
  10.6 260.5 all-gather.1
  314.4 39.6 reduce-scatter.3

commit v11 on v10

--- a/solution.py
+++ b/solution.py
@@ -88,13 +88,19 @@
     after_state = jnp.zeros_like(grad_sum)
     fwd_window = state_sum
     bwd_window = grad_sum
+    shifts = []
     shift = 1
     while shift < seq_count:
+        shifts.append(shift)
+        shift *= 2
+    if len(shifts) >= 3:
+        shifts = shifts[:2] + shifts[3:] + [shifts[2]]
+    for step, shift in enumerate(shifts):
         fwd_pairs = [(src, src + shift) for src in range(seq_count - shift)]
         bwd_pairs = [(src, src - shift) for src in range(shift, seq_count)]
         fwd_arrived = lax.ppermute(fwd_window.astype(jnp.bfloat16), "seq", fwd_pairs)
         bwd_arrived = lax.ppermute(bwd_window.astype(jnp.bfloat16), "seq", bwd_pairs)
-        if 2 * shift == seq_count // 2:
+        if step == len(shifts) - 2:
             all_cotangent, fwd_arrived, bwd_arrived = lax.optimization_barrier(
                 (all_cotangent, fwd_arrived, bwd_arrived)
             )
@@ -102,7 +108,6 @@
         after_state = after_state + bwd_arrived.astype(jnp.float32)
         fwd_window = state_sum + prefix_state
         bwd_window = grad_sum + after_state
-        shift *= 2
     group_term = jnp.dot(
         token_weights, all_cotangent, preferred_element_type=jnp.float32
     ).reshape(hidden_units, EXP_DEV, width)

time: 365 us -> 348 us (0.953)
  waiting for transfers between devices: 198 us -> 179 us
    ppermute x5, waiting for transfers between devices: 168 us -> 155 us  [per_device(): lax.ppermute(fwd_window.astype(jnp.bfloat16), 'seq', fwd_pairs)]
    ppermute x5, waiting for transfers between devices: 29.1 us -> 22.1 us  [per_device(): lax.ppermute(bwd_window.astype(jnp.bfloat16), 'seq', bwd_pairs)]
  transfers between devices with their start and end apart: 13 -> 13, of which waited for: 7 -> 7; matrix products, arithmetic and copies ran while one was open for 18% -> 19% of each run, Pallas kernels for 0% -> 0%
where the time goes in v11:
time: 348 us; the launch traced here: 345 us
  waiting for transfers between devices  179 us (51%)
  matrix products  68.5 us (20%)
  starting transfers between devices  49.7 us (14%)
  local copies, waits for them, and re-layouts  22.5 us (6%)
  between operations  14.5 us (4%)
  other arithmetic  10.5 us (3%)
    ppermute x5, waiting for transfers between devices, per_device(): lax.ppermute(fwd_window.astype(jnp.bfloat16), 'seq', fwd_pairs)  155 us
    dot_general x1, matrix products, per_device(): jnp.dot(token_weights, all_cotangent, preferred_element_type=jnp.float32)  30.2 us
    ppermute x5, starting transfers between devices, per_device(): lax.ppermute(fwd_window.astype(jnp.bfloat16), 'seq', fwd_pairs)  29.9 us
    ppermute x5, waiting for transfers between devices, per_device(): lax.ppermute(bwd_window.astype(jnp.bfloat16), 'seq', bwd_pairs)  22.1 us
    unnamed x66, local copies, waits for them, and re-layouts  15.3 us
    all_to_all x1, starting transfers between devices, per_device(): lax.all_to_all(hidden_slots, 'seq', split_axis=0, concat_axis=0, tiled=True)  11.5 us
    ppermute x5, starting transfers between devices, per_device(): lax.ppermute(bwd_window.astype(jnp.bfloat16), 'seq', bwd_pairs)  8.18 us
    dot_general x1, matrix products, per_device(): jnp.einsum('sxtc,sxcf->fxst', token_pick, arrived_hidden, preferred_eleme...  7.9 us
  transfers between devices with their start and end apart: 13, of which 7 were waited for; matrix products, arithmetic and copies ran while one was open for 19% of the time, Pallas kernels for 0%

profile of v11, /device:TPU:32, one launch (start us, length us, event | category | flops | bytes accessed | tf_op | source)
XLA Modules:
  0.0 345.0 jit_solution(14215147734311384772)
XLA Ops:
  9.9 1.8 reduce-window.6
  12.0 2.0 copy.83
  16.0 1.9 multiply_convert_fusion
  17.9 4.7 %fusion.10 = bf16[2048,768]{1,0:T(8,128)(2,1)} fusion(s32[768]{0:T(1024)S(1)} %multiply_add_fusion, bf16[768,1]{1,0:T(8,128)(2,1)S(1)} %fusion.42, bf16[768,704]{1,0:T(8,128)(2,1)S(1)} %multiply_convert_fusion, bf16[768]{0:T(1024)(128)(2,1)S(1)} %pad.2.clone), kind=kOutput, calls=%fused_computation.8 | convolution fusion | flops 2422603776 | bytes 4233216 | tf_op jit(solution)/shard_map/dot_general | solution.py:47
  22.6 11.5 %all-to-all-start = ((bf16[32,2,32,768]{3,2,1,0:T(8,128)(2,1)}), bf16[32,2,32,768]{3,2,1,0:T(8,128)(2,1)}, u32[]{:S(2)}, u32[]{:S(2)}) async-start(bf16[32,2,32,768]{3,2,1,0:T(8,128)(2,1)} %bitcast.15), calls=%async_computation | async-start | bytes 6291456 | tf_op jit(solution)/shard_map/all_to_all | solution.py:51
  36.1 3.4 collective-permute-start
  40.8 2.2 fusion.58
  43.1 2.5 collective-permute-start.4
  45.6 101.5 %collective-permute-done = bf16[16,128,128]{2,1,0:T(8,128)(2,1)S(1)} collective-permute-done((bf16[16,128,128]{2,1,0:T(8,128)(2,1)}, bf16[16,128,128]{2,1,0:T(8,128)(2,1)S(1)}, u32[]{:S(2)}, u32[]{:S(2)}) %collective-permute-start) | collective-permute-done | bytes 524320 | tf_op jit(solution)/shard_map/ppermute | solution.py:101
  147.2 4.2 %collective-permute-start.1 = (bf16[16,128,128]{2,1,0:T(8,128)(2,1)S(1)}, bf16[16,128,128]{2,1,0:T(8,128)(2,1)S(1)}, u32[]{:S(2)}, u32[]{:S(2)}) collective-permute-start(bf16[16,128,128]{2,1,0:T(8,128)(2,1)S(1)} %fusion.27), channel_id=1, source_target_pairs={{0,16},{8,24},{16,32},{24,40},{32,48},{40,56},{48,64},{56,72},{64,... | collective-permute-start | bytes 1572872 | tf_op jit(solution)/shard_map/ppermute | solution.py:101
  152.9 32.0 %collective-permute-done.1 = bf16[16,128,128]{2,1,0:T(8,128)(2,1)S(1)} collective-permute-done((bf16[16,128,128]{2,1,0:T(8,128)(2,1)S(1)}, bf16[16,128,128]{2,1,0:T(8,128)(2,1)S(1)}, u32[]{:S(2)}, u32[]{:S(2)}) %collective-permute-start.1) | collective-permute-done | bytes 524320 | tf_op jit(solution)/shard_map/ppermute | solution.py:101
  185.1 7.2 %collective-permute-start.2 = (bf16[16,128,128]{2,1,0:T(8,128)(2,1)S(1)}, bf16[16,128,128]{2,1,0:T(8,128)(2,1)S(1)}, u32[]{:S(2)}, u32[]{:S(2)}) collective-permute-start(bf16[16,128,128]{2,1,0:T(8,128)(2,1)S(1)} %add_convert_fusion.5), channel_id=1, source_target_pairs={{0,64},{8,72},{16,80},{24,88},{32,96},{40,104},{48,112},{56,120},{... | collective-permute-start | bytes 1572872 | tf_op jit(solution)/shard_map/ppermute | solution.py:101
  193.8 8.0 %collective-permute-done.2 = bf16[16,128,128]{2,1,0:T(8,128)(2,1)S(1)} collective-permute-done((bf16[16,128,128]{2,1,0:T(8,128)(2,1)S(1)}, bf16[16,128,128]{2,1,0:T(8,128)(2,1)S(1)}, u32[]{:S(2)}, u32[]{:S(2)}) %collective-permute-start.2) | collective-permute-done | bytes 524320 | tf_op jit(solution)/shard_map/ppermute | solution.py:101
  202.9 8.4 %collective-permute-start.3 = (bf16[16,128,128]{2,1,0:T(8,128)(2,1)}, bf16[16,128,128]{2,1,0:T(8,128)(2,1)}, u32[]{:S(2)}, u32[]{:S(2)}) collective-permute-start(bf16[16,128,128]{2,1,0:T(8,128)(2,1)} %add_convert_fusion.4), channel_id=1, source_target_pairs={{0,128},{8,136},{16,144},{24,152},{32,160},{40,168},{48,176},{56,1... | collective-permute-start | bytes 1572872 | tf_op jit(solution)/shard_map/ppermute | solution.py:101
  214.7 2.1 slice.18
  218.3 7.9 %convert_bitcast_fusion = bf16[2,32,88,8,128]{4,3,2,1,0:T(8,128)(2,1)} fusion(s32[32,2,32]{2,0,1:T(8,128)S(1)} %add_bitcast_fusion.1, bf16[32,2,32,768]{3,2,1,0:T(8,128)(2,1)} %all-to-all-done), kind=kOutput, calls=%fused_computation.4 | convolution fusion | flops 375128064 | bytes 14688256 | tf_op jit(solution)/shard_map/sxtc,sxcf->fxst/dot_general | solution.py:58
  226.2 3.5 %collective-permute-done.7 = bf16[16,128,128]{2,1,0:T(8,128)(2,1)} collective-permute-done((bf16[16,128,128]{2,1,0:T(8,128)(2,1)}, bf16[16,128,128]{2,1,0:T(8,128)(2,1)}, u32[]{:S(2)}, u32[]{:S(2)}) %collective-permute-start.7) | collective-permute-done | bytes 524320 | tf_op jit(solution)/shard_map/ppermute | solution.py:102
  231.1 30.2 %fusion.5 = bf16[704,2,2048]{2,0,1:T(8,128)(2,1)S(1)} fusion(bf16[4096,2048]{1,0:T(8,128)(2,1)} %bitcast.132, bf16[2,32,88,8,128]{4,3,2,1,0:T(8,128)(2,1)} %convert_bitcast_fusion), kind=kOutput, calls=%fused_computation.7 | convolution fusion | flops 23625203712 | bytes 34078720 | tf_op jit(solution)/shard_map/dot_general | solution.py:111
  261.3 3.0 copy.103
  264.4 1.8 convolution_multiply_fusion
  269.1 1.8 convolution_bitcast_fusion.1
  274.1 6.6 %collective-permute-start.8 = (bf16[16,128,128]{2,1,0:T(8,128)(2,1)S(1)}, bf16[16,128,128]{2,1,0:T(8,128)(2,1)S(1)}, u32[]{:S(2)}, u32[]{:S(2)}) collective-permute-start(bf16[16,128,128]{2,1,0:T(8,128)(2,1)S(1)} %add_convert_fusion.1), channel_id=1, source_target_pairs={{0,32},{8,40},{16,48},{24,56},{32,64},{40,72},{48,80},{56,88},{64,... | collective-permute-start | bytes 1572872 | tf_op jit(solution)/shard_map/ppermute | solution.py:101
  280.8 2.3 convolution_bitcast_fusion.5
  283.1 2.2 add_convert_fusion
  287.0 13.5 %collective-permute-done.8 = bf16[16,128,128]{2,1,0:T(8,128)(2,1)S(1)} collective-permute-done((bf16[16,128,128]{2,1,0:T(8,128)(2,1)S(1)}, bf16[16,128,128]{2,1,0:T(8,128)(2,1)S(1)}, u32[]{:S(2)}, u32[]{:S(2)}) %collective-permute-start.8) | collective-permute-done | bytes 524320 | tf_op jit(solution)/shard_map/ppermute | solution.py:101
  300.5 2.4 fusion.21
  304.0 3.5 %fusion.22 = bf16[128,16,128]{0,2,1:T(8,128)(2,1)} fusion(f32[128,16,128]{0,2,1:T(8,128)} %convolution_bitcast_fusion.5, bf16[128,16,128]{0,2,1:T(8,128)(2,1)S(1)} %bitcast.114, f32[128]{0:T(128)S(1)} %multiply_rsqrt_fusion, bf16[16,128,128]{2,1,0:T(8,128)(2,1)} %copy-done.22, bf16[16,128,128]{2,1,0:T(8,128)(2,1)} %collective-permute-done.3, ...), kind=kOutput, calls=%fused_computation.35 | convolution fusion | flops 405798912 | bytes 4719104 | tf_op jit(solution)/shard_map/the,hde->thd/dot_general | solution.py:118
  307.5 2.1 copy.88
  309.6 18.7 %collective-permute-done.9 = bf16[16,128,128]{2,1,0:T(8,128)(2,1)} collective-permute-done((bf16[16,128,128]{2,1,0:T(8,128)(2,1)}, bf16[16,128,128]{2,1,0:T(8,128)(2,1)}, u32[]{:S(2)}, u32[]{:S(2)}) %collective-permute-start.9) | collective-permute-done | bytes 524320 | tf_op jit(solution)/shard_map/ppermute | solution.py:102
  328.3 3.1 fusion.19
  332.4 2.8 fusion.20
  336.1 2.0 copy.130
  (106 shorter events, 29.6 us)
Async XLA Ops:
  7.2 224.0 %all-gather.2.cloned.1.call-start = ((), (), s32[]{:S(2)}) async-start(), calls=%async_computation.2 | async-start | bytes 17301504 | tf_op jit(solution)/shard_map/all_gather | solution.py:52
  22.6 11.6 %copy-start.24 = (bf16[1,128,2048]{2,1,0:T(8,128)(2,1)S(1)}, bf16[1,128,2048]{2,1,0:T(8,128)(2,1)}, u32[]{:S(2)}) copy-start(bf16[1,128,2048]{2,1,0:T(8,128)(2,1)} %param.8) | copy-start | bytes 1572868
  22.6 12.2 %copy-start.25 = (bf16[1,128,2048]{2,1,0:T(8,128)(2,1)S(1)}, bf16[1,128,2048]{2,1,0:T(8,128)(2,1)}, u32[]{:S(2)}) copy-start(bf16[1,128,2048]{2,1,0:T(8,128)(2,1)} %param.9) | copy-start | bytes 1572868
  22.6 192.1 %all-to-all-start = ((bf16[32,2,32,768]{3,2,1,0:T(8,128)(2,1)}), bf16[32,2,32,768]{3,2,1,0:T(8,128)(2,1)}, u32[]{:S(2)}, u32[]{:S(2)}) async-start(bf16[32,2,32,768]{3,2,1,0:T(8,128)(2,1)} %bitcast.15), calls=%async_computation | async-start | bytes 6291456 | tf_op jit(solution)/shard_map/all_to_all | solution.py:51
  34.2 5.3 %copy-start.23 = (bf16[1,128,2048]{2,1,0:T(8,128)(2,1)S(1)}, bf16[1,128,2048]{2,1,0:T(8,128)(2,1)}, u32[]{:S(2)}) copy-start(bf16[1,128,2048]{2,1,0:T(8,128)(2,1)} %param.10) | copy-start | bytes 1572868
  34.2 302.0 %reduce-scatter.4.cloned.1.call-start = ((), (), s32[]{:S(2)}) async-start(), calls=%async_computation.3 | async-start | bytes 6488064
  34.4 5.4 %copy-start.26 = (bf16[1,128,2048]{2,1,0:T(8,128)(2,1)S(1)}, bf16[1,128,2048]{2,1,0:T(8,128)(2,1)}, u32[]{:S(2)}) copy-start(bf16[1,128,2048]{2,1,0:T(8,128)(2,1)} %param.7) | copy-start | bytes 1572868
  34.8 4.6 %copy-start.20 = (bf16[128,16,128]{0,2,1:T(8,128)(2,1)}, bf16[128,16,128]{0,2,1:T(8,128)(2,1)S(1)}, u32[]{:S(2)}) copy-start(bf16[128,16,128]{0,2,1:T(8,128)(2,1)S(1)} %copy.66) | copy-start | bytes 1572868
  36.1 111.0 %collective-permute-start = (bf16[16,128,128]{2,1,0:T(8,128)(2,1)}, bf16[16,128,128]{2,1,0:T(8,128)(2,1)S(1)}, u32[]{:S(2)}, u32[]{:S(2)}) collective-permute-start(bf16[16,128,128]{2,1,0:T(8,128)(2,1)} %get-tuple-element.26), channel_id=1, source_target_pairs={{0,8},{8,16},{16,24},{24,32},{32,40},{40,48},{48,56},{56,64},{64,7... | collective-permute-start | bytes 1572872 | tf_op jit(solution)/shard_map/ppermute | solution.py:101
  43.1 108.4 %collective-permute-start.4 = (bf16[16,128,128]{2,1,0:T(8,128)(2,1)S(1)}, bf16[16,128,128]{2,1,0:T(8,128)(2,1)S(1)}, u32[]{:S(2)}, u32[]{:S(2)}) collective-permute-start(bf16[16,128,128]{2,1,0:T(8,128)(2,1)S(1)} %get-tuple-element.28), channel_id=1, source_target_pairs={{8,0},{16,8},{24,16},{32,24},{40,32},{48,40},{56,48},{64,56},{72,6... | collective-permute-start | bytes 1572872 | tf_op jit(solution)/shard_map/ppermute | solution.py:102
  147.2 37.7 %collective-permute-start.1 = (bf16[16,128,128]{2,1,0:T(8,128)(2,1)S(1)}, bf16[16,128,128]{2,1,0:T(8,128)(2,1)S(1)}, u32[]{:S(2)}, u32[]{:S(2)}) collective-permute-start(bf16[16,128,128]{2,1,0:T(8,128)(2,1)S(1)} %fusion.27), channel_id=1, source_target_pairs={{0,16},{8,24},{16,32},{24,40},{32,48},{40,56},{48,64},{56,72},{64,... | collective-permute-start | bytes 1572872 | tf_op jit(solution)/shard_map/ppermute | solution.py:101
  151.6 40.7 %collective-permute-start.5 = (bf16[16,128,128]{2,1,0:T(8,128)(2,1)S(1)}, bf16[16,128,128]{2,1,0:T(8,128)(2,1)S(1)}, u32[]{:S(2)}, u32[]{:S(2)}) collective-permute-start(bf16[16,128,128]{2,1,0:T(8,128)(2,1)S(1)} %fusion.28), channel_id=1, source_target_pairs={{16,0},{24,8},{32,16},{40,24},{48,32},{56,40},{64,48},{72,56},{80,... | collective-permute-start | bytes 1572872 | tf_op jit(solution)/shard_map/ppermute | solution.py:102
  184.9 18.0 %copy-start.3 = (bf16[16,128,128]{2,1,0:T(8,128)(2,1)}, bf16[16,128,128]{2,1,0:T(8,128)(2,1)S(1)}, u32[]{:S(2)}) copy-start(bf16[16,128,128]{2,1,0:T(8,128)(2,1)S(1)} %collective-permute-done.1) | copy-start | bytes 1572868
  185.1 16.8 %collective-permute-start.2 = (bf16[16,128,128]{2,1,0:T(8,128)(2,1)S(1)}, bf16[16,128,128]{2,1,0:T(8,128)(2,1)S(1)}, u32[]{:S(2)}, u32[]{:S(2)}) collective-permute-start(bf16[16,128,128]{2,1,0:T(8,128)(2,1)S(1)} %add_convert_fusion.5), channel_id=1, source_target_pairs={{0,64},{8,72},{16,80},{24,88},{32,96},{40,104},{48,112},{56,120},{... | collective-permute-start | bytes 1572872 | tf_op jit(solution)/shard_map/ppermute | solution.py:101
  192.3 20.9 %copy-start = (bf16[16,128,128]{2,1,0:T(8,128)(2,1)}, bf16[16,128,128]{2,1,0:T(8,128)(2,1)S(1)}, u32[]{:S(2)}) copy-start(bf16[16,128,128]{2,1,0:T(8,128)(2,1)S(1)} %collective-permute-done.5) | copy-start | bytes 1572868
  192.5 18.8 %collective-permute-start.6 = (bf16[16,128,128]{2,1,0:T(8,128)(2,1)S(1)}, bf16[16,128,128]{2,1,0:T(8,128)(2,1)S(1)}, u32[]{:S(2)}, u32[]{:S(2)}) collective-permute-start(bf16[16,128,128]{2,1,0:T(8,128)(2,1)S(1)} %add_convert_fusion.3), channel_id=1, source_target_pairs={{64,0},{72,8},{80,16},{88,24},{96,32},{104,40},{112,48},{120,56},{... | collective-permute-start | bytes 1572872 | tf_op jit(solution)/shard_map/ppermute | solution.py:102
  201.8 11.4 %copy-start.16 = (bf16[16,128,128]{2,1,0:T(8,128)(2,1)}, bf16[16,128,128]{2,1,0:T(8,128)(2,1)S(1)}, u32[]{:S(2)}) copy-start(bf16[16,128,128]{2,1,0:T(8,128)(2,1)S(1)} %collective-permute-done.2) | copy-start | bytes 1572868
  202.9 23.3 %collective-permute-start.3 = (bf16[16,128,128]{2,1,0:T(8,128)(2,1)}, bf16[16,128,128]{2,1,0:T(8,128)(2,1)}, u32[]{:S(2)}, u32[]{:S(2)}) collective-permute-start(bf16[16,128,128]{2,1,0:T(8,128)(2,1)} %add_convert_fusion.4), channel_id=1, source_target_pairs={{0,128},{8,136},{16,144},{24,152},{32,160},{40,168},{48,176},{56,1... | collective-permute-start | bytes 1572872 | tf_op jit(solution)/shard_map/ppermute | solution.py:101
  213.3 16.4 %collective-permute-start.7 = (bf16[16,128,128]{2,1,0:T(8,128)(2,1)}, bf16[16,128,128]{2,1,0:T(8,128)(2,1)}, u32[]{:S(2)}, u32[]{:S(2)}) collective-permute-start(bf16[16,128,128]{2,1,0:T(8,128)(2,1)} %add_convert_fusion.2), channel_id=1, source_target_pairs={{128,0},{136,8},{144,16},{152,24},{160,32},{168,40},{176,48},{184,... | collective-permute-start | bytes 1572872 | tf_op jit(solution)/shard_map/ppermute | solution.py:102
  264.3 3.6 %copy-start.7 = (bf16[16,8,16,128]{3,2,1,0:T(8,128)(2,1)S(1)}, bf16[16,8,16,128]{3,2,1,0:T(8,128)(2,1)}, u32[]{:S(2)}) copy-start(bf16[16,8,16,128]{3,2,1,0:T(8,128)(2,1)} %copy-done.6) | copy-start | bytes 1572868
  264.3 4.7 %copy-start.10 = (bf16[1,128,2048]{1,2,0:T(8,128)(2,1)S(1)}, bf16[1,128,2048]{1,2,0:T(8,128)(2,1)}, u32[]{:S(2)}) copy-start(bf16[1,128,2048]{1,2,0:T(8,128)(2,1)} %copy-done.9) | copy-start | bytes 1572868
  270.9 9.9 %copy-start.21 = (bf16[128,16,128]{0,2,1:T(8,128)(2,1)S(1)}, bf16[128,16,128]{0,2,1:T(8,128)(2,1)}, u32[]{:S(2)}) copy-start(bf16[128,16,128]{0,2,1:T(8,128)(2,1)} %copy-done.20) | copy-start | bytes 1572868
  272.6 10.4 %copy-start.1 = (bf16[16,128,128]{2,1,0:T(8,128)(2,1)S(1)}, bf16[16,128,128]{2,1,0:T(8,128)(2,1)}, u32[]{:S(2)}) copy-start(bf16[16,128,128]{2,1,0:T(8,128)(2,1)} %copy-done) | copy-start | bytes 1572868
  272.6 10.4 %copy-start.14 = (bf16[16,128,128]{2,1,0:T(8,128)(2,1)S(1)}, bf16[16,128,128]{2,1,0:T(8,128)(2,1)}, u32[]{:S(2)}) copy-start(bf16[16,128,128]{2,1,0:T(8,128)(2,1)} %copy-done.13) | copy-start | bytes 1572868
  274.1 26.4 %collective-permute-start.8 = (bf16[16,128,128]{2,1,0:T(8,128)(2,1)S(1)}, bf16[16,128,128]{2,1,0:T(8,128)(2,1)S(1)}, u32[]{:S(2)}, u32[]{:S(2)}) collective-permute-start(bf16[16,128,128]{2,1,0:T(8,128)(2,1)S(1)} %add_convert_fusion.1), channel_id=1, source_target_pairs={{0,32},{8,40},{16,48},{24,56},{32,64},{40,72},{48,80},{56,88},{64,... | collective-permute-start | bytes 1572872 | tf_op jit(solution)/shard_map/ppermute | solution.py:101
  285.3 18.7 %copy-start.5 = (bf16[16,128,128]{2,1,0:T(8,128)(2,1)S(1)}, bf16[16,128,128]{2,1,0:T(8,128)(2,1)}, u32[]{:S(2)}) copy-start(bf16[16,128,128]{2,1,0:T(8,128)(2,1)} %copy-done.3) | copy-start | bytes 1572868
  285.3 18.7 %copy-start.11 = (bf16[1,128,2048]{1,2,0:T(8,128)(2,1)S(1)}, bf16[1,128,2048]{1,2,0:T(8,128)(2,1)}, u32[]{:S(2)}) copy-start(bf16[1,128,2048]{1,2,0:T(8,128)(2,1)} %copy-done.9) | copy-start | bytes 1572868
  285.3 42.9 %collective-permute-start.9 = (bf16[16,128,128]{2,1,0:T(8,128)(2,1)}, bf16[16,128,128]{2,1,0:T(8,128)(2,1)}, u32[]{:S(2)}, u32[]{:S(2)}) collective-permute-start(bf16[16,128,128]{2,1,0:T(8,128)(2,1)} %add_convert_fusion), channel_id=1, source_target_pairs={{32,0},{40,8},{48,16},{56,24},{64,32},{72,40},{80,48},{88,56},{96,... | collective-permute-start | bytes 1572872 | tf_op jit(solution)/shard_map/ppermute | solution.py:102
  304.0 24.3 %copy-start.2 = (bf16[16,128,128]{2,1,0:T(8,128)(2,1)S(1)}, bf16[16,128,128]{2,1,0:T(8,128)(2,1)}, u32[]{:S(2)}) copy-start(bf16[16,128,128]{2,1,0:T(8,128)(2,1)} %copy-done) | copy-start | bytes 1572868
  304.0 24.3 %copy-start.8 = (bf16[16,8,16,128]{3,2,1,0:T(8,128)(2,1)S(1)}, bf16[16,8,16,128]{3,2,1,0:T(8,128)(2,1)}, u32[]{:S(2)}) copy-start(bf16[16,8,16,128]{3,2,1,0:T(8,128)(2,1)} %copy-done.6) | copy-start | bytes 1572868
  309.6 22.8 %copy-start.15 = (bf16[16,128,128]{2,1,0:T(8,128)(2,1)S(1)}, bf16[16,128,128]{2,1,0:T(8,128)(2,1)}, u32[]{:S(2)}) copy-start(bf16[16,128,128]{2,1,0:T(8,128)(2,1)} %copy-done.13) | copy-start | bytes 1572868
  309.6 22.8 %copy-start.19 = (bf16[16,8,16,128]{3,2,1,0:T(8,128)(2,1)S(1)}, bf16[16,8,16,128]{3,2,1,0:T(8,128)(2,1)}, u32[]{:S(2)}) copy-start(bf16[16,8,16,128]{3,2,1,0:T(8,128)(2,1)} %copy-done.18) | copy-start | bytes 1572868
  (8 other events, 19.4 us)
Sparse Core Ops, SparseCore 0:
  10.6 220.4 all-gather.1
  264.4 45.0 reduce-scatter.3

commit v12 on v11

--- a/solution.py
+++ b/solution.py
@@ -94,13 +94,13 @@
         shifts.append(shift)
         shift *= 2
     if len(shifts) >= 3:
-        shifts = shifts[:2] + shifts[3:] + [shifts[2]]
+        shifts = shifts[:1] + shifts[3:] + shifts[1:3]
     for step, shift in enumerate(shifts):
         fwd_pairs = [(src, src + shift) for src in range(seq_count - shift)]
         bwd_pairs = [(src, src - shift) for src in range(shift, seq_count)]
         fwd_arrived = lax.ppermute(fwd_window.astype(jnp.bfloat16), "seq", fwd_pairs)
         bwd_arrived = lax.ppermute(bwd_window.astype(jnp.bfloat16), "seq", bwd_pairs)
-        if step == len(shifts) - 2:
+        if step == len(shifts) - 3:
             all_cotangent, fwd_arrived, bwd_arrived = lax.optimization_barrier(
                 (all_cotangent, fwd_arrived, bwd_arrived)
             )

time: 348 us -> 397 us (1.14)
  the two profiles are of different devices: /device:TPU:32 before, /device:TPU:55 now
where the time goes in v12:
time: 397 us; the launch traced here: 396 us
  waiting for transfers between devices  234 us (59%)
  matrix products  68.4 us (17%)
  starting transfers between devices  43.1 us (11%)
  local copies, waits for them, and re-layouts  23.3 us (6%)
  between operations  14.6 us (4%)
  other arithmetic  12.9 us (3%)
    ppermute x5, waiting for transfers between devices, per_device(): lax.ppermute(fwd_window.astype(jnp.bfloat16), 'seq', fwd_pairs)  192 us
    dot_general x1, matrix products, per_device(): jnp.dot(token_weights, all_cotangent, preferred_element_type=jnp.float32)  30.2 us
    all_gather x1, waiting for transfers between devices, per_device(): all_cotangent = lax.all_gather(cotangent, 'seq', axis=1, tiled=True)[0]  27 us
    ppermute x5, starting transfers between devices, per_device(): lax.ppermute(bwd_window.astype(jnp.bfloat16), 'seq', bwd_pairs)  22 us
    unnamed x62, local copies, waits for them, and re-layouts  16.1 us
    ppermute x5, waiting for transfers between devices, per_device(): lax.ppermute(bwd_window.astype(jnp.bfloat16), 'seq', bwd_pairs)  14 us
    all_to_all x1, starting transfers between devices, per_device(): lax.all_to_all(hidden_slots, 'seq', split_axis=0, concat_axis=0, tiled=True)  10.8 us
    ppermute x5, starting transfers between devices, per_device(): lax.ppermute(fwd_window.astype(jnp.bfloat16), 'seq', fwd_pairs)  10.2 us
  transfers between devices with their start and end apart: 13, of which 7 were waited for; matrix products, arithmetic and copies ran while one was open for 17% of the time, Pallas kernels for 0%

profile of v12, /device:TPU:55, one launch (start us, length us, event | category | flops | bytes accessed | tf_op | source)
XLA Modules:
  0.0 396.2 jit_solution(3144208443178773269)
XLA Ops:
  12.0 2.0 copy.83
  17.9 4.7 %fusion.10 = bf16[2048,768]{1,0:T(8,128)(2,1)} fusion(s32[768]{0:T(1024)S(1)} %multiply_add_fusion, bf16[768,1]{1,0:T(8,128)(2,1)S(1)} %fusion.42, bf16[768,704]{1,0:T(8,128)(2,1)S(1)} %multiply_convert_fusion, bf16[768]{0:T(1024)(128)(2,1)S(1)} %pad.2.clone), kind=kOutput, calls=%fused_computation.8 | convolution fusion | flops 2422603776 | bytes 4233216 | tf_op jit(solution)/shard_map/dot_general | solution.py:47
  22.6 10.8 %all-to-all-start = ((bf16[32,2,32,768]{3,2,1,0:T(8,128)(2,1)}), bf16[32,2,32,768]{3,2,1,0:T(8,128)(2,1)}, u32[]{:S(2)}, u32[]{:S(2)}) async-start(bf16[32,2,32,768]{3,2,1,0:T(8,128)(2,1)} %bitcast.15), calls=%async_computation | async-start | bytes 6291456 | tf_op jit(solution)/shard_map/all_to_all | solution.py:51
  35.3 3.1 collective-permute-start
  39.7 2.3 fusion.58
  42.0 2.2 collective-permute-start.3
  44.2 101.3 %collective-permute-done = bf16[16,128,128]{2,1,0:T(8,128)(2,1)S(1)} collective-permute-done((bf16[16,128,128]{2,1,0:T(8,128)(2,1)}, bf16[16,128,128]{2,1,0:T(8,128)(2,1)S(1)}, u32[]{:S(2)}, u32[]{:S(2)}) %collective-permute-start) | collective-permute-done | bytes 524320 | tf_op jit(solution)/shard_map/ppermute | solution.py:101
  145.6 1.9 collective-permute-start.1
  147.7 3.4 collective-permute-start.4
  151.0 20.9 %collective-permute-done.1 = bf16[16,128,128]{2,1,0:T(8,128)(2,1)S(1)} collective-permute-done((bf16[16,128,128]{2,1,0:T(8,128)(2,1)S(1)}, bf16[16,128,128]{2,1,0:T(8,128)(2,1)S(1)}, u32[]{:S(2)}, u32[]{:S(2)}) %collective-permute-start.1) | collective-permute-done | bytes 524320 | tf_op jit(solution)/shard_map/ppermute | solution.py:101
  176.7 7.1 %collective-permute-start.5 = (bf16[16,128,128]{2,1,0:T(8,128)(2,1)}, bf16[16,128,128]{2,1,0:T(8,128)(2,1)}, u32[]{:S(2)}, u32[]{:S(2)}) collective-permute-start(bf16[16,128,128]{2,1,0:T(8,128)(2,1)} %add_convert_fusion.4), channel_id=1, source_target_pairs={{128,0},{136,8},{144,16},{152,24},{160,32},{168,40},{176,48},{184,... | collective-permute-start | bytes 1572872 | tf_op jit(solution)/shard_map/ppermute | solution.py:102
  183.8 2.1 slice.18
  187.4 7.9 %convert_bitcast_fusion = bf16[2,32,88,8,128]{4,3,2,1,0:T(8,128)(2,1)} fusion(s32[32,2,32]{2,0,1:T(8,128)S(1)} %add_bitcast_fusion.1, bf16[32,2,32,768]{3,2,1,0:T(8,128)(2,1)} %all-to-all-done), kind=kOutput, calls=%fused_computation.4 | convolution fusion | flops 375128064 | bytes 14688256 | tf_op jit(solution)/shard_map/sxtc,sxcf->fxst/dot_general | solution.py:58
  195.4 3.7 collective-permute-done.2
  199.0 27.0 %all-gather.2.cloned.1.call-done = bf16[1,4096,2048]{2,1,0:T(8,128)(2,1)} async-done(((bf16[1,128,2048]{2,1,0:T(8,128)(2,1)}), bf16[1,4096,2048]{2,1,0:T(8,128)(2,1)}) %all-gather.2.cloned.1.call-update) | async-done | bytes 16777232 | tf_op jit(solution)/shard_map/all_gather | solution.py:52
  226.0 30.2 %fusion.5 = bf16[704,2,2048]{2,0,1:T(8,128)(2,1)S(1)} fusion(bf16[4096,2048]{1,0:T(8,128)(2,1)} %bitcast.132, bf16[2,32,88,8,128]{4,3,2,1,0:T(8,128)(2,1)} %convert_bitcast_fusion), kind=kOutput, calls=%fused_computation.7 | convolution fusion | flops 23625203712 | bytes 34078720 | tf_op jit(solution)/shard_map/dot_general | solution.py:111
  256.2 3.0 copy.103
  266.8 4.5 %collective-permute-start.8 = (bf16[16,128,128]{2,1,0:T(8,128)(2,1)S(1)}, bf16[16,128,128]{2,1,0:T(8,128)(2,1)S(1)}, u32[]{:S(2)}, u32[]{:S(2)}) collective-permute-start(bf16[16,128,128]{2,1,0:T(8,128)(2,1)S(1)} %add_convert_fusion.1), channel_id=1, source_target_pairs={{16,0},{24,8},{32,16},{40,24},{48,32},{56,40},{64,48},{72,56},{80,... | collective-permute-start | bytes 1572872 | tf_op jit(solution)/shard_map/ppermute | solution.py:102
  271.4 2.2 convolution_bitcast_fusion.7
  276.8 14.0 %collective-permute-done.8 = bf16[16,128,128]{2,1,0:T(8,128)(2,1)S(1)} collective-permute-done((bf16[16,128,128]{2,1,0:T(8,128)(2,1)S(1)}, bf16[16,128,128]{2,1,0:T(8,128)(2,1)S(1)}, u32[]{:S(2)}, u32[]{:S(2)}) %collective-permute-start.8) | collective-permute-done | bytes 524320 | tf_op jit(solution)/shard_map/ppermute | solution.py:102
  292.5 4.8 %collective-permute-start.9 = (bf16[16,128,128]{2,1,0:T(8,128)(2,1)S(1)}, bf16[16,128,128]{2,1,0:T(8,128)(2,1)S(1)}, u32[]{:S(2)}, u32[]{:S(2)}) collective-permute-start(bf16[16,128,128]{2,1,0:T(8,128)(2,1)S(1)} %add_convert_fusion), channel_id=1, source_target_pairs={{32,0},{40,8},{48,16},{56,24},{64,32},{72,40},{80,48},{88,56},{96,... | collective-permute-start | bytes 1572872 | tf_op jit(solution)/shard_map/ppermute | solution.py:102
  297.3 2.2 convolution_bitcast_fusion.5
  299.6 49.4 %collective-permute-done.6 = bf16[16,128,128]{2,1,0:T(8,128)(2,1)S(1)} collective-permute-done((bf16[16,128,128]{2,1,0:T(8,128)(2,1)S(1)}, bf16[16,128,128]{2,1,0:T(8,128)(2,1)S(1)}, u32[]{:S(2)}, u32[]{:S(2)}) %collective-permute-start.6) | collective-permute-done | bytes 524320 | tf_op jit(solution)/shard_map/ppermute | solution.py:101
  348.9 2.4 add_convert_fusion.2
  351.3 2.0 collective-permute-start.7
  353.4 2.6 fusion.19
  357.1 3.8 fusion.20
  360.9 2.0 copy.90
  362.9 17.0 %collective-permute-done.7 = bf16[16,128,128]{2,1,0:T(8,128)(2,1)} collective-permute-done((bf16[16,128,128]{2,1,0:T(8,128)(2,1)}, bf16[16,128,128]{2,1,0:T(8,128)(2,1)}, u32[]{:S(2)}, u32[]{:S(2)}) %collective-permute-start.7) | collective-permute-done | bytes 524320 | tf_op jit(solution)/shard_map/ppermute | solution.py:101
  379.9 2.9 fusion.21
  383.8 2.5 fusion.22
  387.3 2.0 copy.130
  (102 shorter events, 33.9 us)
Async XLA Ops:
  7.2 218.8 %all-gather.2.cloned.1.call-start = ((), (), s32[]{:S(2)}) async-start(), calls=%async_computation.2 | async-start | bytes 17301504 | tf_op jit(solution)/shard_map/all_gather | solution.py:52
  22.6 10.8 %copy-start.22 = (bf16[1,128,2048]{2,1,0:T(8,128)(2,1)S(1)}, bf16[1,128,2048]{2,1,0:T(8,128)(2,1)}, u32[]{:S(2)}) copy-start(bf16[1,128,2048]{2,1,0:T(8,128)(2,1)} %param.8) | copy-start | bytes 1572868
  22.6 11.5 %copy-start.23 = (bf16[1,128,2048]{2,1,0:T(8,128)(2,1)S(1)}, bf16[1,128,2048]{2,1,0:T(8,128)(2,1)}, u32[]{:S(2)}) copy-start(bf16[1,128,2048]{2,1,0:T(8,128)(2,1)} %param.9) | copy-start | bytes 1572868
  22.6 161.2 %all-to-all-start = ((bf16[32,2,32,768]{3,2,1,0:T(8,128)(2,1)}), bf16[32,2,32,768]{3,2,1,0:T(8,128)(2,1)}, u32[]{:S(2)}, u32[]{:S(2)}) async-start(bf16[32,2,32,768]{3,2,1,0:T(8,128)(2,1)} %bitcast.15), calls=%async_computation | async-start | bytes 6291456 | tf_op jit(solution)/shard_map/all_to_all | solution.py:51
  33.4 5.0 %copy-start.21 = (bf16[1,128,2048]{2,1,0:T(8,128)(2,1)S(1)}, bf16[1,128,2048]{2,1,0:T(8,128)(2,1)}, u32[]{:S(2)}) copy-start(bf16[1,128,2048]{2,1,0:T(8,128)(2,1)} %param.10) | copy-start | bytes 1572868
  33.4 353.9 %reduce-scatter.4.cloned.1.call-start = ((), (), s32[]{:S(2)}) async-start(), calls=%async_computation.3 | async-start | bytes 6488064
  33.6 5.1 %copy-start.24 = (bf16[1,128,2048]{2,1,0:T(8,128)(2,1)S(1)}, bf16[1,128,2048]{2,1,0:T(8,128)(2,1)}, u32[]{:S(2)}) copy-start(bf16[1,128,2048]{2,1,0:T(8,128)(2,1)} %param.7) | copy-start | bytes 1572868
  34.1 4.3 %copy-start.18 = (bf16[128,16,128]{0,2,1:T(8,128)(2,1)}, bf16[128,16,128]{0,2,1:T(8,128)(2,1)S(1)}, u32[]{:S(2)}) copy-start(bf16[128,16,128]{0,2,1:T(8,128)(2,1)S(1)} %copy.66) | copy-start | bytes 1572868
  35.3 110.1 %collective-permute-start = (bf16[16,128,128]{2,1,0:T(8,128)(2,1)}, bf16[16,128,128]{2,1,0:T(8,128)(2,1)S(1)}, u32[]{:S(2)}, u32[]{:S(2)}) collective-permute-start(bf16[16,128,128]{2,1,0:T(8,128)(2,1)} %get-tuple-element.26), channel_id=1, source_target_pairs={{0,8},{8,16},{16,24},{24,32},{32,40},{40,48},{48,56},{56,64},{64,7... | collective-permute-start | bytes 1572872 | tf_op jit(solution)/shard_map/ppermute | solution.py:101
  38.7 3.3 copy-start.8
  42.0 105.5 %collective-permute-start.3 = (bf16[16,128,128]{2,1,0:T(8,128)(2,1)S(1)}, bf16[16,128,128]{2,1,0:T(8,128)(2,1)S(1)}, u32[]{:S(2)}, u32[]{:S(2)}) collective-permute-start(bf16[16,128,128]{2,1,0:T(8,128)(2,1)S(1)} %get-tuple-element.28), channel_id=1, source_target_pairs={{8,0},{16,8},{24,16},{32,24},{40,32},{48,40},{56,48},{64,56},{72,6... | collective-permute-start | bytes 1572872 | tf_op jit(solution)/shard_map/ppermute | solution.py:102
  145.6 26.3 %collective-permute-start.1 = (bf16[16,128,128]{2,1,0:T(8,128)(2,1)S(1)}, bf16[16,128,128]{2,1,0:T(8,128)(2,1)S(1)}, u32[]{:S(2)}, u32[]{:S(2)}) collective-permute-start(bf16[16,128,128]{2,1,0:T(8,128)(2,1)S(1)} %fusion.27), channel_id=1, source_target_pairs={{0,64},{8,72},{16,80},{24,88},{32,96},{40,104},{48,112},{56,120},{... | collective-permute-start | bytes 1572872 | tf_op jit(solution)/shard_map/ppermute | solution.py:101
  147.7 27.3 %collective-permute-start.4 = (bf16[16,128,128]{2,1,0:T(8,128)(2,1)S(1)}, bf16[16,128,128]{2,1,0:T(8,128)(2,1)S(1)}, u32[]{:S(2)}, u32[]{:S(2)}) collective-permute-start(bf16[16,128,128]{2,1,0:T(8,128)(2,1)S(1)} %fusion.28), channel_id=1, source_target_pairs={{64,0},{72,8},{80,16},{88,24},{96,32},{104,40},{112,48},{120,56},{... | collective-permute-start | bytes 1572872 | tf_op jit(solution)/shard_map/ppermute | solution.py:102
  173.7 25.4 %collective-permute-start.2 = (bf16[16,128,128]{2,1,0:T(8,128)(2,1)}, bf16[16,128,128]{2,1,0:T(8,128)(2,1)}, u32[]{:S(2)}, u32[]{:S(2)}) collective-permute-start(bf16[16,128,128]{2,1,0:T(8,128)(2,1)} %add_convert_fusion.5), channel_id=1, source_target_pairs={{0,128},{8,136},{16,144},{24,152},{32,160},{40,168},{48,176},{56,1... | collective-permute-start | bytes 1572872 | tf_op jit(solution)/shard_map/ppermute | solution.py:101
  176.7 22.3 %collective-permute-start.5 = (bf16[16,128,128]{2,1,0:T(8,128)(2,1)}, bf16[16,128,128]{2,1,0:T(8,128)(2,1)}, u32[]{:S(2)}, u32[]{:S(2)}) collective-permute-start(bf16[16,128,128]{2,1,0:T(8,128)(2,1)} %add_convert_fusion.4), channel_id=1, source_target_pairs={{128,0},{136,8},{144,16},{152,24},{160,32},{168,40},{176,48},{184,... | collective-permute-start | bytes 1572872 | tf_op jit(solution)/shard_map/ppermute | solution.py:102
  259.2 3.6 copy-start.9
  259.2 5.4 %copy-start.11 = (bf16[1,128,2048]{1,2,0:T(8,128)(2,1)S(1)}, bf16[1,128,2048]{1,2,0:T(8,128)(2,1)}, u32[]{:S(2)}) copy-start(bf16[1,128,2048]{1,2,0:T(8,128)(2,1)} %copy.62) | copy-start | bytes 1572868
  264.6 6.7 %copy-start.7 = (bf16[16,8,16,128]{3,2,1,0:T(8,128)(2,1)S(1)}, bf16[16,8,16,128]{3,2,1,0:T(8,128)(2,1)}, u32[]{:S(2)}) copy-start(bf16[16,8,16,128]{3,2,1,0:T(8,128)(2,1)} %copy-done.6) | copy-start | bytes 1572868
  265.4 8.1 %copy-start.1 = (bf16[16,128,128]{2,1,0:T(8,128)(2,1)S(1)}, bf16[16,128,128]{2,1,0:T(8,128)(2,1)}, u32[]{:S(2)}) copy-start(bf16[16,128,128]{2,1,0:T(8,128)(2,1)} %copy-done) | copy-start | bytes 1572868
  266.8 24.1 %collective-permute-start.8 = (bf16[16,128,128]{2,1,0:T(8,128)(2,1)S(1)}, bf16[16,128,128]{2,1,0:T(8,128)(2,1)S(1)}, u32[]{:S(2)}, u32[]{:S(2)}) collective-permute-start(bf16[16,128,128]{2,1,0:T(8,128)(2,1)S(1)} %add_convert_fusion.1), channel_id=1, source_target_pairs={{16,0},{24,8},{32,16},{40,24},{48,32},{56,40},{64,48},{72,56},{80,... | collective-permute-start | bytes 1572872 | tf_op jit(solution)/shard_map/ppermute | solution.py:102
  273.5 23.8 %copy-start.19 = (bf16[128,16,128]{0,2,1:T(8,128)(2,1)S(1)}, bf16[128,16,128]{0,2,1:T(8,128)(2,1)}, u32[]{:S(2)}) copy-start(bf16[128,16,128]{0,2,1:T(8,128)(2,1)} %copy-done.18) | copy-start | bytes 1572868
  274.9 74.0 %collective-permute-start.6 = (bf16[16,128,128]{2,1,0:T(8,128)(2,1)S(1)}, bf16[16,128,128]{2,1,0:T(8,128)(2,1)S(1)}, u32[]{:S(2)}, u32[]{:S(2)}) collective-permute-start(bf16[16,128,128]{2,1,0:T(8,128)(2,1)S(1)} %add_convert_fusion.3), channel_id=1, source_target_pairs={{0,16},{8,24},{16,32},{24,40},{32,48},{40,56},{48,64},{56,72},{64,... | collective-permute-start | bytes 1572872 | tf_op jit(solution)/shard_map/ppermute | solution.py:101
  290.9 62.5 %copy-start.17 = (bf16[16,128,128]{2,1,0:T(8,128)(2,1)}, bf16[16,128,128]{2,1,0:T(8,128)(2,1)S(1)}, u32[]{:S(2)}) copy-start(bf16[16,128,128]{2,1,0:T(8,128)(2,1)S(1)} %collective-permute-done.8) | copy-start | bytes 1572868
  292.5 60.9 %collective-permute-start.9 = (bf16[16,128,128]{2,1,0:T(8,128)(2,1)S(1)}, bf16[16,128,128]{2,1,0:T(8,128)(2,1)S(1)}, u32[]{:S(2)}, u32[]{:S(2)}) collective-permute-start(bf16[16,128,128]{2,1,0:T(8,128)(2,1)S(1)} %add_convert_fusion), channel_id=1, source_target_pairs={{32,0},{40,8},{48,16},{56,24},{64,32},{72,40},{80,48},{88,56},{96,... | collective-permute-start | bytes 1572872 | tf_op jit(solution)/shard_map/ppermute | solution.py:102
  348.9 7.1 %copy-start.15 = (bf16[16,128,128]{2,1,0:T(8,128)(2,1)}, bf16[16,128,128]{2,1,0:T(8,128)(2,1)S(1)}, u32[]{:S(2)}) copy-start(bf16[16,128,128]{2,1,0:T(8,128)(2,1)S(1)} %collective-permute-done.6) | copy-start | bytes 1572868
  351.3 5.7 %copy-start.5 = (bf16[16,128,128]{2,1,0:T(8,128)(2,1)S(1)}, bf16[16,128,128]{2,1,0:T(8,128)(2,1)}, u32[]{:S(2)}) copy-start(bf16[16,128,128]{2,1,0:T(8,128)(2,1)} %copy-done.3) | copy-start | bytes 1572868
  351.3 5.7 %copy-start.14 = (bf16[16,8,16,128]{3,2,1,0:T(8,128)(2,1)S(1)}, bf16[16,8,16,128]{3,2,1,0:T(8,128)(2,1)}, u32[]{:S(2)}) copy-start(bf16[16,8,16,128]{3,2,1,0:T(8,128)(2,1)} %copy-done.13) | copy-start | bytes 1572868
  351.3 28.6 %collective-permute-start.7 = (bf16[16,128,128]{2,1,0:T(8,128)(2,1)}, bf16[16,128,128]{2,1,0:T(8,128)(2,1)}, u32[]{:S(2)}, u32[]{:S(2)}) collective-permute-start(bf16[16,128,128]{2,1,0:T(8,128)(2,1)} %add_convert_fusion.2), channel_id=1, source_target_pairs={{0,32},{8,40},{16,48},{24,56},{32,64},{40,72},{48,80},{56,88},{64,... | collective-permute-start | bytes 1572872 | tf_op jit(solution)/shard_map/ppermute | solution.py:101
  357.0 22.9 %copy-start.2 = (bf16[16,128,128]{2,1,0:T(8,128)(2,1)S(1)}, bf16[16,128,128]{2,1,0:T(8,128)(2,1)}, u32[]{:S(2)}) copy-start(bf16[16,128,128]{2,1,0:T(8,128)(2,1)} %copy-done) | copy-start | bytes 1572868
  357.0 22.9 %copy-start.12 = (bf16[1,128,2048]{1,2,0:T(8,128)(2,1)S(1)}, bf16[1,128,2048]{1,2,0:T(8,128)(2,1)}, u32[]{:S(2)}) copy-start(bf16[1,128,2048]{1,2,0:T(8,128)(2,1)} %copy.62) | copy-start | bytes 1572868
  362.9 20.9 %copy-start.10 = (bf16[1,128,2048]{1,2,0:T(8,128)(2,1)S(1)}, bf16[1,128,2048]{1,2,0:T(8,128)(2,1)}, u32[]{:S(2)}) copy-start(bf16[1,128,2048]{1,2,0:T(8,128)(2,1)} %copy-done.8) | copy-start | bytes 1572868
  362.9 20.9 %copy-start.16 = (bf16[16,128,128]{2,1,0:T(8,128)(2,1)S(1)}, bf16[16,128,128]{2,1,0:T(8,128)(2,1)}, u32[]{:S(2)}) copy-start(bf16[16,128,128]{2,1,0:T(8,128)(2,1)} %copy-done.15) | copy-start | bytes 1572868
  (6 other events, 9.7 us)
Sparse Core Ops, SparseCore 0:
  10.6 215.3 all-gather.1
  259.3 43.2 reduce-scatter.3
